TPU v7x, 512 devices: a whole 4x8x8 slice. The times are simulated.
512 devices in a mesh: ctx: 128 (over x, z, y_lo, core), head: 4 (over y_hi).
Axes of the slice: x: 4, y: 8 (y_hi: 4, y_lo: 2; y = y_hi * 2 + y_lo), z: 8, core: 2. Of those that a mesh axis runs over, the one named last changes fastest.
Arguments:
- queries: bfloat16 [32768, 2048], P('ctx', 'head'), may hold values from -8 to 8
- keys: bfloat16 [32768, 2048], P('ctx', 'head'), may hold values from -8 to 8
- values: bfloat16 [32768, 2048], P('ctx', 'head'), may hold values from -6 to 6
- out_grad: bfloat16 [32768, 2048], P('ctx', 'head'), may hold values from -6 to 6
Outputs:
- attended: bfloat16 [32768, 2048], P('ctx', 'head')
- query_grad: bfloat16 [32768, 2048], P('ctx', 'head')
- key_grad: bfloat16 [32768, 2048], P('ctx', 'head')
- value_grad: bfloat16 [32768, 2048], P('ctx', 'head')
All inputs are finite; a program needn't handle non-finite values.
Results may differ from a plain program's by a relative error of at most 0.017.
Values may be sent and summed in bfloat16 or wider, within the bound.
No kernel may reach another device: no remote copies, remote signals or barrier semaphores. Data moves between devices by JAX's collectives and lax.ppermute only.
A program may use at most 64 MiB of HBM per device.

v0:
```python
import math

import jax
import jax.numpy as jnp
from jax import lax
from jax.sharding import PartitionSpec as P

HD = 128
STRIDE = 128
SUMMARY = 4


def split_heads(matrix):
    blocks = matrix.shape[0] // STRIDE
    half_heads = matrix.shape[1] // (2 * HD)
    shaped = matrix.reshape(blocks, STRIDE, matrix.shape[1] // (4 * HD), 4, HD)
    fixed = shaped[:, :, :, :2].reshape(blocks, STRIDE, half_heads, HD)
    strided = shaped[:, :, :, 2:].reshape(blocks, STRIDE, half_heads, HD)
    return (fixed, strided)


def join_heads(fixed, strided):
    blocks, positions, half_heads, head_dim = fixed.shape
    paired = jnp.concatenate(
        [
            fixed.reshape(blocks, positions, half_heads // 2, 2, head_dim),
            strided.reshape(blocks, positions, half_heads // 2, 2, head_dim),
        ],
        axis=3,
    )
    return paired.reshape(blocks * positions, 2 * half_heads * head_dim)


def fixed_heads(query, key_rows, value_rows, grad_rows, scaling):
    blocks_here, positions, half_heads, head_dim = query.shape
    summary_keys = key_rows[:, positions - SUMMARY :]
    summary_values = value_rows[:, positions - SUMMARY :]
    every_key, every_value = (
        lax.all_gather(summary_keys, "ctx", axis=0, tiled=True),
        lax.all_gather(summary_values, "ctx", axis=0, tiled=True),
    )
    summary_count = every_key.shape[0] * SUMMARY
    flat_keys = every_key.reshape(summary_count, half_heads, head_dim)
    flat_values = every_value.reshape(summary_count, half_heads, head_dim)
    block_ids = lax.axis_index("ctx") * blocks_here + jnp.arange(blocks_here, dtype=jnp.int32)
    summary_block = jnp.arange(summary_count, dtype=jnp.int32) // SUMMARY
    earlier = (summary_block[None, :] < block_ids[:, None])[:, None, None, :]
    causal = (jnp.arange(positions)[:, None] >= jnp.arange(positions)[None, :])[None, None]
    local_scores = (
        jnp.einsum("bqgd,bkgd->bgqk", query, key_rows, preferred_element_type=jnp.float32) * scaling
    )
    summary_scores = (
        jnp.einsum("bqgd,mgd->bgqm", query, flat_keys, preferred_element_type=jnp.float32) * scaling
    )
    local_scores = jnp.where(causal, local_scores, -jnp.inf)
    summary_scores = jnp.where(earlier, summary_scores, -jnp.inf)
    row_max = jnp.maximum(jnp.max(local_scores, axis=-1), jnp.max(summary_scores, axis=-1))[
        ..., None
    ]
    local_raised = jnp.exp(local_scores - row_max)
    summary_raised = jnp.exp(summary_scores - row_max)
    totals = jnp.sum(local_raised, axis=-1, keepdims=True) + jnp.sum(
        summary_raised, axis=-1, keepdims=True
    )
    local_weights = local_raised / totals
    summary_weights = summary_raised / totals
    local_low = local_weights.astype(jnp.bfloat16)
    summary_low = summary_weights.astype(jnp.bfloat16)
    attended = (
        jnp.einsum("bgqk,bkgd->bqgd", local_low, value_rows, preferred_element_type=jnp.float32)
        + jnp.einsum("bgqm,mgd->bqgd", summary_low, flat_values, preferred_element_type=jnp.float32)
    ).astype(jnp.bfloat16)
    local_dweights = jnp.einsum(
        "bqgd,bkgd->bgqk", grad_rows, value_rows, preferred_element_type=jnp.float32
    )
    summary_dweights = jnp.einsum(
        "bqgd,mgd->bgqm", grad_rows, flat_values, preferred_element_type=jnp.float32
    )
    row_delta = jnp.sum(grad_rows.astype(jnp.float32) * attended.astype(jnp.float32), axis=-1)
    row_delta = jnp.transpose(row_delta, (0, 2, 1))[..., None]
    local_dscores = (local_weights * (local_dweights - row_delta)).astype(jnp.bfloat16)
    summary_dscores = (summary_weights * (summary_dweights - row_delta)).astype(jnp.bfloat16)
    query_grad = (
        jnp.einsum("bgqk,bkgd->bqgd", local_dscores, key_rows, preferred_element_type=jnp.float32)
        + jnp.einsum(
            "bgqm,mgd->bqgd", summary_dscores, flat_keys, preferred_element_type=jnp.float32
        )
    ) * scaling
    key_grad = (
        jnp.einsum("bgqk,bqgd->bkgd", local_dscores, query, preferred_element_type=jnp.float32)
        * scaling
    )
    value_grad = jnp.einsum(
        "bgqk,bqgd->bkgd", local_low, grad_rows, preferred_element_type=jnp.float32
    )
    key_terms = (
        jnp.einsum("bgqm,bqgd->mgd", summary_dscores, query, preferred_element_type=jnp.float32)
        * scaling
    )
    value_terms = jnp.einsum(
        "bgqm,bqgd->mgd", summary_low, grad_rows, preferred_element_type=jnp.float32
    )
    shares = lax.psum_scatter(
        jnp.stack([key_terms, value_terms], axis=1), "ctx", scatter_dimension=0, tiled=True
    )
    shares = shares.reshape(blocks_here, SUMMARY, 2, half_heads, head_dim)
    key_grad = key_grad.at[:, positions - SUMMARY :].add(shares[:, :, 0])
    value_grad = value_grad.at[:, positions - SUMMARY :].add(shares[:, :, 1])
    return (
        attended,
        query_grad.astype(jnp.bfloat16),
        key_grad.astype(jnp.bfloat16),
        value_grad.astype(jnp.bfloat16),
    )


def strided_heads(query, key_rows, value_rows, grad_rows, scaling):
    query_all = lax.all_to_all(query, "ctx", split_axis=1, concat_axis=0, tiled=True)
    keys_all = lax.all_to_all(key_rows, "ctx", split_axis=1, concat_axis=0, tiled=True)
    values_all = lax.all_to_all(value_rows, "ctx", split_axis=1, concat_axis=0, tiled=True)
    grads_all = lax.all_to_all(grad_rows, "ctx", split_axis=1, concat_axis=0, tiled=True)
    blocks = query_all.shape[0]
    causal = (jnp.arange(blocks)[:, None] >= jnp.arange(blocks)[None, :])[None, None]
    scores = (
        jnp.einsum("brgd,crgd->rgbc", query_all, keys_all, preferred_element_type=jnp.float32)
        * scaling
    )
    scores = jnp.where(causal, scores, -jnp.inf)
    row_max = jnp.max(scores, axis=-1, keepdims=True)
    raised = jnp.exp(scores - row_max)
    weights = raised / jnp.sum(raised, axis=-1, keepdims=True)
    weights_low = weights.astype(jnp.bfloat16)
    attended = jnp.einsum(
        "rgbc,crgd->brgd", weights_low, values_all, preferred_element_type=jnp.float32
    ).astype(jnp.bfloat16)
    dweights = jnp.einsum(
        "brgd,crgd->rgbc", grads_all, values_all, preferred_element_type=jnp.float32
    )
    row_delta = jnp.sum(grads_all.astype(jnp.float32) * attended.astype(jnp.float32), axis=-1)
    row_delta = jnp.transpose(row_delta, (1, 2, 0))[..., None]
    dscores = (weights * (dweights - row_delta)).astype(jnp.bfloat16)
    query_grad = (
        jnp.einsum("rgbc,crgd->brgd", dscores, keys_all, preferred_element_type=jnp.float32)
        * scaling
    ).astype(jnp.bfloat16)
    key_grad = (
        jnp.einsum("rgbc,brgd->crgd", dscores, query_all, preferred_element_type=jnp.float32)
        * scaling
    ).astype(jnp.bfloat16)
    value_grad = jnp.einsum(
        "rgbc,brgd->crgd", weights_low, grads_all, preferred_element_type=jnp.float32
    ).astype(jnp.bfloat16)
    return (
        lax.all_to_all(attended, "ctx", split_axis=0, concat_axis=1, tiled=True),
        lax.all_to_all(query_grad, "ctx", split_axis=0, concat_axis=1, tiled=True),
        lax.all_to_all(key_grad, "ctx", split_axis=0, concat_axis=1, tiled=True),
        lax.all_to_all(value_grad, "ctx", split_axis=0, concat_axis=1, tiled=True),
    )


def shards(queries, keys, values, out_grad):
    scaling = 1.0 / math.sqrt(HD)
    query_fixed, query_strided = split_heads(queries)
    key_fixed, key_strided = split_heads(keys)
    value_fixed, value_strided = split_heads(values)
    grad_fixed, grad_strided = split_heads(out_grad)
    fixed_out = fixed_heads(query_fixed, key_fixed, value_fixed, grad_fixed, scaling)
    strided_out = strided_heads(query_strided, key_strided, value_strided, grad_strided, scaling)
    return (
        join_heads(fixed_out[0], strided_out[0]),
        join_heads(fixed_out[1], strided_out[1]),
        join_heads(fixed_out[2], strided_out[2]),
        join_heads(fixed_out[3], strided_out[3]),
    )


def solution(mesh):
    return jax.shard_map(
        shards,
        mesh=mesh,
        in_specs=(P("ctx", "head"), P("ctx", "head"), P("ctx", "head"), P("ctx", "head")),
        out_specs=(P("ctx", "head"), P("ctx", "head"), P("ctx", "head"), P("ctx", "head")),
        check_vma=False,
    )
```

profile of v0, /device:TPU:1, one launch (start us, length us, event | category | flops | bytes accessed | tf_op | source)
XLA Modules:
  0.0 904.9 jit_solution(8492532768877551417)
XLA Ops:
  7.3 1.1 reshape.335
  8.8 1.0 reshape.319
  11.0 166.4 %all_gather.7 = bf16[256,4,2,128]{3,1,2,0:T(4,128)(2,1)S(1)} all-gather(bf16[2,4,2,128]{3,1,2,0:T(4,128)(2,1)S(1)} %copy.203), channel_id=1, replica_groups=mesh['ctx'=128,'head'=4] {'ctx'}, dimensions={0}, use_global_device_ids=true | all-gather | bytes 528384 | tf_op jit(solution)/shard_map/all_gather | solution.py:40
  177.6 153.2 %all_gather.6 = bf16[256,4,2,128]{3,1,2,0:T(4,128)(2,1)S(1)} all-gather(bf16[2,4,2,128]{3,1,2,0:T(4,128)(2,1)S(1)} %slice.111), channel_id=1, replica_groups=mesh['ctx'=128,'head'=4] {'ctx'}, dimensions={0}, use_global_device_ids=true | all-gather | bytes 528384 | tf_op jit(solution)/shard_map/all_gather | solution.py:39
  331.3 0.5 fusion.66
  331.8 0.3 fusion.4
  332.1 0.3 fusion.30
  332.5 0.4 convolution_bitcast_fusion.5
  332.9 0.9 multiply_reduce_fusion.1
  333.7 0.4 convolution_bitcast_fusion
  334.1 0.6 fusion.2
  334.7 0.4 fusion.6
  335.2 1.5 pad_maximum_fusion
  336.7 0.7 copy.207
  337.4 5.3 all-to-all-start
  342.8 0.7 copy.209
  343.5 10.4 %all-to-all-done = bf16[2,128,2,128]{3,2,0,1:T(2,128)(2,1)S(1)} async-done(((bf16[2,128,2,128]{3,2,0,1:T(2,128)(2,1)}), bf16[2,128,2,128]{3,2,0,1:T(2,128)(2,1)S(1)}, u32[]{:S(2)}, u32[]{:S(2)}) %all-to-all-start) | async-done | bytes 131104 | tf_op jit(solution)/shard_map/all_to_all | solution.py:118
  353.9 6.1 all-to-all-start.1
  360.0 0.7 copy.211
  360.7 10.6 %all-to-all-done.1 = bf16[2,128,2,128]{3,2,0,1:T(2,128)(2,1)S(1)} async-done(((bf16[2,128,2,128]{3,2,0,1:T(2,128)(2,1)}), bf16[2,128,2,128]{3,2,0,1:T(2,128)(2,1)S(1)}, u32[]{:S(2)}, u32[]{:S(2)}) %all-to-all-start.1) | async-done | bytes 131104 | tf_op jit(solution)/shard_map/all_to_all | solution.py:119
  371.3 6.1 all-to-all-start.2
  377.4 0.7 copy.227
  378.2 10.2 %all-to-all-done.2 = bf16[2,128,2,128]{3,2,0,1:T(2,128)(2,1)S(1)} async-done(((bf16[2,128,2,128]{3,2,0,1:T(2,128)(2,1)}), bf16[2,128,2,128]{3,2,0,1:T(2,128)(2,1)S(1)}, u32[]{:S(2)}, u32[]{:S(2)}) %all-to-all-start.2) | async-done | bytes 131104 | tf_op jit(solution)/shard_map/all_to_all | solution.py:120
  388.4 6.1 all-to-all-start.4
  394.6 0.7 iota_compare_fusion
  395.4 10.1 %all-to-all-done.4 = bf16[2,128,2,128]{3,2,0,1:T(2,128)(2,1)S(1)} async-done(((bf16[2,128,2,128]{3,2,0,1:T(2,128)(2,1)}), bf16[2,128,2,128]{3,2,0,1:T(2,128)(2,1)S(1)}, u32[]{:S(2)}, u32[]{:S(2)}) %all-to-all-start.4) | async-done | bytes 131104 | tf_op jit(solution)/shard_map/all_to_all | solution.py:121
  406.1 2.0 fusion.64
  408.1 1.3 multiply_reduce_fusion
  409.4 1.3 fusion.11
  410.9 0.8 copy.242
  411.7 6.2 all-to-all-start.6
  418.5 0.8 copy.234
  419.3 9.7 %all-to-all-done.6 = bf16[256,1,2,128]{3,2,1,0:T(2,128)(2,1)S(1)} async-done(((bf16[256,1,2,128]{3,2,1,0:T(2,128)(2,1)}), bf16[256,1,2,128]{3,2,1,0:T(2,128)(2,1)S(1)}, u32[]{:S(2)}, u32[]{:S(2)}) %all-to-all-start.6) | async-done | bytes 131104 | tf_op jit(solution)/shard_map/all_to_all | solution.py:156
  428.9 6.1 all-to-all-start.5
  435.3 1.3 fusion.24
  436.6 0.8 copy.248
  437.3 8.8 all-to-all-done.5
  446.2 6.4 all-to-all-start.7
  452.6 0.5 convolution_bitcast_fusion.4
  453.1 0.8 copy.215
  453.9 9.8 %all-to-all-done.7 = bf16[256,1,2,128]{3,2,1,0:T(2,128)(2,1)S(1)} async-done(((bf16[256,1,2,128]{3,2,1,0:T(2,128)(2,1)}), bf16[256,1,2,128]{3,2,1,0:T(2,128)(2,1)S(1)}, u32[]{:S(2)}, u32[]{:S(2)}) %all-to-all-start.7) | async-done | bytes 131104 | tf_op jit(solution)/shard_map/all_to_all | solution.py:157
  463.7 6.1 all-to-all-start.3
  470.5 10.4 %all-to-all-done.3 = bf16[256,1,2,128]{3,2,1,0:T(2,128)(2,1)S(1)} async-done(((bf16[256,1,2,128]{3,2,1,0:T(2,128)(2,1)}), bf16[256,1,2,128]{3,2,1,0:T(2,128)(2,1)S(1)}, u32[]{:S(2)}, u32[]{:S(2)}) %all-to-all-start.3) | async-done | bytes 131104 | tf_op jit(solution)/shard_map/all_to_all | solution.py:154
  481.6 0.9 copy_bitcast_fusion.2
  482.4 412.0 %reduce-scatter.2.cloned.1.call-done = f32[8,2,2,128]{3,0,2,1:T(8,128)} async-done(((f32[1024,2,2,128]{3,0,2,1:T(8,128)}), f32[8,2,2,128]{3,0,2,1:T(8,128)}) %reduce-scatter.2.cloned.1.call-update) | async-done | bytes 16400 | tf_op jit(solution)/shard_map/reduce_scatter | solution.py:103
  894.4 0.7 fusion.63
  895.7 1.2 scatter-add.6
  897.2 0.9 copy_bitcast_fusion
  (69 shorter events, 6.0 us)
Async XLA Ops:
  7.2 2.9 copy-start
  7.2 3.2 copy-start.1
  7.2 887.2 %reduce-scatter.2.cloned.1.call-start = ((), (), s32[]{:S(2)}) async-start(), calls=%async_computation.9 | async-start | bytes 2113536 | tf_op jit(solution)/shard_map/reduce_scatter | solution.py:103
  337.4 16.5 %all-to-all-start = ((bf16[2,128,2,128]{3,2,0,1:T(2,128)(2,1)}), bf16[2,128,2,128]{3,2,0,1:T(2,128)(2,1)S(1)}, u32[]{:S(2)}, u32[]{:S(2)}) async-start(bf16[2,128,2,128]{3,2,0,1:T(2,128)(2,1)} %copy.207), calls=%async_computation | async-start | bytes 262144 | tf_op jit(solution)/shard_map/all_to_all | solution.py:118
  353.9 17.4 %all-to-all-start.1 = ((bf16[2,128,2,128]{3,2,0,1:T(2,128)(2,1)}), bf16[2,128,2,128]{3,2,0,1:T(2,128)(2,1)S(1)}, u32[]{:S(2)}, u32[]{:S(2)}) async-start(bf16[2,128,2,128]{3,2,0,1:T(2,128)(2,1)} %copy.209), calls=%async_computation.1 | async-start | bytes 262144 | tf_op jit(solution)/shard_map/all_to_all | solution.py:119
  371.3 17.1 %all-to-all-start.2 = ((bf16[2,128,2,128]{3,2,0,1:T(2,128)(2,1)}), bf16[2,128,2,128]{3,2,0,1:T(2,128)(2,1)S(1)}, u32[]{:S(2)}, u32[]{:S(2)}) async-start(bf16[2,128,2,128]{3,2,0,1:T(2,128)(2,1)} %copy.211), calls=%async_computation.2 | async-start | bytes 262144 | tf_op jit(solution)/shard_map/all_to_all | solution.py:120
  388.4 17.2 %all-to-all-start.4 = ((bf16[2,128,2,128]{3,2,0,1:T(2,128)(2,1)}), bf16[2,128,2,128]{3,2,0,1:T(2,128)(2,1)S(1)}, u32[]{:S(2)}, u32[]{:S(2)}) async-start(bf16[2,128,2,128]{3,2,0,1:T(2,128)(2,1)} %copy.227), calls=%async_computation.4 | async-start | bytes 262144 | tf_op jit(solution)/shard_map/all_to_all | solution.py:121
  406.1 4.6 copy-start.2
  410.9 24.4 %copy-start.3 = (bf16[128,2,1,2,128]{4,1,0,3,2:T(2,128)(2,1)S(1)}, bf16[128,2,1,2,128]{4,1,0,3,2:T(2,128)(2,1)}, u32[]{:S(2)}) copy-start(bf16[128,2,1,2,128]{4,1,0,3,2:T(2,128)(2,1)} %copy-done.2) | copy-start | bytes 393220
  411.7 17.2 %all-to-all-start.6 = ((bf16[256,1,2,128]{3,2,1,0:T(2,128)(2,1)}), bf16[256,1,2,128]{3,2,1,0:T(2,128)(2,1)S(1)}, u32[]{:S(2)}, u32[]{:S(2)}) async-start(bf16[256,1,2,128]{3,2,1,0:T(2,128)(2,1)} %copy.242), calls=%async_computation.7 | async-start | bytes 262144 | tf_op jit(solution)/shard_map/all_to_all | solution.py:156
  428.9 17.3 %all-to-all-start.5 = ((bf16[256,1,2,128]{3,2,1,0:T(2,128)(2,1)}), bf16[256,1,2,128]{3,2,1,0:T(2,128)(2,1)S(1)}, u32[]{:S(2)}, u32[]{:S(2)}) async-start(bf16[256,1,2,128]{3,2,1,0:T(2,128)(2,1)} %copy.234), calls=%async_computation.5 | async-start | bytes 262144 | tf_op jit(solution)/shard_map/all_to_all | solution.py:155
  446.2 17.5 %all-to-all-start.7 = ((bf16[256,1,2,128]{3,2,1,0:T(2,128)(2,1)}), bf16[256,1,2,128]{3,2,1,0:T(2,128)(2,1)S(1)}, u32[]{:S(2)}, u32[]{:S(2)}) async-start(bf16[256,1,2,128]{3,2,1,0:T(2,128)(2,1)} %copy.248), calls=%async_computation.8 | async-start | bytes 262144 | tf_op jit(solution)/shard_map/all_to_all | solution.py:157
  453.9 27.4 %copy-start.4 = (bf16[2,128,2,128]{1,3,2,0:T(8,128)(2,1)S(1)}, bf16[2,128,2,128]{1,3,2,0:T(8,128)(2,1)}, u32[]{:S(2)}) copy-start(bf16[2,128,2,128]{1,3,2,0:T(8,128)(2,1)} %get-tuple-element.49) | copy-start | bytes 393220
  463.7 17.3 %all-to-all-start.3 = ((bf16[256,1,2,128]{3,2,1,0:T(2,128)(2,1)}), bf16[256,1,2,128]{3,2,1,0:T(2,128)(2,1)S(1)}, u32[]{:S(2)}, u32[]{:S(2)}) async-start(bf16[256,1,2,128]{3,2,1,0:T(2,128)(2,1)} %copy.215), calls=%async_computation.3 | async-start | bytes 262144 | tf_op jit(solution)/shard_map/all_to_all | solution.py:154
Sparse Core Ops, SparseCore 0:
  336.8 557.5 reduce-scatter.1
where the time goes:
time: 911 us; the launch traced here: 905 us
  waiting for transfers between devices  492 us (54%)
  blocking collectives  320 us (35%)
  starting transfers between devices  48.5 us (5%)
  local copies, waits for them, and re-layouts  15.7 us (2%)
  between operations  14.6 us (2%)
  matrix products  11.1 us (1%)
    reduce_scatter x1, waiting for transfers between devices, fixed_heads(): lax.psum_scatter(jnp.stack([key_terms, value_terms], axis=1), 'ctx', scat...  412 us
    all_gather x1, blocking collectives, fixed_heads(): lax.all_gather(summary_values, 'ctx', axis=0, tiled=True)  166 us
    all_gather x1, blocking collectives, fixed_heads(): lax.all_gather(summary_keys, 'ctx', axis=0, tiled=True)  153 us
  transfers between devices with their start and end apart: 9, of which 9 were waited for; matrix products, arithmetic and copies ran while one was open for 2% of the time, Pallas kernels for 0%

commit v1 on v0

--- a/solution.py
+++ b/solution.py
@@ -31,17 +31,9 @@
     return paired.reshape(blocks * positions, 2 * half_heads * head_dim)
 
 
-def fixed_heads(query, key_rows, value_rows, grad_rows, scaling):
+def fixed_heads(query, key_rows, value_rows, grad_rows, flat_keys, flat_values, scaling):
     blocks_here, positions, half_heads, head_dim = query.shape
-    summary_keys = key_rows[:, positions - SUMMARY :]
-    summary_values = value_rows[:, positions - SUMMARY :]
-    every_key, every_value = (
-        lax.all_gather(summary_keys, "ctx", axis=0, tiled=True),
-        lax.all_gather(summary_values, "ctx", axis=0, tiled=True),
-    )
-    summary_count = every_key.shape[0] * SUMMARY
-    flat_keys = every_key.reshape(summary_count, half_heads, head_dim)
-    flat_values = every_value.reshape(summary_count, half_heads, head_dim)
+    summary_count = flat_keys.shape[0]
     block_ids = lax.axis_index("ctx") * blocks_here + jnp.arange(blocks_here, dtype=jnp.int32)
     summary_block = jnp.arange(summary_count, dtype=jnp.int32) // SUMMARY
     earlier = (summary_block[None, :] < block_ids[:, None])[:, None, None, :]
@@ -100,25 +92,10 @@
     value_terms = jnp.einsum(
         "bgqm,bqgd->mgd", summary_low, grad_rows, preferred_element_type=jnp.float32
     )
-    shares = lax.psum_scatter(
-        jnp.stack([key_terms, value_terms], axis=1), "ctx", scatter_dimension=0, tiled=True
-    )
-    shares = shares.reshape(blocks_here, SUMMARY, 2, half_heads, head_dim)
-    key_grad = key_grad.at[:, positions - SUMMARY :].add(shares[:, :, 0])
-    value_grad = value_grad.at[:, positions - SUMMARY :].add(shares[:, :, 1])
-    return (
-        attended,
-        query_grad.astype(jnp.bfloat16),
-        key_grad.astype(jnp.bfloat16),
-        value_grad.astype(jnp.bfloat16),
-    )
-
-
-def strided_heads(query, key_rows, value_rows, grad_rows, scaling):
-    query_all = lax.all_to_all(query, "ctx", split_axis=1, concat_axis=0, tiled=True)
-    keys_all = lax.all_to_all(key_rows, "ctx", split_axis=1, concat_axis=0, tiled=True)
-    values_all = lax.all_to_all(value_rows, "ctx", split_axis=1, concat_axis=0, tiled=True)
-    grads_all = lax.all_to_all(grad_rows, "ctx", split_axis=1, concat_axis=0, tiled=True)
+    return (attended, query_grad, key_grad, value_grad, jnp.stack([key_terms, value_terms]))
+
+
+def strided_heads(query_all, keys_all, values_all, grads_all, scaling):
     blocks = query_all.shape[0]
     causal = (jnp.arange(blocks)[:, None] >= jnp.arange(blocks)[None, :])[None, None]
     scores = (
@@ -150,12 +127,7 @@
     value_grad = jnp.einsum(
         "rgbc,brgd->crgd", weights_low, grads_all, preferred_element_type=jnp.float32
     ).astype(jnp.bfloat16)
-    return (
-        lax.all_to_all(attended, "ctx", split_axis=0, concat_axis=1, tiled=True),
-        lax.all_to_all(query_grad, "ctx", split_axis=0, concat_axis=1, tiled=True),
-        lax.all_to_all(key_grad, "ctx", split_axis=0, concat_axis=1, tiled=True),
-        lax.all_to_all(value_grad, "ctx", split_axis=0, concat_axis=1, tiled=True),
-    )
+    return jnp.stack([attended, query_grad, key_grad, value_grad])
 
 
 def shards(queries, keys, values, out_grad):
@@ -164,13 +136,61 @@
     key_fixed, key_strided = split_heads(keys)
     value_fixed, value_strided = split_heads(values)
     grad_fixed, grad_strided = split_heads(out_grad)
-    fixed_out = fixed_heads(query_fixed, key_fixed, value_fixed, grad_fixed, scaling)
-    strided_out = strided_heads(query_strided, key_strided, value_strided, grad_strided, scaling)
+    blocks_here, positions, half_heads, head_dim = query_fixed.shape
+    peers = lax.axis_size("ctx")
+    residues = positions // peers
+
+    strided_rows = jnp.stack([query_strided, key_strided, value_strided, grad_strided])
+    strided_rows = strided_rows.reshape(4, blocks_here, peers, residues, half_heads, head_dim)
+    strided_rows = strided_rows.transpose(2, 0, 1, 3, 4, 5).reshape(peers, -1)
+    summary_rows = jnp.stack(
+        [key_fixed[:, positions - SUMMARY :], value_fixed[:, positions - SUMMARY :]]
+    ).reshape(1, -1)
+    summary_rows = jnp.broadcast_to(summary_rows, (peers, summary_rows.shape[1]))
+    strided_size = strided_rows.shape[1]
+    received = lax.all_to_all(
+        jnp.concatenate([strided_rows, summary_rows], axis=1), "ctx", 0, 0, tiled=True
+    )
+    gathered = received[:, :strided_size].reshape(
+        peers, 4, blocks_here, residues, half_heads, head_dim
+    )
+    gathered = gathered.transpose(1, 0, 2, 3, 4, 5).reshape(
+        4, peers * blocks_here, residues, half_heads, head_dim
+    )
+    summaries = received[:, strided_size:].reshape(
+        peers, 2, blocks_here * SUMMARY, half_heads, head_dim
+    )
+    summaries = summaries.transpose(1, 0, 2, 3, 4).reshape(
+        2, peers * blocks_here * SUMMARY, half_heads, head_dim
+    )
+
+    attended, query_grad, key_grad, value_grad, terms = fixed_heads(
+        query_fixed,
+        key_fixed,
+        value_fixed,
+        grad_fixed,
+        summaries[0],
+        summaries[1],
+        scaling,
+    )
+    strided_out = strided_heads(gathered[0], gathered[1], gathered[2], gathered[3], scaling)
+
+    strided_out = strided_out.reshape(4, peers, blocks_here, residues, half_heads, head_dim)
+    strided_out = lax.all_to_all(strided_out.reshape(4, peers, -1).transpose(1, 0, 2), "ctx", 0, 0, tiled=True)
+    strided_out = strided_out.reshape(peers, 4, blocks_here, residues, half_heads, head_dim)
+    strided_out = strided_out.transpose(1, 2, 0, 3, 4, 5).reshape(
+        4, blocks_here, positions, half_heads, head_dim
+    )
+    terms = terms.reshape(2, peers, -1).transpose(1, 0, 2)
+    shares = jnp.sum(lax.all_to_all(terms, "ctx", 0, 0, tiled=True), axis=0)
+    shares = shares.reshape(2, blocks_here, SUMMARY, half_heads, head_dim)
+    key_grad = key_grad.at[:, positions - SUMMARY :].add(shares[0])
+    value_grad = value_grad.at[:, positions - SUMMARY :].add(shares[1])
     return (
-        join_heads(fixed_out[0], strided_out[0]),
-        join_heads(fixed_out[1], strided_out[1]),
-        join_heads(fixed_out[2], strided_out[2]),
-        join_heads(fixed_out[3], strided_out[3]),
+        join_heads(attended, strided_out[0]),
+        join_heads(query_grad.astype(jnp.bfloat16), strided_out[1]),
+        join_heads(key_grad.astype(jnp.bfloat16), strided_out[2]),
+        join_heads(value_grad.astype(jnp.bfloat16), strided_out[3]),
     )
 
 

time: 911 us -> 188 us (0.21)
  waiting for transfers between devices: 492 us -> 80.3 us
  blocking collectives: 320 us -> 0 us
  local copies, waits for them, and re-layouts: 15.7 us -> 49.7 us
  between operations: 14.6 us -> 1.35 us
  starting transfers between devices: 48.5 us -> 37.7 us
    reduce_scatter x1 -> x0, waiting for transfers between devices: 412 us -> none  [fixed_heads(): lax.psum_scatter(jnp.stack([key_terms, value_terms], axis=1), 'ctx', scat...]
    all_gather x2 -> x0, blocking collectives: 320 us -> none  [the longest x1 166 us: fixed_heads(): lax.all_gather(summary_values, 'ctx', axis=0, tiled=True)]
    unnamed x15 -> x39, local copies, waits for them, and re-layouts: 0.46 us -> 16.5 us
    all_to_all x8 -> x3, starting transfers between devices: 48.5 us -> 37.7 us  [the longest x1 17 us: shards(): lax.all_to_all(jnp.concatenate([strided_rows, summary_rows], axis=1), 'ct...]
    all_to_all x8 -> x3, waiting for transfers between devices: 80 us -> 80.3 us  [the longest x1 43.1 us: shards(): shares = jnp.sum(lax.all_to_all(terms, 'ctx', 0, 0, tiled=True), axis=0)]
  transfers between devices with their start and end apart: 9 -> 3, of which waited for: 9 -> 2; matrix products, arithmetic and copies ran while one was open for 2% -> 15% of each run, Pallas kernels for 0% -> 0%
where the time goes in v1:
time: 188 us; the launch traced here: 186 us
  waiting for transfers between devices  80.3 us (43%)
  local copies, waits for them, and re-layouts  49.7 us (26%)
  starting transfers between devices  37.7 us (20%)
  matrix products  8.69 us (5%)
  other arithmetic  8.49 us (5%)
    all_to_all x1, waiting for transfers between devices, shards(): shares = jnp.sum(lax.all_to_all(terms, 'ctx', 0, 0, tiled=True), axis=0)  43.1 us
    all_to_all x1, waiting for transfers between devices, shards(): lax.all_to_all(jnp.concatenate([strided_rows, summary_rows], axis=1), 'ct...  37.1 us
    all_to_all x1, starting transfers between devices, shards(): lax.all_to_all(jnp.concatenate([strided_rows, summary_rows], axis=1), 'ct...  17 us
    unnamed x39, local copies, waits for them, and re-layouts  16.5 us
    all_to_all x1, starting transfers between devices, shards(): shares = jnp.sum(lax.all_to_all(terms, 'ctx', 0, 0, tiled=True), axis=0)  12.4 us
    all_to_all x1, starting transfers between devices, shards(): lax.all_to_all(strided_out.reshape(4, peers, -1).transpose(1, 0, 2), 'ctx...  8.19 us
    all_to_all x2, local copies, waits for them, and re-layouts, shards(): lax.all_to_all(jnp.concatenate([strided_rows, summary_rows], axis=1), 'ct...  5.25 us
    another operation x2, local copies, waits for them, and re-layouts, fixed_heads(): jnp.stack([key_terms, value_terms])  4.89 us
  transfers between devices with their start and end apart: 3, of which 2 were waited for; matrix products, arithmetic and copies ran while one was open for 15% of the time, Pallas kernels for 0%

profile of v1, /device:TPU:1, one launch (start us, length us, event | category | flops | bytes accessed | tf_op | source)
XLA Modules:
  0.0 186.2 jit_solution(1796111284784797456)
XLA Ops:
  0.6 1.1 reshape.350
  1.7 1.0 reshape.352
  2.7 1.0 reshape.354
  3.7 0.4 fusion.62
  4.3 0.4 fusion.60
  4.8 1.0 maximum_bitcast_fusion.2
  5.7 0.4 copy.225
  6.6 0.5 broadcast.128
  7.1 1.9 %reduce.9 = bf16[128,6144]{1,0:T(8,128)(2,1)S(1)} reduce(bf16[128,1,6144]{2,0,1:T(8,128)(2,1)S(1)} %maximum_bitcast_fusion.1, bf16[]{:T(256)} %broadcast.128), dimensions={1}, to_apply=%copy.229.reduce_sub_computation | reduce | bytes 3145730 | tf_op jit(solution)/shard_map/all_to_all | solution.py:151
  9.0 2.1 %reshape.385 = bf16[128,2,3072]{2,1,0:T(2,128)(2,1)} reshape(bf16[128,6144]{1,0:T(8,128)(2,1)S(1)} %reduce.9) | data formatting | bytes 3145728
  11.1 17.0 %all-to-all-start = ((bf16[128,2,3072]{2,1,0:T(2,128)(2,1)}), bf16[128,2,3072]{2,1,0:T(2,128)(2,1)}, u32[]{:S(2)}, u32[]{:S(2)}) async-start(bf16[128,2,3072]{2,1,0:T(2,128)(2,1)} %reshape.385), calls=%async_computation | async-start | bytes 3145728 | tf_op jit(solution)/shard_map/all_to_all | solution.py:151
  28.1 0.8 copy.325
  28.9 0.8 copy.327
  29.8 0.9 fusion.66
  30.7 37.1 %all-to-all-done = bf16[128,2,3072]{2,1,0:T(2,128)(2,1)} async-done(((bf16[128,2,3072]{2,1,0:T(2,128)(2,1)}), bf16[128,2,3072]{2,1,0:T(2,128)(2,1)}, u32[]{:S(2)}, u32[]{:S(2)}) %all-to-all-start) | async-done | bytes 1572896 | tf_op jit(solution)/shard_map/all_to_all | solution.py:151
  67.8 9.1 %reshape.386 = bf16[128,1,6144]{2,1,0:T(2,128)(2,1)S(1)} reshape(bf16[128,2,3072]{2,1,0:T(2,128)(2,1)} %all-to-all-done) | data formatting | bytes 3145728
  76.9 4.7 %copy.230 = bf16[128,1,6144]{0,2,1:T(8,128)(2,1)} copy(bf16[128,1,6144]{2,1,0:T(2,128)(2,1)S(1)} %reshape.386) | data formatting | bytes 3145728 | tf_op jit(solution)/shard_map/all_to_all | solution.py:151
  81.7 1.1 slice.180
  82.7 1.3 slice.177
  87.8 1.2 copy.261
  89.0 8.2 %all-to-all-start.1 = ((bf16[128,4,512]{2,1,0:T(4,128)(2,1)}), bf16[128,4,512]{2,1,0:T(4,128)(2,1)}, u32[]{:S(2)}, u32[]{:S(2)}) async-start(bf16[128,4,512]{2,1,0:T(4,128)(2,1)} %copy.261), calls=%async_computation.1 | async-start | bytes 1048576 | tf_op jit(solution)/shard_map/all_to_all | solution.py:179
  97.5 0.5 fusion.67
  98.0 1.0 fusion.37
  100.4 0.9 multiply_reduce_fusion
  101.3 0.4 convolution_bitcast_fusion
  101.9 0.6 copy.271
  102.5 1.8 copy.279
  104.3 3.0 %stack.46 = f32[1,128,2048]{2,1,0:T(8,128)} reshape(f32[1024,2,128]{2,1,0:T(2,128)} %copy.279) | data formatting | bytes 2097152 | tf_op jit(solution)/shard_map/stack | solution.py:95
  107.3 1.2 fusion.2
  108.6 1.0 copy-done
  109.6 0.4 fusion.6
  110.0 0.8 copy.277
  110.8 1.9 stack.45
  112.7 1.4 maximum_bitcast_fusion
  114.1 3.0 %copy.280 = f32[128,2,2048]{2,1,0:T(2,128)} copy(f32[128,2,2048]{2,0,1:T(8,128)S(1)} %maximum_bitcast_fusion) | data formatting | bytes 4194304 | tf_op jit(solution)/shard_map/transpose | solution.py:184
  117.1 12.4 %all-to-all-start.2 = ((f32[128,2,2048]{2,1,0:T(2,128)}), f32[128,2,2048]{2,1,0:T(2,128)S(1)}, u32[]{:S(2)}, u32[]{:S(2)}) async-start(f32[128,2,2048]{2,1,0:T(2,128)} %copy.280), calls=%async_computation.2 | async-start | bytes 4194304 | tf_op jit(solution)/shard_map/all_to_all | solution.py:185
  129.8 1.6 convolution_bitcast_fusion.4
  132.1 1.5 copy.262
  133.5 0.7 slice_bitcast_fusion.1
  134.5 0.7 copy.369
  135.2 1.0 pad_maximum_fusion
  136.4 0.7 copy.370
  137.2 43.1 %all-to-all-done.2 = f32[128,2,2048]{2,1,0:T(2,128)S(1)} async-done(((f32[128,2,2048]{2,1,0:T(2,128)}), f32[128,2,2048]{2,1,0:T(2,128)S(1)}, u32[]{:S(2)}, u32[]{:S(2)}) %all-to-all-start.2) | async-done | bytes 2097184 | tf_op jit(solution)/shard_map/all_to_all | solution.py:185
  180.3 0.7 reduce_sum.62
  181.3 1.2 scatter-add.6
  182.9 0.7 copy.368
  183.9 1.2 scatter-add.9
  185.4 0.7 copy.367
  (95 shorter events, 8.5 us)
Async XLA Ops:
  0.6 3.6 %copy-start.6 = (bf16[256,512]{1,0:T(8,128)(2,1)S(1)}, bf16[256,512]{1,0:T(8,128)(2,1)}, u32[]{:S(2)}) copy-start(bf16[256,512]{1,0:T(8,128)(2,1)} %param.11) | copy-start | bytes 786436
  4.1 0.7 copy-start.3
  11.1 56.7 %all-to-all-start = ((bf16[128,2,3072]{2,1,0:T(2,128)(2,1)}), bf16[128,2,3072]{2,1,0:T(2,128)(2,1)}, u32[]{:S(2)}, u32[]{:S(2)}) async-start(bf16[128,2,3072]{2,1,0:T(2,128)(2,1)} %reshape.385), calls=%async_computation | async-start | bytes 3145728 | tf_op jit(solution)/shard_map/all_to_all | solution.py:151
  89.0 28.1 %all-to-all-start.1 = ((bf16[128,4,512]{2,1,0:T(4,128)(2,1)}), bf16[128,4,512]{2,1,0:T(4,128)(2,1)}, u32[]{:S(2)}, u32[]{:S(2)}) async-start(bf16[128,4,512]{2,1,0:T(4,128)(2,1)} %copy.261), calls=%async_computation.1 | async-start | bytes 1048576 | tf_op jit(solution)/shard_map/all_to_all | solution.py:179
  99.3 0.9 copy-start.4
  99.3 1.0 copy-start.7
  99.3 1.0 copy-start.10
  99.7 1.6 copy-start.2
  101.3 0.6 copy-start.13
  108.6 1.0 copy-start
  110.0 2.7 %copy-start.1 = (f32[1,128,2048]{2,1,0:T(8,128)S(1)}, f32[1,128,2048]{2,1,0:T(8,128)}, u32[]{:S(2)}) copy-start(f32[1,128,2048]{2,1,0:T(8,128)} %stack.46) | copy-start | bytes 3145732
  117.1 12.5 %copy-start.5 = (bf16[2,128,1,2,128]{4,3,1,0,2:T(2,128)(2,1)S(1)}, bf16[2,128,1,2,128]{4,3,1,0,2:T(2,128)(2,1)}, u32[]{:S(2)}) copy-start(bf16[2,128,1,2,128]{4,3,1,0,2:T(2,128)(2,1)} %copy-done.3) | copy-start | bytes 393220
  117.1 12.5 %copy-start.8 = (f32[2,2,128,128]{2,3,1,0:T(8,128)S(1)}, f32[2,2,128,128]{2,3,1,0:T(8,128)}, u32[]{:S(2)}) copy-start(f32[2,2,128,128]{2,3,1,0:T(8,128)} %get-tuple-element.54) | copy-start | bytes 786436
  117.1 12.5 %copy-start.11 = (bf16[2,128,1,2,128]{1,4,3,0,2:T(8,128)(2,1)S(1)}, bf16[2,128,1,2,128]{1,4,3,0,2:T(8,128)(2,1)}, u32[]{:S(2)}) copy-start(bf16[2,128,1,2,128]{1,4,3,0,2:T(8,128)(2,1)} %copy.325) | copy-start | bytes 393220
  117.1 12.5 %copy-start.14 = (f32[2,128,2]{1,2,0:T(2,128)S(1)}, f32[2,128,2]{1,2,0:T(2,128)}, u32[]{:S(2)}) copy-start(f32[2,128,2]{1,2,0:T(2,128)} %copy-done.13) | copy-start | bytes 6148
  117.1 63.2 %all-to-all-start.2 = ((f32[128,2,2048]{2,1,0:T(2,128)}), f32[128,2,2048]{2,1,0:T(2,128)S(1)}, u32[]{:S(2)}, u32[]{:S(2)}) async-start(f32[128,2,2048]{2,1,0:T(2,128)} %copy.280), calls=%async_computation.2 | async-start | bytes 4194304 | tf_op jit(solution)/shard_map/all_to_all | solution.py:185
  129.6 2.3 %copy-start.9 = (f32[2,2,128,128]{2,3,1,0:T(8,128)S(1)}, f32[2,2,128,128]{2,3,1,0:T(8,128)}, u32[]{:S(2)}) copy-start(f32[2,2,128,128]{2,3,1,0:T(8,128)} %get-tuple-element.54) | copy-start | bytes 786436
  129.6 2.3 %copy-start.12 = (bf16[2,128,1,2,128]{1,4,3,0,2:T(8,128)(2,1)S(1)}, bf16[2,128,1,2,128]{1,4,3,0,2:T(8,128)(2,1)}, u32[]{:S(2)}) copy-start(bf16[2,128,1,2,128]{1,4,3,0,2:T(8,128)(2,1)} %copy.325) | copy-start | bytes 393220

commit v2 on v1

--- a/solution.py
+++ b/solution.py
@@ -175,14 +175,18 @@
     )
     strided_out = strided_heads(gathered[0], gathered[1], gathered[2], gathered[3], scaling)
 
-    strided_out = strided_out.reshape(4, peers, blocks_here, residues, half_heads, head_dim)
-    strided_out = lax.all_to_all(strided_out.reshape(4, peers, -1).transpose(1, 0, 2), "ctx", 0, 0, tiled=True)
-    strided_out = strided_out.reshape(peers, 4, blocks_here, residues, half_heads, head_dim)
+    strided_out = strided_out.reshape(4, peers, -1).transpose(1, 0, 2).reshape(peers, -1)
+    terms = terms.astype(jnp.bfloat16).reshape(2, peers, -1).transpose(1, 0, 2).reshape(peers, -1)
+    returned = lax.all_to_all(
+        jnp.concatenate([strided_out, terms], axis=1), "ctx", 0, 0, tiled=True
+    )
+    strided_out = returned[:, :strided_size].reshape(
+        peers, 4, blocks_here, residues, half_heads, head_dim
+    )
     strided_out = strided_out.transpose(1, 2, 0, 3, 4, 5).reshape(
         4, blocks_here, positions, half_heads, head_dim
     )
-    terms = terms.reshape(2, peers, -1).transpose(1, 0, 2)
-    shares = jnp.sum(lax.all_to_all(terms, "ctx", 0, 0, tiled=True), axis=0)
+    shares = jnp.sum(returned[:, strided_size:].astype(jnp.float32), axis=0)
     shares = shares.reshape(2, blocks_here, SUMMARY, half_heads, head_dim)
     key_grad = key_grad.at[:, positions - SUMMARY :].add(shares[0])
     value_grad = value_grad.at[:, positions - SUMMARY :].add(shares[1])

time: 188 us -> 173 us (0.920)
  starting transfers between devices: 37.7 us -> 25.5 us
  waiting for transfers between devices: 80.3 us -> 73.6 us
  local copies, waits for them, and re-layouts: 49.7 us -> 54.6 us
    all_to_all x2 -> x1, starting transfers between devices: 20.6 us -> 8.49 us  [shards(): lax.all_to_all(jnp.concatenate([strided_out, terms], axis=1), 'ctx', 0, 0...]
    unnamed x39 -> x46, local copies, waits for them, and re-layouts: 16.5 us -> 28.1 us
    all_to_all x2 -> x1, waiting for transfers between devices: 43.1 us -> 37.1 us  [shards(): lax.all_to_all(jnp.concatenate([strided_out, terms], axis=1), 'ctx', 0, 0...]
    another operation x2, local copies, waits for them, and re-layouts: 4.89 us -> 0.78 us  [fixed_heads(): jnp.stack([key_terms, value_terms])]
    all_to_all x1, local copies, waits for them, and re-layouts: 1.46 us -> 4.73 us  [shards(): lax.all_to_all(jnp.concatenate([strided_out, terms], axis=1), 'ctx', 0, 0...]
    transpose x2, local copies, waits for them, and re-layouts: 4.16 us -> 0.93 us  [the longest x1 0.66 us: shards(): terms.astype(jnp.bfloat16).reshape(2, peers, -1).transpose(1, 0, 2)]
  transfers between devices with their start and end apart: 3 -> 2, of which waited for: 2 -> 2; matrix products, arithmetic and copies ran while one was open for 15% -> 3% of each run, Pallas kernels for 0% -> 0%
where the time goes in v2:
time: 173 us; the launch traced here: 172 us
  waiting for transfers between devices  73.6 us (43%)
  local copies, waits for them, and re-layouts  54.6 us (32%)
  starting transfers between devices  25.5 us (15%)
  other arithmetic  8.54 us (5%)
  matrix products  8.18 us (5%)
    all_to_all x1, waiting for transfers between devices, shards(): lax.all_to_all(jnp.concatenate([strided_out, terms], axis=1), 'ctx', 0, 0...  37.1 us
    all_to_all x1, waiting for transfers between devices, shards(): lax.all_to_all(jnp.concatenate([strided_rows, summary_rows], axis=1), 'ct...  36.5 us
    unnamed x46, local copies, waits for them, and re-layouts  28.1 us
    all_to_all x1, starting transfers between devices, shards(): lax.all_to_all(jnp.concatenate([strided_rows, summary_rows], axis=1), 'ct...  17 us
    all_to_all x1, starting transfers between devices, shards(): lax.all_to_all(jnp.concatenate([strided_out, terms], axis=1), 'ctx', 0, 0...  8.49 us
    all_to_all x2, local copies, waits for them, and re-layouts, shards(): lax.all_to_all(jnp.concatenate([strided_rows, summary_rows], axis=1), 'ct...  5.21 us
    all_to_all x1, local copies, waits for them, and re-layouts, shards(): lax.all_to_all(jnp.concatenate([strided_out, terms], axis=1), 'ctx', 0, 0...  4.73 us
  transfers between devices with their start and end apart: 2, of which 2 were waited for; matrix products, arithmetic and copies ran while one was open for 3% of the time, Pallas kernels for 0%

profile of v2, /device:TPU:1, one launch (start us, length us, event | category | flops | bytes accessed | tf_op | source)
XLA Modules:
  0.0 171.9 jit_solution(16661384407219599284)
XLA Ops:
  0.7 1.1 reshape.373
  1.7 1.0 reshape.375
  2.7 0.4 slice_bitcast_fusion.7
  3.3 0.4 fusion.63
  3.7 1.0 maximum_bitcast_fusion.3
  4.7 0.4 copy.228
  5.7 0.5 broadcast.128
  6.1 1.8 %reduce.9 = bf16[128,6144]{1,0:T(8,128)(2,1)S(1)} reduce(bf16[128,1,6144]{2,0,1:T(8,128)(2,1)S(1)} %maximum_bitcast_fusion, bf16[]{:T(256)} %broadcast.128), dimensions={1}, to_apply=%copy.232.reduce_sub_computation | reduce | bytes 3145730 | tf_op jit(solution)/shard_map/all_to_all | solution.py:151
  7.9 2.1 %reshape.408 = bf16[128,2,3072]{2,1,0:T(2,128)(2,1)} reshape(bf16[128,6144]{1,0:T(8,128)(2,1)S(1)} %reduce.9) | data formatting | bytes 3145728
  10.0 17.0 %all-to-all-start = ((bf16[128,2,3072]{2,1,0:T(2,128)(2,1)}), bf16[128,2,3072]{2,1,0:T(2,128)(2,1)}, u32[]{:S(2)}, u32[]{:S(2)}) async-start(bf16[128,2,3072]{2,1,0:T(2,128)(2,1)} %reshape.408), calls=%async_computation | async-start | bytes 3145728 | tf_op jit(solution)/shard_map/all_to_all | solution.py:151
  27.0 0.8 copy.329
  27.8 0.8 copy.331
  28.6 0.6 iota_compare_fusion
  29.3 0.9 fusion.66
  30.2 36.5 %all-to-all-done = bf16[128,2,3072]{2,1,0:T(2,128)(2,1)} async-done(((bf16[128,2,3072]{2,1,0:T(2,128)(2,1)}), bf16[128,2,3072]{2,1,0:T(2,128)(2,1)}, u32[]{:S(2)}, u32[]{:S(2)}) %all-to-all-start) | async-done | bytes 1572896 | tf_op jit(solution)/shard_map/all_to_all | solution.py:151
  66.7 9.1 %reshape.409 = bf16[128,1,6144]{2,1,0:T(2,128)(2,1)S(1)} reshape(bf16[128,2,3072]{2,1,0:T(2,128)(2,1)} %all-to-all-done) | data formatting | bytes 3145728
  75.8 4.7 %copy.233 = bf16[128,1,6144]{0,2,1:T(8,128)(2,1)} copy(bf16[128,1,6144]{2,1,0:T(2,128)(2,1)S(1)} %reshape.409) | data formatting | bytes 3145728 | tf_op jit(solution)/shard_map/all_to_all | solution.py:151
  80.6 1.1 slice.210
  81.6 1.3 slice.207
  87.3 0.5 fusion.67
  88.7 0.4 convolution_bitcast_fusion.5
  89.2 0.4 fusion.11
  89.7 0.9 multiply_reduce_fusion
  90.6 0.6 fusion.2
  91.2 1.0 copy-done.2
  92.2 0.4 fusion.10
  92.6 0.5 copy.269
  93.2 0.4 stack.45
  93.5 0.5 copy.271
  94.1 0.4 stack.46
  94.6 0.7 copy.272
  95.4 1.8 %reduce.10 = bf16[128,6144]{0,1:T(8,128)(2,1)S(1)} reduce(bf16[128,1,6144]{0,2,1:T(8,128)(2,1)S(1)} %maximum_bitcast_fusion.1, bf16[]{:T(256)} %broadcast.128), dimensions={1}, to_apply=%copy.273.reduce_sub_computation | reduce | bytes 3145730 | tf_op jit(solution)/shard_map/all_to_all | solution.py:180
  97.1 0.7 copy.378
  97.9 2.1 %reshape.410 = bf16[128,2,3072]{2,1,0:T(2,128)(2,1)} reshape(bf16[128,6144]{1,0:T(8,128)(2,1)S(1)} %copy.378) | data formatting | bytes 3145728
  99.9 8.5 %all-to-all-start.1 = ((bf16[128,2,3072]{2,1,0:T(2,128)(2,1)}), bf16[128,2,3072]{2,1,0:T(2,128)(2,1)}, u32[]{:S(2)}, u32[]{:S(2)}) async-start(bf16[128,2,3072]{2,1,0:T(2,128)(2,1)} %reshape.410), calls=%async_computation.1 | async-start | bytes 3145728 | tf_op jit(solution)/shard_map/all_to_all | solution.py:180
  109.0 0.9 fusion.30
  110.1 0.9 fusion.46
  111.1 37.1 %all-to-all-done.1 = bf16[128,2,3072]{2,1,0:T(2,128)(2,1)} async-done(((bf16[128,2,3072]{2,1,0:T(2,128)(2,1)}), bf16[128,2,3072]{2,1,0:T(2,128)(2,1)}, u32[]{:S(2)}, u32[]{:S(2)}) %all-to-all-start.1) | async-done | bytes 1572896 | tf_op jit(solution)/shard_map/all_to_all | solution.py:180
  148.1 9.1 %reshape.411 = bf16[128,1,6144]{2,1,0:T(2,128)(2,1)S(1)} reshape(bf16[128,2,3072]{2,1,0:T(2,128)(2,1)} %all-to-all-done.1) | data formatting | bytes 3145728
  157.2 4.7 %copy.274 = bf16[128,1,6144]{0,2,1:T(8,128)(2,1)} copy(bf16[128,1,6144]{2,1,0:T(2,128)(2,1)S(1)} %reshape.411) | data formatting | bytes 3145728 | tf_op jit(solution)/shard_map/all_to_all | solution.py:180
  162.0 1.6 convert_reduce_fusion
  163.6 1.1 slice.216
  165.0 0.7 copy.373
  166.0 0.7 copy.374
  167.0 1.2 scatter-add.6
  168.6 0.7 copy.372
  169.6 1.2 scatter-add.9
  171.1 0.7 copy.371
  (103 shorter events, 8.5 us)
Async XLA Ops:
  0.6 2.5 %copy-start.9 = (bf16[256,512]{1,0:T(8,128)(2,1)S(1)}, bf16[256,512]{1,0:T(8,128)(2,1)}, u32[]{:S(2)}) copy-start(bf16[256,512]{1,0:T(8,128)(2,1)} %param.10) | copy-start | bytes 786436
  0.6 2.6 %copy-start.10 = (bf16[256,512]{1,0:T(8,128)(2,1)S(1)}, bf16[256,512]{1,0:T(8,128)(2,1)}, u32[]{:S(2)}) copy-start(bf16[256,512]{1,0:T(8,128)(2,1)} %param.11) | copy-start | bytes 786436
  3.7 1.7 %copy-start.6 = (bf16[2,128,1,2,128]{4,3,1,0,2:T(2,128)(2,1)}, bf16[2,128,1,2,128]{4,3,1,0,2:T(2,128)(2,1)S(1)}, u32[]{:S(2)}) copy-start(bf16[2,128,1,2,128]{4,3,1,0,2:T(2,128)(2,1)S(1)} %get-tuple-element.62) | copy-start | bytes 393220
  10.0 56.7 %all-to-all-start = ((bf16[128,2,3072]{2,1,0:T(2,128)(2,1)}), bf16[128,2,3072]{2,1,0:T(2,128)(2,1)}, u32[]{:S(2)}, u32[]{:S(2)}) async-start(bf16[128,2,3072]{2,1,0:T(2,128)(2,1)} %reshape.408), calls=%async_computation | async-start | bytes 3145728 | tf_op jit(solution)/shard_map/all_to_all | solution.py:151
  82.9 0.9 copy-start.16
  87.0 1.0 copy-start.11
  87.3 1.0 copy-start
  88.3 0.9 copy-start.8
  88.7 1.0 copy-start.7
  88.7 1.0 copy-start.13
  91.2 1.0 copy-start.2
  99.9 8.5 %copy-start.12 = (f32[2,2,128,128]{2,3,1,0:T(8,128)S(1)}, f32[2,2,128,128]{2,3,1,0:T(8,128)}, u32[]{:S(2)}) copy-start(f32[2,2,128,128]{2,3,1,0:T(8,128)} %get-tuple-element.50) | copy-start | bytes 786436
  99.9 8.5 %copy-start.14 = (bf16[2,128,1,2,128]{1,4,3,0,2:T(8,128)(2,1)S(1)}, bf16[2,128,1,2,128]{1,4,3,0,2:T(8,128)(2,1)}, u32[]{:S(2)}) copy-start(bf16[2,128,1,2,128]{1,4,3,0,2:T(8,128)(2,1)} %copy.329) | copy-start | bytes 393220
  99.9 8.7 %copy-start.1 = (bf16[1,128,8,2,128]{4,2,1,3,0:T(8,128)(2,1)S(1)}, bf16[1,128,8,2,128]{4,2,1,3,0:T(8,128)(2,1)}, u32[]{:S(2)}) copy-start(bf16[1,128,8,2,128]{4,2,1,3,0:T(8,128)(2,1)} %copy-done) | copy-start | bytes 1572868
  99.9 8.7 %copy-start.3 = (bf16[2,2,128,1024]{2,3,0,1:T(8,128)(2,1)S(1)}, bf16[2,2,128,1024]{2,3,0,1:T(8,128)(2,1)}, u32[]{:S(2)}) copy-start(bf16[2,2,128,1024]{2,3,0,1:T(8,128)(2,1)} %copy-done.2) | copy-start | bytes 3145732
  99.9 48.2 %all-to-all-start.1 = ((bf16[128,2,3072]{2,1,0:T(2,128)(2,1)}), bf16[128,2,3072]{2,1,0:T(2,128)(2,1)}, u32[]{:S(2)}, u32[]{:S(2)}) async-start(bf16[128,2,3072]{2,1,0:T(2,128)(2,1)} %reshape.410), calls=%async_computation.1 | async-start | bytes 3145728 | tf_op jit(solution)/shard_map/all_to_all | solution.py:180
  162.0 2.8 %copy-start.5 = (bf16[2,128,1,2,128]{1,4,3,0,2:T(8,128)(2,1)S(1)}, bf16[2,128,1,2,128]{1,4,3,0,2:T(8,128)(2,1)}, u32[]{:S(2)}) copy-start(bf16[2,128,1,2,128]{1,4,3,0,2:T(8,128)(2,1)} %fusion.30) | copy-start | bytes 393220
  163.6 2.2 %copy-start.15 = (bf16[2,128,2,128]{1,3,2,0:T(8,128)(2,1)S(1)}, bf16[2,128,2,128]{1,3,2,0:T(8,128)(2,1)}, u32[]{:S(2)}) copy-start(bf16[2,128,2,128]{1,3,2,0:T(8,128)(2,1)} %get-tuple-element.54) | copy-start | bytes 393220
  166.0 3.5 %copy-start.4 = (f32[2,2,128,128]{2,3,1,0:T(8,128)S(1)}, f32[2,2,128,128]{2,3,1,0:T(8,128)}, u32[]{:S(2)}) copy-start(f32[2,2,128,128]{2,3,1,0:T(8,128)} %fusion.46) | copy-start | bytes 786436

commit v3 on v2

--- a/solution.py
+++ b/solution.py
@@ -142,11 +142,11 @@
 
     strided_rows = jnp.stack([query_strided, key_strided, value_strided, grad_strided])
     strided_rows = strided_rows.reshape(4, blocks_here, peers, residues, half_heads, head_dim)
-    strided_rows = strided_rows.transpose(2, 0, 1, 3, 4, 5).reshape(peers, -1)
+    strided_rows = strided_rows.transpose(2, 0, 1, 3, 4, 5).reshape(peers, -1, head_dim)
     summary_rows = jnp.stack(
         [key_fixed[:, positions - SUMMARY :], value_fixed[:, positions - SUMMARY :]]
-    ).reshape(1, -1)
-    summary_rows = jnp.broadcast_to(summary_rows, (peers, summary_rows.shape[1]))
+    ).reshape(1, -1, head_dim)
+    summary_rows = jnp.broadcast_to(summary_rows, (peers,) + summary_rows.shape[1:])
     strided_size = strided_rows.shape[1]
     received = lax.all_to_all(
         jnp.concatenate([strided_rows, summary_rows], axis=1), "ctx", 0, 0, tiled=True
@@ -175,8 +175,10 @@
     )
     strided_out = strided_heads(gathered[0], gathered[1], gathered[2], gathered[3], scaling)
 
-    strided_out = strided_out.reshape(4, peers, -1).transpose(1, 0, 2).reshape(peers, -1)
-    terms = terms.astype(jnp.bfloat16).reshape(2, peers, -1).transpose(1, 0, 2).reshape(peers, -1)
+    strided_out = strided_out.reshape(4, peers, -1, head_dim).transpose(1, 0, 2, 3)
+    strided_out = strided_out.reshape(peers, -1, head_dim)
+    terms = terms.astype(jnp.bfloat16).reshape(2, peers, -1, head_dim).transpose(1, 0, 2, 3)
+    terms = terms.reshape(peers, -1, head_dim)
     returned = lax.all_to_all(
         jnp.concatenate([strided_out, terms], axis=1), "ctx", 0, 0, tiled=True
     )

time: 173 us -> 134 us (0.77)
  local copies, waits for them, and re-layouts: 54.6 us -> 15.4 us
  matrix products: 8.18 us -> 11.6 us
  other arithmetic: 8.54 us -> 5.59 us
  waiting for transfers between devices: 73.6 us -> 75.5 us
    unnamed x46 -> x25, local copies, waits for them, and re-layouts: 28.1 us -> 4.36 us
    all_to_all x3 -> x0, local copies, waits for them, and re-layouts: 9.94 us -> none  [the longest x2 5.21 us: shards(): lax.all_to_all(jnp.concatenate([strided_rows, summary_rows], axis=1), 'ct...]
    all_to_all x4 -> x0, other arithmetic: 3.84 us -> none  [the longest x2 1.97 us: shards(): lax.all_to_all(jnp.concatenate([strided_rows, summary_rows], axis=1), 'ct...]
    concatenate x0 -> x2, other arithmetic: none -> 2.51 us  [the longest x1 1.26 us: shards(): jnp.concatenate([strided_rows, summary_rows], axis=1)]
where the time goes in v3:
time: 134 us
  waiting for transfers between devices  75.5 us (56%)
  starting transfers between devices  24.4 us (18%)
  local copies, waits for them, and re-layouts  15.4 us (11%)
  matrix products  11.6 us (9%)
  other arithmetic  5.59 us (4%)
  between operations  1.34 us (1%)
    all_to_all x1, waiting for transfers between devices, shards(): lax.all_to_all(jnp.concatenate([strided_rows, summary_rows], axis=1), 'ct...  38 us
    all_to_all x1, waiting for transfers between devices, shards(): lax.all_to_all(jnp.concatenate([strided_out, terms], axis=1), 'ctx', 0, 0...  37.4 us
    all_to_all x1, starting transfers between devices, shards(): lax.all_to_all(jnp.concatenate([strided_rows, summary_rows], axis=1), 'ct...  16.6 us
    all_to_all x1, starting transfers between devices, shards(): lax.all_to_all(jnp.concatenate([strided_out, terms], axis=1), 'ctx', 0, 0...  7.75 us
    unnamed x25, local copies, waits for them, and re-layouts  4.36 us
  transfers between devices with their start and end apart: 2, of which 2 were waited for; matrix products, arithmetic and copies ran while one was open for 3% of the time, Pallas kernels for 0%

profile of v3, /device:TPU:1, one launch (start us, length us, event | category | flops | bytes accessed | tf_op | source)
XLA Modules:
  0.0 133.8 jit_solution(8079523766541881654)
XLA Ops:
  0.7 1.1 reshape.357
  1.7 1.0 reshape.359
  2.7 0.4 slice_bitcast_fusion.7
  3.3 0.4 slice_bitcast_fusion.6
  3.7 1.0 maximum_bitcast_fusion.1
  4.8 0.3 copy.224
  5.3 1.3 pad_maximum_fusion
  6.6 16.6 %all-to-all-start = ((bf16[128,48,128]{2,1,0:T(8,128)(2,1)}), bf16[128,48,128]{2,1,0:T(8,128)(2,1)S(1)}, u32[]{:S(2)}, u32[]{:S(2)}) async-start(bf16[128,48,128]{2,1,0:T(8,128)(2,1)} %pad_maximum_fusion), calls=%async_computation | async-start | bytes 3145728 | tf_op jit(solution)/shard_map/all_to_all | solution.py:151
  23.3 0.8 copy.323
  24.3 0.9 fusion.69
  25.2 38.0 %all-to-all-done = bf16[128,48,128]{2,1,0:T(8,128)(2,1)S(1)} async-done(((bf16[128,48,128]{2,1,0:T(8,128)(2,1)}), bf16[128,48,128]{2,1,0:T(8,128)(2,1)S(1)}, u32[]{:S(2)}, u32[]{:S(2)}) %all-to-all-start) | async-done | bytes 1572896 | tf_op jit(solution)/shard_map/all_to_all | solution.py:151
  63.5 0.2 copy.245
  64.4 1.1 fusion.71
  65.5 1.3 %fusion.27 = bf16[256,1,2,128]{0,3,2,1:T(8,128)(2,1)S(1)} fusion(bf16[256,2,128]{2,0,1:T(8,128)(2,1)S(1)} %bitcast.264, f32[2,256,256]{1,2,0:T(8,128)} %get-tuple-element.56, f32[2,256]{1,0:T(2,128)S(1)} %get-tuple-element.55), kind=kOutput, calls=%fused_computation.48 | convolution fusion | flops 33882112 | bytes 788480 | tf_op jit(solution)/shard_map/rgbc,brgd->crgd/dot_general | solution.py:127
  66.9 1.3 multiply_reduce_fusion.1
  68.2 0.2 fusion.14
  68.4 0.2 fusion.28
  68.7 0.2 fusion.29
  69.0 0.4 copy.321
  70.0 0.5 maximum_bitcast_fusion.2
  70.6 0.3 copy.266
  71.0 0.6 fusion.70
  71.7 0.3 fusion.4
  72.0 0.3 fusion.33
  72.4 0.6 convolution_bitcast_fusion.5
  73.0 0.4 fusion.11
  73.4 0.9 multiply_reduce_fusion
  74.3 0.8 fusion.2
  75.1 0.4 fusion.10
  75.6 0.5 copy.262
  76.1 0.5 copy.264
  77.0 1.3 pad_maximum_fusion.1
  78.2 7.7 %all-to-all-start.1 = ((bf16[128,48,128]{2,1,0:T(8,128)(2,1)}), bf16[128,48,128]{2,1,0:T(8,128)(2,1)S(1)}, u32[]{:S(2)}, u32[]{:S(2)}) async-start(bf16[128,48,128]{2,1,0:T(8,128)(2,1)} %pad_maximum_fusion.1), calls=%async_computation.1 | async-start | bytes 3145728 | tf_op jit(solution)/shard_map/all_to_all | solution.py:182
  86.0 1.2 fusion.25
  87.2 0.6 convolution_bitcast_fusion.4
  87.8 0.2 fusion.30
  88.1 0.2 fusion.16
  88.3 0.2 fusion.50
  88.5 37.4 %all-to-all-done.1 = bf16[128,48,128]{2,1,0:T(8,128)(2,1)S(1)} async-done(((bf16[128,48,128]{2,1,0:T(8,128)(2,1)}), bf16[128,48,128]{2,1,0:T(8,128)(2,1)S(1)}, u32[]{:S(2)}, u32[]{:S(2)}) %all-to-all-start.1) | async-done | bytes 1572896 | tf_op jit(solution)/shard_map/all_to_all | solution.py:182
  126.0 0.5 copy.267
  126.8 0.2 copy.275
  127.0 0.7 copy.385
  128.0 0.7 copy.386
  129.0 1.2 scatter-add.6
  130.5 0.7 copy.384
  131.6 1.2 scatter-add.9
  132.9 0.2 copy.283
  133.1 0.7 copy.383
  (71 shorter events, 4.2 us)
Async XLA Ops:
  0.6 2.5 %copy-start = (bf16[256,512]{1,0:T(8,128)(2,1)S(1)}, bf16[256,512]{1,0:T(8,128)(2,1)}, u32[]{:S(2)}) copy-start(bf16[256,512]{1,0:T(8,128)(2,1)} %param.10) | copy-start | bytes 786436
  0.6 2.6 %copy-start.1 = (bf16[256,512]{1,0:T(8,128)(2,1)S(1)}, bf16[256,512]{1,0:T(8,128)(2,1)}, u32[]{:S(2)}) copy-start(bf16[256,512]{1,0:T(8,128)(2,1)} %param.11) | copy-start | bytes 786436
  6.6 56.6 %all-to-all-start = ((bf16[128,48,128]{2,1,0:T(8,128)(2,1)}), bf16[128,48,128]{2,1,0:T(8,128)(2,1)S(1)}, u32[]{:S(2)}, u32[]{:S(2)}) async-start(bf16[128,48,128]{2,1,0:T(8,128)(2,1)} %pad_maximum_fusion), calls=%async_computation | async-start | bytes 3145728 | tf_op jit(solution)/shard_map/all_to_all | solution.py:151
  65.5 2.6 %copy-start.7 = (f32[2,256,256]{1,2,0:T(8,128)S(1)}, f32[2,256,256]{1,2,0:T(8,128)}, u32[]{:S(2)}) copy-start(f32[2,256,256]{1,2,0:T(8,128)} %get-tuple-element.56) | copy-start | bytes 1572868
  70.6 1.0 copy-start.2
  72.4 1.0 copy-start.4
  78.2 47.7 %all-to-all-start.1 = ((bf16[128,48,128]{2,1,0:T(8,128)(2,1)}), bf16[128,48,128]{2,1,0:T(8,128)(2,1)S(1)}, u32[]{:S(2)}, u32[]{:S(2)}) async-start(bf16[128,48,128]{2,1,0:T(8,128)(2,1)} %pad_maximum_fusion.1), calls=%async_computation.1 | async-start | bytes 3145728 | tf_op jit(solution)/shard_map/all_to_all | solution.py:182
  86.0 2.3 %copy-start.3 = (f32[2,2,128,128]{2,3,1,0:T(8,128)S(1)}, f32[2,2,128,128]{2,3,1,0:T(8,128)}, u32[]{:S(2)}) copy-start(f32[2,2,128,128]{2,3,1,0:T(8,128)} %get-tuple-element.50) | copy-start | bytes 786436
  86.0 2.3 %copy-start.5 = (bf16[2,128,1,2,128]{1,4,3,0,2:T(8,128)(2,1)S(1)}, bf16[2,128,1,2,128]{1,4,3,0,2:T(8,128)(2,1)}, u32[]{:S(2)}) copy-start(bf16[2,128,1,2,128]{1,4,3,0,2:T(8,128)(2,1)} %copy.323) | copy-start | bytes 393220
  126.5 1.2 copy-start.6

commit v4 on v3

--- a/solution.py
+++ b/solution.py
@@ -3,7 +3,7 @@
 import jax
 import jax.numpy as jnp
 from jax import lax
-from jax.sharding import PartitionSpec as P
+from jax.sharding import Mesh, PartitionSpec as P
 
 HD = 128
 STRIDE = 128
@@ -31,10 +31,10 @@
     return paired.reshape(blocks * positions, 2 * half_heads * head_dim)
 
 
-def fixed_heads(query, key_rows, value_rows, grad_rows, flat_keys, flat_values, scaling):
+def fixed_heads(query, key_rows, value_rows, grad_rows, flat_keys, flat_values, scaling, here):
     blocks_here, positions, half_heads, head_dim = query.shape
     summary_count = flat_keys.shape[0]
-    block_ids = lax.axis_index("ctx") * blocks_here + jnp.arange(blocks_here, dtype=jnp.int32)
+    block_ids = here * blocks_here + jnp.arange(blocks_here, dtype=jnp.int32)
     summary_block = jnp.arange(summary_count, dtype=jnp.int32) // SUMMARY
     earlier = (summary_block[None, :] < block_ids[:, None])[:, None, None, :]
     causal = (jnp.arange(positions)[:, None] >= jnp.arange(positions)[None, :])[None, None]
@@ -130,6 +130,10 @@
     return jnp.stack([attended, query_grad, key_grad, value_grad])
 
 
+def exchange(rows, axis):
+    return lax.all_to_all(rows, axis, 0, 0, tiled=True)
+
+
 def shards(queries, keys, values, out_grad):
     scaling = 1.0 / math.sqrt(HD)
     query_fixed, query_strided = split_heads(queries)
@@ -137,27 +141,37 @@
     value_fixed, value_strided = split_heads(values)
     grad_fixed, grad_strided = split_heads(out_grad)
     blocks_here, positions, half_heads, head_dim = query_fixed.shape
-    peers = lax.axis_size("ctx")
+    high = lax.axis_size("ctx_hi")
+    low = lax.axis_size("ctx_lo")
+    peers = high * low
     residues = positions // peers
+    here = lax.axis_index("ctx_hi") * low + lax.axis_index("ctx_lo")
 
     strided_rows = jnp.stack([query_strided, key_strided, value_strided, grad_strided])
-    strided_rows = strided_rows.reshape(4, blocks_here, peers, residues, half_heads, head_dim)
-    strided_rows = strided_rows.transpose(2, 0, 1, 3, 4, 5).reshape(peers, -1, head_dim)
+    strided_rows = strided_rows.reshape(4, blocks_here, high, low, residues, half_heads, head_dim)
+    strided_rows = strided_rows.transpose(3, 0, 1, 2, 4, 5, 6).reshape(low, -1, head_dim)
     summary_rows = jnp.stack(
         [key_fixed[:, positions - SUMMARY :], value_fixed[:, positions - SUMMARY :]]
     ).reshape(1, -1, head_dim)
-    summary_rows = jnp.broadcast_to(summary_rows, (peers,) + summary_rows.shape[1:])
+    summary_size = summary_rows.shape[1]
+    summary_rows = jnp.broadcast_to(summary_rows, (low, summary_size, head_dim))
     strided_size = strided_rows.shape[1]
-    received = lax.all_to_all(
-        jnp.concatenate([strided_rows, summary_rows], axis=1), "ctx", 0, 0, tiled=True
-    )
-    gathered = received[:, :strided_size].reshape(
-        peers, 4, blocks_here, residues, half_heads, head_dim
-    )
-    gathered = gathered.transpose(1, 0, 2, 3, 4, 5).reshape(
+    first = exchange(jnp.concatenate([strided_rows, summary_rows], axis=1), "ctx_lo")
+    strided_rows = first[:, :strided_size].reshape(
+        low, 4, blocks_here, high, residues, half_heads, head_dim
+    )
+    strided_rows = strided_rows.transpose(3, 0, 1, 2, 4, 5, 6).reshape(high, -1, head_dim)
+    summary_rows = first[:, strided_size:].reshape(1, low * summary_size, head_dim)
+    summary_rows = jnp.broadcast_to(summary_rows, (high, low * summary_size, head_dim))
+    plane_size = strided_rows.shape[1]
+    second = exchange(jnp.concatenate([strided_rows, summary_rows], axis=1), "ctx_hi")
+    gathered = second[:, :plane_size].reshape(
+        high, low, 4, blocks_here, residues, half_heads, head_dim
+    )
+    gathered = gathered.transpose(2, 0, 1, 3, 4, 5, 6).reshape(
         4, peers * blocks_here, residues, half_heads, head_dim
     )
-    summaries = received[:, strided_size:].reshape(
+    summaries = second[:, plane_size:].reshape(
         peers, 2, blocks_here * SUMMARY, half_heads, head_dim
     )
     summaries = summaries.transpose(1, 0, 2, 3, 4).reshape(
@@ -172,26 +186,39 @@
         summaries[0],
         summaries[1],
         scaling,
+        here,
     )
     strided_out = strided_heads(gathered[0], gathered[1], gathered[2], gathered[3], scaling)
 
-    strided_out = strided_out.reshape(4, peers, -1, head_dim).transpose(1, 0, 2, 3)
-    strided_out = strided_out.reshape(peers, -1, head_dim)
-    terms = terms.astype(jnp.bfloat16).reshape(2, peers, -1, head_dim).transpose(1, 0, 2, 3)
-    terms = terms.reshape(peers, -1, head_dim)
-    returned = lax.all_to_all(
-        jnp.concatenate([strided_out, terms], axis=1), "ctx", 0, 0, tiled=True
-    )
-    strided_out = returned[:, :strided_size].reshape(
-        peers, 4, blocks_here, residues, half_heads, head_dim
-    )
-    strided_out = strided_out.transpose(1, 2, 0, 3, 4, 5).reshape(
+    strided_out = strided_out.reshape(
+        4, high, low, blocks_here, residues, half_heads, head_dim
+    ).transpose(1, 2, 0, 3, 4, 5, 6)
+    strided_out = strided_out.reshape(high, -1, head_dim)
+    terms = terms.astype(jnp.bfloat16).reshape(2, high, low, -1, head_dim)
+    terms = terms.transpose(1, 2, 0, 3, 4).reshape(high, -1, head_dim)
+    back = exchange(jnp.concatenate([strided_out, terms], axis=1), "ctx_hi")
+    strided_out = back[:, :plane_size].reshape(
+        high, low, 4, blocks_here, residues, half_heads, head_dim
+    )
+    strided_out = strided_out.transpose(1, 0, 2, 3, 4, 5, 6).reshape(low, -1, head_dim)
+    terms = jnp.sum(back[:, plane_size:].astype(jnp.float32), axis=0).astype(jnp.bfloat16)
+    terms = terms.reshape(low, -1, head_dim)
+    back = exchange(jnp.concatenate([strided_out, terms], axis=1), "ctx_lo")
+    strided_out = back[:, :strided_size].reshape(
+        low, high, 4, blocks_here, residues, half_heads, head_dim
+    )
+    strided_out = strided_out.transpose(2, 3, 1, 0, 4, 5, 6).reshape(
         4, blocks_here, positions, half_heads, head_dim
     )
-    shares = jnp.sum(returned[:, strided_size:].astype(jnp.float32), axis=0)
+    shares = jnp.sum(back[:, strided_size:].astype(jnp.float32), axis=0)
     shares = shares.reshape(2, blocks_here, SUMMARY, half_heads, head_dim)
-    key_grad = key_grad.at[:, positions - SUMMARY :].add(shares[0])
-    value_grad = value_grad.at[:, positions - SUMMARY :].add(shares[1])
+    key_grad = jnp.concatenate(
+        [key_grad[:, : positions - SUMMARY], key_grad[:, positions - SUMMARY :] + shares[0]], axis=1
+    )
+    value_grad = jnp.concatenate(
+        [value_grad[:, : positions - SUMMARY], value_grad[:, positions - SUMMARY :] + shares[1]],
+        axis=1,
+    )
     return (
         join_heads(attended, strided_out[0]),
         join_heads(query_grad.astype(jnp.bfloat16), strided_out[1]),
@@ -201,10 +228,14 @@
 
 
 def solution(mesh):
+    peers, heads = mesh.devices.shape
+    high = 4 if peers % 4 == 0 else 1
+    split = Mesh(mesh.devices.reshape(high, peers // high, heads), ("ctx_hi", "ctx_lo", "head"))
+    spec = P(("ctx_hi", "ctx_lo"), "head")
     return jax.shard_map(
         shards,
-        mesh=mesh,
-        in_specs=(P("ctx", "head"), P("ctx", "head"), P("ctx", "head"), P("ctx", "head")),
-        out_specs=(P("ctx", "head"), P("ctx", "head"), P("ctx", "head"), P("ctx", "head")),
+        mesh=split,
+        in_specs=(spec, spec, spec, spec),
+        out_specs=(spec, spec, spec, spec),
         check_vma=False,
     )

time: 134 us -> 138 us (1.030)
  blocking collectives: 0 us -> 56.2 us
  waiting for transfers between devices: 75.5 us -> 38.9 us
  starting transfers between devices: 24.4 us -> 11.4 us
  matrix products: 11.6 us -> 9.25 us
  other arithmetic: 5.59 us -> 4.09 us
    all_to_all x0 -> x2, blocking collectives: none -> 56.2 us  [exchange(): return lax.all_to_all(rows, axis, 0, 0, tiled=True)]
    all_to_all x2, waiting for transfers between devices: 75.5 us -> 38.9 us  [exchange(): return lax.all_to_all(rows, axis, 0, 0, tiled=True)]
    all_to_all x2, starting transfers between devices: 24.4 us -> 11.4 us  [exchange(): return lax.all_to_all(rows, axis, 0, 0, tiled=True)]
    scatter-add x2 -> x0, local copies, waits for them, and re-layouts: 2.49 us -> none  [the longest x1 1.25 us: shards(): value_grad = value_grad.at[:, positions - SUMMARY:].add(shares[1])]
    concatenate x0 -> x4, local copies, waits for them, and re-layouts: none -> 1.53 us  [the longest x1 1.18 us: shards(): back = exchange(jnp.concatenate([strided_out, terms], axis=1), 'ctx_lo')]
    unnamed x25 -> x24, local copies, waits for them, and re-layouts: 4.36 us -> 4.25 us
  transfers between devices with their start and end apart: 2 -> 2, of which waited for: 2 -> 2; matrix products, arithmetic and copies ran while one was open for 3% -> 2% of each run, Pallas kernels for 0% -> 0%
where the time goes in v4:
time: 138 us; the launch traced here: 137 us
  blocking collectives  56.2 us (41%)
  waiting for transfers between devices  38.9 us (28%)
  local copies, waits for them, and re-layouts  15.7 us (11%)
  starting transfers between devices  11.4 us (8%)
  matrix products  9.25 us (7%)
  other arithmetic  4.09 us (3%)
  between operations  1.47 us (1%)
    all_to_all x2, blocking collectives, exchange(): return lax.all_to_all(rows, axis, 0, 0, tiled=True)  56.2 us
    all_to_all x2, waiting for transfers between devices, exchange(): return lax.all_to_all(rows, axis, 0, 0, tiled=True)  38.9 us
    all_to_all x2, starting transfers between devices, exchange(): return lax.all_to_all(rows, axis, 0, 0, tiled=True)  11.4 us
    unnamed x24, local copies, waits for them, and re-layouts  4.25 us
  transfers between devices with their start and end apart: 2, of which 2 were waited for; matrix products, arithmetic and copies ran while one was open for 2% of the time, Pallas kernels for 0%

profile of v4, /device:TPU:1, one launch (start us, length us, event | category | flops | bytes accessed | tf_op | source)
XLA Modules:
  0.0 137.1 jit_solution(1457170418051215837)
XLA Ops:
  0.6 1.1 reshape.365
  1.7 1.1 reshape.367
  2.8 0.4 fusion.73
  4.2 0.3 copy.409
  4.5 35.4 %all_to_all.20 = bf16[32,96,128]{2,1,0:T(8,128)(2,1)S(1)} all-to-all(bf16[32,96,128]{2,1,0:T(8,128)(2,1)S(1)} %copy.409), channel_id=1, replica_groups=mesh['ctx_hi'=4,'ctx_lo'=32,'head'=4] {'ctx_lo'}, dimensions={0} | all-to-all | bytes 1572864 | tf_op jit(solution)/shard_map/all_to_all | solution.py:134
  40.0 0.4 copy.410
  40.5 1.3 pad_maximum_fusion
  41.8 4.0 %all-to-all-start.1 = ((bf16[4,1536,128]{2,1,0:T(8,128)(2,1)}), bf16[4,1536,128]{2,1,0:T(8,128)(2,1)S(1)}, u32[]{:S(2)}, u32[]{:S(2)}) async-start(bf16[4,1536,128]{2,1,0:T(8,128)(2,1)} %pad_maximum_fusion), calls=%async_computation.1 | async-start | bytes 3145728 | tf_op jit(solution)/shard_map/all_to_all | solution.py:134
  45.8 0.8 copy.511
  46.8 0.2 fusion.77
  47.1 18.3 %all-to-all-done.1 = bf16[4,1536,128]{2,1,0:T(8,128)(2,1)S(1)} async-done(((bf16[4,1536,128]{2,1,0:T(8,128)(2,1)}), bf16[4,1536,128]{2,1,0:T(8,128)(2,1)S(1)}, u32[]{:S(2)}, u32[]{:S(2)}) %all-to-all-start.1) | async-done | bytes 1572896 | tf_op jit(solution)/shard_map/all_to_all | solution.py:134
  65.7 0.2 copy.430
  66.6 1.1 fusion.79
  67.7 1.3 fusion.27
  69.0 1.9 %multiply_reduce_fusion.1 = (f32[256,2]{0,1:T(2,128)S(1)}, bf16[256,1,2,128]{0,3,2,1:T(8,128)(2,1)}) fusion(f32[256,1,2,128]{0,3,2,1:T(8,128)S(1)} %copy.431, bf16[256,2,128]{2,0,1:T(8,128)(2,1)S(1)} %bitcast.282, f32[2,256,256]{1,2,0:T(8,128)} %get-tuple-element.32, f32[2,256]{1,0:T(2,128)S(1)} %get-tuple-element.31), kind=kOutput, calls=%fused_computation.84 | convolution fusion | flops 34078208 | bytes 1052672 | tf_op jit(solution)/shard_map/rgbc,crgd->brgd/dot_general | solution.py:110
  71.0 0.2 fusion.14
  71.2 0.2 fusion.28
  71.5 0.2 fusion.29
  71.8 0.7 fusion.70
  73.0 1.0 maximum_bitcast_fusion.2
  74.0 0.8 copy.442
  74.8 0.5 fusion.78
  75.4 0.3 fusion.4
  75.7 0.3 fusion.33
  76.1 0.4 convolution_bitcast_fusion.6
  76.4 0.4 fusion.11
  77.0 0.3 multiply_reduce_fusion
  77.2 0.6 fusion.2
  77.9 0.4 fusion.10
  78.3 0.5 copy.447
  78.9 0.5 copy.449
  79.8 20.8 %all_to_all.21 = bf16[4,1536,128]{2,1,0:T(8,128)(2,1)S(1)} all-to-all(bf16[4,1536,128]{2,1,0:T(8,128)(2,1)S(1)} %pad_maximum_fusion.1), channel_id=1, replica_groups=mesh['ctx_hi'=4,'ctx_lo'=32,'head'=4] {'ctx_hi'}, dimensions={0} | all-to-all | bytes 3145728 | tf_op jit(solution)/shard_map/all_to_all | solution.py:134
  101.2 1.2 copy.453
  102.4 7.4 %all-to-all-start.3 = ((bf16[32,96,128]{2,1,0:T(8,128)(2,1)}), bf16[32,96,128]{2,1,0:T(8,128)(2,1)S(1)}, u32[]{:S(2)}, u32[]{:S(2)}) async-start(bf16[32,96,128]{2,1,0:T(8,128)(2,1)} %copy.453), calls=%async_computation.3 | async-start | bytes 1572864 | tf_op jit(solution)/shard_map/all_to_all | solution.py:134
  110.0 0.5 convolution_bitcast_fusion.5
  110.5 0.2 fusion.30
  110.8 0.2 convolution_bitcast_fusion.2
  111.0 0.2 fusion.16
  111.3 20.6 %all-to-all-done.3 = bf16[32,96,128]{2,1,0:T(8,128)(2,1)S(1)} async-done(((bf16[32,96,128]{2,1,0:T(8,128)(2,1)}), bf16[32,96,128]{2,1,0:T(8,128)(2,1)S(1)}, u32[]{:S(2)}, u32[]{:S(2)}) %all-to-all-start.3) | async-done | bytes 786464 | tf_op jit(solution)/shard_map/all_to_all | solution.py:134
  132.0 0.3 copy.512
  132.5 0.2 copy.474
  132.7 0.7 copy.577
  133.7 0.2 copy.465
  133.9 0.7 copy.579
  134.8 0.2 copy.457
  135.0 0.7 copy.580
  136.2 0.2 copy.470
  136.4 0.7 copy.578
  (90 shorter events, 5.1 us)
Async XLA Ops:
  0.6 2.6 %copy-start.2 = (bf16[256,512]{1,0:T(8,128)(2,1)S(1)}, bf16[256,512]{1,0:T(8,128)(2,1)}, u32[]{:S(2)}) copy-start(bf16[256,512]{1,0:T(8,128)(2,1)} %param.6) | copy-start | bytes 786436
  1.7 1.9 %copy-start.3 = (bf16[256,512]{1,0:T(8,128)(2,1)S(1)}, bf16[256,512]{1,0:T(8,128)(2,1)}, u32[]{:S(2)}) copy-start(bf16[256,512]{1,0:T(8,128)(2,1)} %param.7) | copy-start | bytes 786436
  41.8 23.6 %all-to-all-start.1 = ((bf16[4,1536,128]{2,1,0:T(8,128)(2,1)}), bf16[4,1536,128]{2,1,0:T(8,128)(2,1)S(1)}, u32[]{:S(2)}, u32[]{:S(2)}) async-start(bf16[4,1536,128]{2,1,0:T(8,128)(2,1)} %pad_maximum_fusion), calls=%async_computation.1 | async-start | bytes 3145728 | tf_op jit(solution)/shard_map/all_to_all | solution.py:134
  67.7 3.3 %copy-start.7 = (f32[2,256,256]{1,2,0:T(8,128)S(1)}, f32[2,256,256]{1,2,0:T(8,128)}, u32[]{:S(2)}) copy-start(f32[2,256,256]{1,2,0:T(8,128)} %get-tuple-element.32) | copy-start | bytes 1572868
  71.8 1.1 copy-start.6
  72.5 2.8 %copy-start = (bf16[1,128,8,2,128]{4,3,2,0,1:T(2,128)(2,1)}, bf16[1,128,8,2,128]{4,3,2,0,1:T(2,128)(2,1)S(1)}, u32[]{:S(2)}) copy-start(bf16[1,128,8,2,128]{4,3,2,0,1:T(2,128)(2,1)S(1)} %get-tuple-element.5) | copy-start | bytes 1572868
  76.1 0.9 copy-start.4
  101.2 8.8 %copy-start.1 = (bf16[1,128,8,2,128]{4,3,2,0,1:T(2,128)(2,1)S(1)}, bf16[1,128,8,2,128]{4,3,2,0,1:T(2,128)(2,1)}, u32[]{:S(2)}) copy-start(bf16[1,128,8,2,128]{4,3,2,0,1:T(2,128)(2,1)} %copy-done) | copy-start | bytes 1572868
  102.4 29.6 %all-to-all-start.3 = ((bf16[32,96,128]{2,1,0:T(8,128)(2,1)}), bf16[32,96,128]{2,1,0:T(8,128)(2,1)S(1)}, u32[]{:S(2)}, u32[]{:S(2)}) async-start(bf16[32,96,128]{2,1,0:T(8,128)(2,1)} %copy.453), calls=%async_computation.3 | async-start | bytes 1572864 | tf_op jit(solution)/shard_map/all_to_all | solution.py:134
  109.8 1.0 copy-start.5

commit v5 on v3

--- a/solution.py
+++ b/solution.py
@@ -190,8 +190,13 @@
     )
     shares = jnp.sum(returned[:, strided_size:].astype(jnp.float32), axis=0)
     shares = shares.reshape(2, blocks_here, SUMMARY, half_heads, head_dim)
-    key_grad = key_grad.at[:, positions - SUMMARY :].add(shares[0])
-    value_grad = value_grad.at[:, positions - SUMMARY :].add(shares[1])
+    key_grad = jnp.concatenate(
+        [key_grad[:, : positions - SUMMARY], key_grad[:, positions - SUMMARY :] + shares[0]], axis=1
+    )
+    value_grad = jnp.concatenate(
+        [value_grad[:, : positions - SUMMARY], value_grad[:, positions - SUMMARY :] + shares[1]],
+        axis=1,
+    )
     return (
         join_heads(attended, strided_out[0]),
         join_heads(query_grad.astype(jnp.bfloat16), strided_out[1]),

time: 134 us -> 133 us (level)
  local copies, waits for them, and re-layouts: 15.4 us -> 13 us
    scatter-add x2 -> x0, local copies, waits for them, and re-layouts: 2.49 us -> none  [the longest x1 1.25 us: shards(): value_grad = value_grad.at[:, positions - SUMMARY:].add(shares[1])]
    unnamed x25 -> x29, local copies, waits for them, and re-layouts: 4.36 us -> 4.38 us
where the time goes in v5:
time: 133 us; the launch traced here: 132 us
  waiting for transfers between devices  75.3 us (57%)
  starting transfers between devices  24.4 us (18%)
  local copies, waits for them, and re-layouts  13 us (10%)
  matrix products  12.6 us (9%)
  other arithmetic  5.72 us (4%)
  between operations  1.35 us (1%)
    all_to_all x1, waiting for transfers between devices, shards(): lax.all_to_all(jnp.concatenate([strided_rows, summary_rows], axis=1), 'ct...  38 us
    all_to_all x1, waiting for transfers between devices, shards(): lax.all_to_all(jnp.concatenate([strided_out, terms], axis=1), 'ctx', 0, 0...  37.3 us
    all_to_all x1, starting transfers between devices, shards(): lax.all_to_all(jnp.concatenate([strided_rows, summary_rows], axis=1), 'ct...  16.6 us
    all_to_all x1, starting transfers between devices, shards(): lax.all_to_all(jnp.concatenate([strided_out, terms], axis=1), 'ctx', 0, 0...  7.73 us
    unnamed x29, local copies, waits for them, and re-layouts  4.38 us
  transfers between devices with their start and end apart: 2, of which 2 were waited for; matrix products, arithmetic and copies ran while one was open for 3% of the time, Pallas kernels for 0%

profile of v5, /device:TPU:1, one launch (start us, length us, event | category | flops | bytes accessed | tf_op | source)
XLA Modules:
  0.0 132.3 jit_solution(9323755390743438407)
XLA Ops:
  0.7 1.1 reshape.342
  1.7 1.0 reshape.344
  2.7 0.4 slice_bitcast_fusion.6
  3.3 0.4 slice_bitcast_fusion.5
  3.7 1.0 maximum_bitcast_fusion.1
  4.8 0.3 copy.221
  5.4 1.3 pad_maximum_fusion
  6.6 16.6 %all-to-all-start = ((bf16[128,48,128]{2,1,0:T(8,128)(2,1)}), bf16[128,48,128]{2,1,0:T(8,128)(2,1)S(1)}, u32[]{:S(2)}, u32[]{:S(2)}) async-start(bf16[128,48,128]{2,1,0:T(8,128)(2,1)} %pad_maximum_fusion), calls=%async_computation | async-start | bytes 3145728 | tf_op jit(solution)/shard_map/all_to_all | solution.py:151
  23.3 0.8 copy.319
  24.3 0.9 fusion.73
  25.2 38.0 %all-to-all-done = bf16[128,48,128]{2,1,0:T(8,128)(2,1)S(1)} async-done(((bf16[128,48,128]{2,1,0:T(8,128)(2,1)}), bf16[128,48,128]{2,1,0:T(8,128)(2,1)S(1)}, u32[]{:S(2)}, u32[]{:S(2)}) %all-to-all-start) | async-done | bytes 1572896 | tf_op jit(solution)/shard_map/all_to_all | solution.py:151
  63.5 0.2 copy.242
  64.5 1.1 fusion.75
  65.6 1.3 %fusion.27 = bf16[256,1,2,128]{0,3,2,1:T(8,128)(2,1)S(1)} fusion(bf16[256,2,128]{2,0,1:T(8,128)(2,1)S(1)} %bitcast.264, f32[2,256,256]{1,2,0:T(8,128)} %get-tuple-element.32, f32[2,256]{1,0:T(2,128)S(1)} %get-tuple-element.31), kind=kOutput, calls=%fused_computation.49 | convolution fusion | flops 33882112 | bytes 788480 | tf_op jit(solution)/shard_map/rgbc,brgd->crgd/dot_general | solution.py:127
  66.9 1.3 multiply_reduce_fusion.1
  68.2 0.2 fusion.14
  68.4 0.2 fusion.28
  68.7 0.2 fusion.29
  69.0 0.4 copy.317
  70.0 0.5 maximum_bitcast_fusion.2
  70.6 0.3 copy.263
  71.0 0.6 fusion.74
  71.7 0.3 fusion.4
  72.0 0.3 fusion.33
  72.4 0.6 convolution_bitcast_fusion.6
  73.0 0.4 fusion.11
  73.4 0.9 multiply_reduce_fusion
  74.3 1.7 %fusion.2 = bf16[2,2,128,1024]{2,3,0,1:T(8,128)(2,1)S(1)} fusion(f32[2,2,128]{2,0,1:T(2,128)S(1)} %copy.257, f32[2,2,128]{2,0,1:T(2,128)S(1)} %copy.231, f32[2,2,128,1024]{2,3,0,1:T(8,128)S(1)} %get-tuple-element.28, f32[2,2,128]{2,0,1:T(2,128)S(1)} %copy.226, bf16[1,128,8,2,128]{4,1,3,2,0:T(8,128)(2,1)S(1)} %get-tuple-element.4, ...), kind=kOutput, calls=%fused_computation.3 | convolution fusion | flops 136839168 | bytes 3807232 | tf_op jit(solution)/shard_map/bqgd,mgd->bgqm/dot_general | solution.py:68
  76.1 0.4 fusion.10
  76.5 0.5 copy.259
  77.0 0.5 copy.261
  77.9 1.3 pad_maximum_fusion.1
  79.2 7.7 %all-to-all-start.1 = ((bf16[128,48,128]{2,1,0:T(8,128)(2,1)}), bf16[128,48,128]{2,1,0:T(8,128)(2,1)S(1)}, u32[]{:S(2)}, u32[]{:S(2)}) async-start(bf16[128,48,128]{2,1,0:T(8,128)(2,1)} %pad_maximum_fusion.1), calls=%async_computation.1 | async-start | bytes 3145728 | tf_op jit(solution)/shard_map/all_to_all | solution.py:182
  86.9 1.3 fusion.25
  88.2 0.6 convolution_bitcast_fusion.5
  88.8 0.2 fusion.30
  89.0 0.2 convolution_bitcast_fusion.2
  89.3 0.2 fusion.16
  89.6 37.3 %all-to-all-done.1 = bf16[128,48,128]{2,1,0:T(8,128)(2,1)S(1)} async-done(((bf16[128,48,128]{2,1,0:T(8,128)(2,1)}), bf16[128,48,128]{2,1,0:T(8,128)(2,1)S(1)}, u32[]{:S(2)}, u32[]{:S(2)}) %all-to-all-start.1) | async-done | bytes 1572896 | tf_op jit(solution)/shard_map/all_to_all | solution.py:182
  126.9 0.5 copy.264
  127.5 0.2 convert_reduce_fusion
  127.7 0.2 copy.272
  127.9 0.7 copy.381
  128.7 0.2 copy.265
  128.9 0.7 copy.382
  130.0 0.2 copy.275
  130.2 0.7 copy.380
  131.6 0.7 copy.379
  (73 shorter events, 3.9 us)
Async XLA Ops:
  0.6 2.5 %copy-start.2 = (bf16[256,512]{1,0:T(8,128)(2,1)S(1)}, bf16[256,512]{1,0:T(8,128)(2,1)}, u32[]{:S(2)}) copy-start(bf16[256,512]{1,0:T(8,128)(2,1)} %param.6) | copy-start | bytes 786436
  0.6 2.6 %copy-start.3 = (bf16[256,512]{1,0:T(8,128)(2,1)S(1)}, bf16[256,512]{1,0:T(8,128)(2,1)}, u32[]{:S(2)}) copy-start(bf16[256,512]{1,0:T(8,128)(2,1)} %param.7) | copy-start | bytes 786436
  3.7 69.7 %copy-start = (bf16[2,128,1,2,128]{4,3,1,0,2:T(2,128)(2,1)}, bf16[2,128,1,2,128]{4,3,1,0,2:T(2,128)(2,1)S(1)}, u32[]{:S(2)}) copy-start(bf16[2,128,1,2,128]{4,3,1,0,2:T(2,128)(2,1)S(1)} %get-tuple-element.22) | copy-start | bytes 393220
  6.6 56.6 %all-to-all-start = ((bf16[128,48,128]{2,1,0:T(8,128)(2,1)}), bf16[128,48,128]{2,1,0:T(8,128)(2,1)S(1)}, u32[]{:S(2)}, u32[]{:S(2)}) async-start(bf16[128,48,128]{2,1,0:T(8,128)(2,1)} %pad_maximum_fusion), calls=%async_computation | async-start | bytes 3145728 | tf_op jit(solution)/shard_map/all_to_all | solution.py:151
  24.2 48.8 %copy-start.1 = (bf16[2,128,1,2,128]{1,4,0,3,2:T(8,128)(2,1)}, bf16[2,128,1,2,128]{1,4,0,3,2:T(8,128)(2,1)S(1)}, u32[]{:S(2)}) copy-start(bf16[2,128,1,2,128]{1,4,0,3,2:T(8,128)(2,1)S(1)} %copy.321) | copy-start | bytes 393220
  65.6 2.6 %copy-start.9 = (f32[2,256,256]{1,2,0:T(8,128)S(1)}, f32[2,256,256]{1,2,0:T(8,128)}, u32[]{:S(2)}) copy-start(f32[2,256,256]{1,2,0:T(8,128)} %get-tuple-element.32) | copy-start | bytes 1572868
  70.6 1.0 copy-start.4
  72.4 1.0 copy-start.6
  79.2 47.7 %all-to-all-start.1 = ((bf16[128,48,128]{2,1,0:T(8,128)(2,1)}), bf16[128,48,128]{2,1,0:T(8,128)(2,1)S(1)}, u32[]{:S(2)}, u32[]{:S(2)}) async-start(bf16[128,48,128]{2,1,0:T(8,128)(2,1)} %pad_maximum_fusion.1), calls=%async_computation.1 | async-start | bytes 3145728 | tf_op jit(solution)/shard_map/all_to_all | solution.py:182
  86.9 2.1 %copy-start.5 = (f32[2,2,128,128]{2,3,1,0:T(8,128)S(1)}, f32[2,2,128,128]{2,3,1,0:T(8,128)}, u32[]{:S(2)}) copy-start(f32[2,2,128,128]{2,3,1,0:T(8,128)} %get-tuple-element.26) | copy-start | bytes 786436
  86.9 2.1 %copy-start.7 = (bf16[2,128,1,2,128]{1,4,3,0,2:T(8,128)(2,1)S(1)}, bf16[2,128,1,2,128]{1,4,3,0,2:T(8,128)(2,1)}, u32[]{:S(2)}) copy-start(bf16[2,128,1,2,128]{1,4,3,0,2:T(8,128)(2,1)} %copy.319) | copy-start | bytes 393220
  127.4 1.2 copy-start.8

commit v6 on v5

--- a/solution.py
+++ b/solution.py
@@ -1,8 +1,11 @@
+import functools
 import math
 
 import jax
 import jax.numpy as jnp
 from jax import lax
+from jax.experimental import pallas as pl
+from jax.experimental.pallas import tpu as pltpu
 from jax.sharding import PartitionSpec as P
 
 HD = 128
@@ -31,68 +34,106 @@
     return paired.reshape(blocks * positions, 2 * half_heads * head_dim)
 
 
-def fixed_heads(query, key_rows, value_rows, grad_rows, flat_keys, flat_values, scaling):
+def product(left, right, left_dim, right_dim):
+    return lax.dot_general(
+        left, right, (((left_dim,), (right_dim,)), ((), ())), preferred_element_type=jnp.float32
+    )
+
+
+def fixed_kernel(
+    start_ref, q_ref, k_ref, v_ref, g_ref, sk_ref, sv_ref,
+    att_ref, qg_ref, kg_ref, vg_ref, kt_ref, vt_ref, *, scaling,
+):
+    blocks_here, half_heads, positions, _ = q_ref.shape
+    summary_count = sk_ref.shape[1]
+    causal = lax.broadcasted_iota(jnp.int32, (positions, positions), 0) >= lax.broadcasted_iota(
+        jnp.int32, (positions, positions), 1
+    )
+    summary_block = lax.broadcasted_iota(jnp.int32, (positions, summary_count), 1) // SUMMARY
+    for head in range(half_heads):
+        summary_keys = sk_ref[head]
+        summary_values = sv_ref[head]
+        key_terms = jnp.zeros(summary_keys.shape, jnp.float32)
+        value_terms = jnp.zeros(summary_values.shape, jnp.float32)
+        for block in range(blocks_here):
+            query = q_ref[block, head]
+            key_rows = k_ref[block, head]
+            value_rows = v_ref[block, head]
+            grad_rows = g_ref[block, head]
+            earlier = summary_block < start_ref[0] + block
+            local_scores = jnp.where(causal, product(query, key_rows, 1, 1) * scaling, -jnp.inf)
+            summary_scores = jnp.where(
+                earlier, product(query, summary_keys, 1, 1) * scaling, -jnp.inf
+            )
+            row_max = jnp.maximum(
+                jnp.max(local_scores, axis=1, keepdims=True),
+                jnp.max(summary_scores, axis=1, keepdims=True),
+            )
+            local_raised = jnp.exp(local_scores - row_max)
+            summary_raised = jnp.exp(summary_scores - row_max)
+            totals = jnp.sum(local_raised, axis=1, keepdims=True) + jnp.sum(
+                summary_raised, axis=1, keepdims=True
+            )
+            local_weights = local_raised / totals
+            summary_weights = summary_raised / totals
+            local_low = local_weights.astype(jnp.bfloat16)
+            summary_low = summary_weights.astype(jnp.bfloat16)
+            attended = (
+                product(local_low, value_rows, 1, 0) + product(summary_low, summary_values, 1, 0)
+            ).astype(jnp.bfloat16)
+            row_delta = jnp.sum(
+                grad_rows.astype(jnp.float32) * attended.astype(jnp.float32), axis=1, keepdims=True
+            )
+            local_dscores = (
+                local_weights * (product(grad_rows, value_rows, 1, 1) - row_delta)
+            ).astype(jnp.bfloat16)
+            summary_dscores = (
+                summary_weights * (product(grad_rows, summary_values, 1, 1) - row_delta)
+            ).astype(jnp.bfloat16)
+            att_ref[block, head] = attended
+            qg_ref[block, head] = (
+                (product(local_dscores, key_rows, 1, 0) + product(summary_dscores, summary_keys, 1, 0))
+                * scaling
+            ).astype(jnp.bfloat16)
+            kg_ref[block, head] = product(local_dscores, query, 0, 0) * scaling
+            vg_ref[block, head] = product(local_low, grad_rows, 0, 0)
+            key_terms = key_terms + product(summary_dscores, query, 0, 0)
+            value_terms = value_terms + product(summary_low, grad_rows, 0, 0)
+        kt_ref[head] = key_terms * scaling
+        vt_ref[head] = value_terms
+
+
+def fixed_heads(query, key_rows, value_rows, grad_rows, flat_keys, flat_values, scaling, here):
     blocks_here, positions, half_heads, head_dim = query.shape
     summary_count = flat_keys.shape[0]
-    block_ids = lax.axis_index("ctx") * blocks_here + jnp.arange(blocks_here, dtype=jnp.int32)
-    summary_block = jnp.arange(summary_count, dtype=jnp.int32) // SUMMARY
-    earlier = (summary_block[None, :] < block_ids[:, None])[:, None, None, :]
-    causal = (jnp.arange(positions)[:, None] >= jnp.arange(positions)[None, :])[None, None]
-    local_scores = (
-        jnp.einsum("bqgd,bkgd->bgqk", query, key_rows, preferred_element_type=jnp.float32) * scaling
-    )
-    summary_scores = (
-        jnp.einsum("bqgd,mgd->bgqm", query, flat_keys, preferred_element_type=jnp.float32) * scaling
-    )
-    local_scores = jnp.where(causal, local_scores, -jnp.inf)
-    summary_scores = jnp.where(earlier, summary_scores, -jnp.inf)
-    row_max = jnp.maximum(jnp.max(local_scores, axis=-1), jnp.max(summary_scores, axis=-1))[
-        ..., None
-    ]
-    local_raised = jnp.exp(local_scores - row_max)
-    summary_raised = jnp.exp(summary_scores - row_max)
-    totals = jnp.sum(local_raised, axis=-1, keepdims=True) + jnp.sum(
-        summary_raised, axis=-1, keepdims=True
-    )
-    local_weights = local_raised / totals
-    summary_weights = summary_raised / totals
-    local_low = local_weights.astype(jnp.bfloat16)
-    summary_low = summary_weights.astype(jnp.bfloat16)
-    attended = (
-        jnp.einsum("bgqk,bkgd->bqgd", local_low, value_rows, preferred_element_type=jnp.float32)
-        + jnp.einsum("bgqm,mgd->bqgd", summary_low, flat_values, preferred_element_type=jnp.float32)
-    ).astype(jnp.bfloat16)
-    local_dweights = jnp.einsum(
-        "bqgd,bkgd->bgqk", grad_rows, value_rows, preferred_element_type=jnp.float32
-    )
-    summary_dweights = jnp.einsum(
-        "bqgd,mgd->bgqm", grad_rows, flat_values, preferred_element_type=jnp.float32
-    )
-    row_delta = jnp.sum(grad_rows.astype(jnp.float32) * attended.astype(jnp.float32), axis=-1)
-    row_delta = jnp.transpose(row_delta, (0, 2, 1))[..., None]
-    local_dscores = (local_weights * (local_dweights - row_delta)).astype(jnp.bfloat16)
-    summary_dscores = (summary_weights * (summary_dweights - row_delta)).astype(jnp.bfloat16)
-    query_grad = (
-        jnp.einsum("bgqk,bkgd->bqgd", local_dscores, key_rows, preferred_element_type=jnp.float32)
-        + jnp.einsum(
-            "bgqm,mgd->bqgd", summary_dscores, flat_keys, preferred_element_type=jnp.float32
-        )
-    ) * scaling
-    key_grad = (
-        jnp.einsum("bgqk,bqgd->bkgd", local_dscores, query, preferred_element_type=jnp.float32)
-        * scaling
-    )
-    value_grad = jnp.einsum(
-        "bgqk,bqgd->bkgd", local_low, grad_rows, preferred_element_type=jnp.float32
-    )
-    key_terms = (
-        jnp.einsum("bgqm,bqgd->mgd", summary_dscores, query, preferred_element_type=jnp.float32)
-        * scaling
-    )
-    value_terms = jnp.einsum(
-        "bgqm,bqgd->mgd", summary_low, grad_rows, preferred_element_type=jnp.float32
-    )
-    return (attended, query_grad, key_grad, value_grad, jnp.stack([key_terms, value_terms]))
+    by_head = lambda rows: rows.transpose(0, 2, 1, 3)
+    local_shape = (blocks_here, half_heads, positions, head_dim)
+    summary_shape = (half_heads, summary_count, head_dim)
+    vmem = pl.BlockSpec(memory_space=pltpu.VMEM)
+    outs = pl.pallas_call(
+        functools.partial(fixed_kernel, scaling=scaling),
+        out_shape=(
+            jax.ShapeDtypeStruct(local_shape, jnp.bfloat16),
+            jax.ShapeDtypeStruct(local_shape, jnp.bfloat16),
+            jax.ShapeDtypeStruct(local_shape, jnp.float32),
+            jax.ShapeDtypeStruct(local_shape, jnp.float32),
+            jax.ShapeDtypeStruct(summary_shape, jnp.float32),
+            jax.ShapeDtypeStruct(summary_shape, jnp.float32),
+        ),
+        in_specs=[pl.BlockSpec(memory_space=pltpu.SMEM)] + [vmem] * 6,
+        out_specs=[vmem] * 6,
+    )(
+        (here * blocks_here).reshape(1).astype(jnp.int32),
+        by_head(query),
+        by_head(key_rows),
+        by_head(value_rows),
+        by_head(grad_rows),
+        flat_keys.transpose(1, 0, 2),
+        flat_values.transpose(1, 0, 2),
+    )
+    attended, query_grad, key_grad, value_grad = (by_head(out) for out in outs[:4])
+    terms = jnp.stack([outs[4], outs[5]]).transpose(0, 2, 1, 3)
+    return (attended, query_grad, key_grad, value_grad, terms)
 
 
 def strided_heads(query_all, keys_all, values_all, grads_all, scaling):
@@ -172,6 +213,7 @@
         summaries[0],
         summaries[1],
         scaling,
+        lax.axis_index("ctx"),
     )
     strided_out = strided_heads(gathered[0], gathered[1], gathered[2], gathered[3], scaling)
 

time: 133 us -> 134 us (level)
  matrix products: 12.6 us -> 1.52 us
  Pallas kernels: 0 us -> 6.94 us
  waiting for transfers between devices: 75.3 us -> 78.5 us
  local copies, waits for them, and re-layouts: 13 us -> 15.3 us
    dot_general x12 -> x0, matrix products: 8.13 us -> none  [the longest x1 1.71 us: fixed_heads(): jnp.einsum('bqgd,mgd->bgqm', grad_rows, flat_values, preferred_element_ty...]
    pallas_call x0 -> x1, Pallas kernels: none -> 6.94 us  [fixed_heads(): pl.pallas_call(functools.partial(fixed_kernel, scaling=scaling), out_shap...]
    all_to_all x1, waiting for transfers between devices: 37.3 us -> 39.9 us  [shards(): lax.all_to_all(jnp.concatenate([strided_out, terms], axis=1), 'ctx', 0, 0...]
    another operation x0 -> x2, other arithmetic: none -> 1.45 us  [fixed_heads(): terms = jnp.stack([outs[4], outs[5]]).transpose(0, 2, 1, 3)]
    unnamed x29 -> x28, local copies, waits for them, and re-layouts: 4.38 us -> 5.08 us
  transfers between devices with their start and end apart: 2 -> 2, of which waited for: 2 -> 2; matrix products, arithmetic and copies ran while one was open for 3% -> 1% of each run, Pallas kernels for 0% -> 0%
where the time goes in v6:
time: 134 us
  waiting for transfers between devices  78.5 us (59%)
  starting transfers between devices  24.5 us (18%)
  local copies, waits for them, and re-layouts  15.3 us (11%)
  Pallas kernels  6.94 us (5%)
  other arithmetic  5.95 us (4%)
  matrix products  1.52 us (1%)
    all_to_all x1, waiting for transfers between devices, shards(): lax.all_to_all(jnp.concatenate([strided_out, terms], axis=1), 'ctx', 0, 0...  39.9 us
    all_to_all x1, waiting for transfers between devices, shards(): lax.all_to_all(jnp.concatenate([strided_rows, summary_rows], axis=1), 'ct...  38.6 us
    all_to_all x1, starting transfers between devices, shards(): lax.all_to_all(jnp.concatenate([strided_rows, summary_rows], axis=1), 'ct...  16.6 us
    all_to_all x1, starting transfers between devices, shards(): lax.all_to_all(jnp.concatenate([strided_out, terms], axis=1), 'ctx', 0, 0...  7.86 us
    pallas_call x1, Pallas kernels, fixed_heads(): pl.pallas_call(functools.partial(fixed_kernel, scaling=scaling), out_shap...  6.94 us
    unnamed x28, local copies, waits for them, and re-layouts  5.08 us
  transfers between devices with their start and end apart: 2, of which 2 were waited for; matrix products, arithmetic and copies ran while one was open for 1% of the time, Pallas kernels for 0%

profile of v6, /device:TPU:1, one launch (start us, length us, event | category | flops | bytes accessed | tf_op | source)
XLA Modules:
  0.0 133.9 jit_solution(8990892087413720414)
XLA Ops:
  0.7 1.1 reshape.278
  1.7 1.0 reshape.280
  2.7 0.2 slice_bitcast_fusion.6
  3.1 0.2 slice_bitcast_fusion.5
  3.4 0.4 slice_bitcast_fusion.4
  3.8 1.0 maximum_bitcast_fusion.1
  4.9 0.3 copy.97
  5.2 0.1 broadcast_in_dim.26
  5.4 1.3 pad_maximum_fusion
  6.7 16.6 %all-to-all-start = ((bf16[128,48,128]{2,1,0:T(8,128)(2,1)}), bf16[128,48,128]{2,1,0:T(8,128)(2,1)S(1)}, u32[]{:S(2)}, u32[]{:S(2)}) async-start(bf16[128,48,128]{2,1,0:T(8,128)(2,1)} %pad_maximum_fusion), calls=%async_computation | async-start | bytes 3145728 | tf_op jit(solution)/shard_map/all_to_all | solution.py:192
  23.3 0.7 copy.175
  24.0 0.7 copy.176
  24.7 38.6 %all-to-all-done = bf16[128,48,128]{2,1,0:T(8,128)(2,1)S(1)} async-done(((bf16[128,48,128]{2,1,0:T(8,128)(2,1)}), bf16[128,48,128]{2,1,0:T(8,128)(2,1)S(1)}, u32[]{:S(2)}, u32[]{:S(2)}) %all-to-all-start) | async-done | bytes 1572896 | tf_op jit(solution)/shard_map/all_to_all | solution.py:192
  63.3 0.1 copy.146
  63.6 0.2 copy.109
  63.9 0.1 copy.108
  64.1 0.1 copy.104
  64.2 0.1 copy.103
  64.3 0.1 copy.102
  64.5 0.3 fusion.26
  64.8 0.2 fusion.9
  65.1 0.2 multiply_reduce_fusion
  65.3 0.2 fusion.5
  65.6 0.2 fusion.10
  65.8 0.2 fusion.11
  66.1 0.4 copy.145
  66.7 1.2 copy.169
  68.3 0.5 maximum_bitcast_fusion.2
  68.9 0.3 copy.124
  69.2 1.2 copy.170
  70.4 6.9 %shard_map.75 = (bf16[2,2,128,128]{3,2,1,0:T(8,128)(2,1)}, bf16[2,2,128,128]{3,2,1,0:T(8,128)(2,1)}, f32[2,2,128,128]{3,2,1,0:T(8,128)}, f32[2,2,128,128]{3,2,1,...) custom-call(s32[1]{0:T(128)} %bitcast.start_ref, bf16[2,2,128,128]{3,2,1,0:T(8,128)(2,1)} %bitcast.182, ...), custom_call_target="tpu_custom_call" | custom-call | tf_op jit(solution)/shard_map/pallas_call | solution.py:113
  77.3 1.4 %convert_bitcast_fusion.1 = bf16[1,2,1024,128]{3,2,1,0:T(8,128)(2,1)S(1)} fusion(f32[2,1024,128]{2,1,0:T(8,128)} %get-tuple-element.11), kind=kLoop, calls=%fused_computation.27 | loop fusion | flops 262144 | bytes 1572864 | tf_op jit(solution)/shard_map/stack | solution.py:135
  78.7 0.2 copy-done
  79.1 1.1 copy.122
  80.2 0.2 copy.123
  80.3 1.3 pad_maximum_fusion.1
  81.6 7.9 %all-to-all-start.1 = ((bf16[128,48,128]{2,1,0:T(8,128)(2,1)}), bf16[128,48,128]{2,1,0:T(8,128)(2,1)S(1)}, u32[]{:S(2)}, u32[]{:S(2)}) async-start(bf16[128,48,128]{2,1,0:T(8,128)(2,1)} %pad_maximum_fusion.1), calls=%async_computation.1 | async-start | bytes 3145728 | tf_op jit(solution)/shard_map/all_to_all | solution.py:224
  89.6 39.9 %all-to-all-done.1 = bf16[128,48,128]{2,1,0:T(8,128)(2,1)S(1)} async-done(((bf16[128,48,128]{2,1,0:T(8,128)(2,1)}), bf16[128,48,128]{2,1,0:T(8,128)(2,1)S(1)}, u32[]{:S(2)}, u32[]{:S(2)}) %all-to-all-start.1) | async-done | bytes 1572896 | tf_op jit(solution)/shard_map/all_to_all | solution.py:224
  129.5 0.1 copy.125
  129.7 0.2 convert_reduce_fusion
  130.0 0.2 copy.131
  130.2 0.7 copy.171
  131.0 0.2 copy.129
  131.2 0.7 copy.172
  132.0 0.2 copy.127
  132.2 0.7 copy.173
  133.0 0.2 copy.126
  133.2 0.7 copy.174
  (49 shorter events, 1.8 us)
Async XLA Ops:
  0.6 2.3 %copy-start.3 = (bf16[256,512]{1,0:T(8,128)(2,1)S(1)}, bf16[256,512]{1,0:T(8,128)(2,1)}, u32[]{:S(2)}) copy-start(bf16[256,512]{1,0:T(8,128)(2,1)} %param.6) | copy-start | bytes 786436
  0.6 2.7 %copy-start.4 = (bf16[256,512]{1,0:T(8,128)(2,1)S(1)}, bf16[256,512]{1,0:T(8,128)(2,1)}, u32[]{:S(2)}) copy-start(bf16[256,512]{1,0:T(8,128)(2,1)} %param.7) | copy-start | bytes 786436
  3.0 1.8 %copy-start.1 = (bf16[2,128,1,2,128]{4,1,3,0,2:T(8,128)(2,1)}, bf16[2,128,1,2,128]{4,1,3,0,2:T(8,128)(2,1)S(1)}, u32[]{:S(2)}) copy-start(bf16[2,128,1,2,128]{4,1,3,0,2:T(8,128)(2,1)S(1)} %copy.178) | copy-start | bytes 393220
  3.3 1.6 %copy-start.2 = (bf16[2,128,1,2,128]{4,1,3,0,2:T(8,128)(2,1)}, bf16[2,128,1,2,128]{4,1,3,0,2:T(8,128)(2,1)S(1)}, u32[]{:S(2)}) copy-start(bf16[2,128,1,2,128]{4,1,3,0,2:T(8,128)(2,1)S(1)} %copy.177) | copy-start | bytes 393220
  6.7 56.6 %all-to-all-start = ((bf16[128,48,128]{2,1,0:T(8,128)(2,1)}), bf16[128,48,128]{2,1,0:T(8,128)(2,1)S(1)}, u32[]{:S(2)}, u32[]{:S(2)}) async-start(bf16[128,48,128]{2,1,0:T(8,128)(2,1)} %pad_maximum_fusion), calls=%async_computation | async-start | bytes 3145728 | tf_op jit(solution)/shard_map/all_to_all | solution.py:192
  77.3 1.5 %copy-start = (f32[2,1024,128]{2,1,0:T(8,128)S(1)}, f32[2,1024,128]{2,1,0:T(8,128)}, u32[]{:S(2)}) copy-start(f32[2,1024,128]{2,1,0:T(8,128)} %get-tuple-element.12) | copy-start | bytes 3145732
  81.6 7.9 %copy-start.7 = (f32[2,2,128,128]{3,2,1,0:T(8,128)S(1)}, f32[2,2,128,128]{3,2,1,0:T(8,128)}, u32[]{:S(2)}) copy-start(f32[2,2,128,128]{3,2,1,0:T(8,128)} %get-tuple-element.14) | copy-start | bytes 786436
  81.6 7.9 %copy-start.8 = (f32[2,2,128,128]{3,2,1,0:T(8,128)S(1)}, f32[2,2,128,128]{3,2,1,0:T(8,128)}, u32[]{:S(2)}) copy-start(f32[2,2,128,128]{3,2,1,0:T(8,128)} %get-tuple-element.15) | copy-start | bytes 786436
  81.6 47.9 %all-to-all-start.1 = ((bf16[128,48,128]{2,1,0:T(8,128)(2,1)}), bf16[128,48,128]{2,1,0:T(8,128)(2,1)S(1)}, u32[]{:S(2)}, u32[]{:S(2)}) async-start(bf16[128,48,128]{2,1,0:T(8,128)(2,1)} %pad_maximum_fusion.1), calls=%async_computation.1 | async-start | bytes 3145728 | tf_op jit(solution)/shard_map/all_to_all | solution.py:224
  129.9 2.0 %copy-start.6 = (bf16[2,2,128,128]{3,2,1,0:T(8,128)(2,1)S(1)}, bf16[2,2,128,128]{3,2,1,0:T(8,128)(2,1)}, u32[]{:S(2)}) copy-start(bf16[2,2,128,128]{3,2,1,0:T(8,128)(2,1)} %get-tuple-element.13) | copy-start | bytes 393220
  130.9 2.0 %copy-start.5 = (bf16[2,2,128,128]{3,2,1,0:T(8,128)(2,1)S(1)}, bf16[2,2,128,128]{3,2,1,0:T(8,128)(2,1)}, u32[]{:S(2)}) copy-start(bf16[2,2,128,128]{3,2,1,0:T(8,128)(2,1)} %get-tuple-element.10) | copy-start | bytes 393220

commit v7 on v5

--- a/solution.py
+++ b/solution.py
@@ -3,11 +3,12 @@
 import jax
 import jax.numpy as jnp
 from jax import lax
-from jax.sharding import PartitionSpec as P
+from jax.sharding import Mesh, PartitionSpec as P
 
 HD = 128
 STRIDE = 128
 SUMMARY = 4
+CTX = ("ctx_chip", "ctx_core")
 
 
 def split_heads(matrix):
@@ -31,10 +32,10 @@
     return paired.reshape(blocks * positions, 2 * half_heads * head_dim)
 
 
-def fixed_heads(query, key_rows, value_rows, grad_rows, flat_keys, flat_values, scaling):
+def fixed_heads(query, key_rows, value_rows, grad_rows, flat_keys, flat_values, scaling, here):
     blocks_here, positions, half_heads, head_dim = query.shape
     summary_count = flat_keys.shape[0]
-    block_ids = lax.axis_index("ctx") * blocks_here + jnp.arange(blocks_here, dtype=jnp.int32)
+    block_ids = here * blocks_here + jnp.arange(blocks_here, dtype=jnp.int32)
     summary_block = jnp.arange(summary_count, dtype=jnp.int32) // SUMMARY
     earlier = (summary_block[None, :] < block_ids[:, None])[:, None, None, :]
     causal = (jnp.arange(positions)[:, None] >= jnp.arange(positions)[None, :])[None, None]
@@ -137,19 +138,22 @@
     value_fixed, value_strided = split_heads(values)
     grad_fixed, grad_strided = split_heads(out_grad)
     blocks_here, positions, half_heads, head_dim = query_fixed.shape
-    peers = lax.axis_size("ctx")
+    peers = lax.axis_size("ctx_chip") * 2
     residues = positions // peers
+    core = lax.axis_index("ctx_core")
+    swap = [(0, 1), (1, 0)]
 
     strided_rows = jnp.stack([query_strided, key_strided, value_strided, grad_strided])
     strided_rows = strided_rows.reshape(4, blocks_here, peers, residues, half_heads, head_dim)
     strided_rows = strided_rows.transpose(2, 0, 1, 3, 4, 5).reshape(peers, -1, head_dim)
     summary_rows = jnp.stack(
         [key_fixed[:, positions - SUMMARY :], value_fixed[:, positions - SUMMARY :]]
-    ).reshape(1, -1, head_dim)
-    summary_rows = jnp.broadcast_to(summary_rows, (peers,) + summary_rows.shape[1:])
+    ).reshape(1, 2, -1, head_dim)
+    summary_rows = jnp.broadcast_to(summary_rows, (peers // 2,) + summary_rows.shape[1:])
+    summary_rows = summary_rows.reshape(peers, -1, head_dim)
     strided_size = strided_rows.shape[1]
     received = lax.all_to_all(
-        jnp.concatenate([strided_rows, summary_rows], axis=1), "ctx", 0, 0, tiled=True
+        jnp.concatenate([strided_rows, summary_rows], axis=1), CTX, 0, 0, tiled=True
     )
     gathered = received[:, :strided_size].reshape(
         peers, 4, blocks_here, residues, half_heads, head_dim
@@ -157,30 +161,32 @@
     gathered = gathered.transpose(1, 0, 2, 3, 4, 5).reshape(
         4, peers * blocks_here, residues, half_heads, head_dim
     )
-    summaries = received[:, strided_size:].reshape(
-        peers, 2, blocks_here * SUMMARY, half_heads, head_dim
-    )
-    summaries = summaries.transpose(1, 0, 2, 3, 4).reshape(
-        2, peers * blocks_here * SUMMARY, half_heads, head_dim
-    )
+    mine = received[:, strided_size:]
+    sibling = lax.ppermute(mine, "ctx_core", swap)
+    summary_shape = (peers * blocks_here * SUMMARY, half_heads, head_dim)
+    summary_keys = jnp.where(core == 0, mine, sibling).reshape(summary_shape)
+    summary_values = jnp.where(core == 0, sibling, mine).reshape(summary_shape)
 
     attended, query_grad, key_grad, value_grad, terms = fixed_heads(
         query_fixed,
         key_fixed,
         value_fixed,
         grad_fixed,
-        summaries[0],
-        summaries[1],
+        summary_keys,
+        summary_values,
         scaling,
+        lax.axis_index("ctx_chip") * 2 + core,
     )
     strided_out = strided_heads(gathered[0], gathered[1], gathered[2], gathered[3], scaling)
 
     strided_out = strided_out.reshape(4, peers, -1, head_dim).transpose(1, 0, 2, 3)
     strided_out = strided_out.reshape(peers, -1, head_dim)
-    terms = terms.astype(jnp.bfloat16).reshape(2, peers, -1, head_dim).transpose(1, 0, 2, 3)
-    terms = terms.reshape(peers, -1, head_dim)
+    terms = terms.reshape(2, peers, -1, head_dim)
+    keep = jnp.where(core == 0, terms[0], terms[1])
+    give = jnp.where(core == 0, terms[1], terms[0])
+    terms = (keep + lax.ppermute(give, "ctx_core", swap)).astype(jnp.bfloat16)
     returned = lax.all_to_all(
-        jnp.concatenate([strided_out, terms], axis=1), "ctx", 0, 0, tiled=True
+        jnp.concatenate([strided_out, terms], axis=1), CTX, 0, 0, tiled=True
     )
     strided_out = returned[:, :strided_size].reshape(
         peers, 4, blocks_here, residues, half_heads, head_dim
@@ -188,7 +194,8 @@
     strided_out = strided_out.transpose(1, 2, 0, 3, 4, 5).reshape(
         4, blocks_here, positions, half_heads, head_dim
     )
-    shares = jnp.sum(returned[:, strided_size:].astype(jnp.float32), axis=0)
+    shares = returned[:, strided_size:].astype(jnp.float32)
+    shares = jnp.sum(shares.reshape(peers // 2, 2, -1, head_dim), axis=0)
     shares = shares.reshape(2, blocks_here, SUMMARY, half_heads, head_dim)
     key_grad = jnp.concatenate(
         [key_grad[:, : positions - SUMMARY], key_grad[:, positions - SUMMARY :] + shares[0]], axis=1
@@ -206,10 +213,13 @@
 
 
 def solution(mesh):
+    peers, heads = mesh.devices.shape
+    split = Mesh(mesh.devices.reshape(peers // 2, 2, heads), CTX + ("head",))
+    spec = P(CTX, "head")
     return jax.shard_map(
         shards,
-        mesh=mesh,
-        in_specs=(P("ctx", "head"), P("ctx", "head"), P("ctx", "head"), P("ctx", "head")),
-        out_specs=(P("ctx", "head"), P("ctx", "head"), P("ctx", "head"), P("ctx", "head")),
+        mesh=split,
+        in_specs=(spec, spec, spec, spec),
+        out_specs=(spec, spec, spec, spec),
         check_vma=False,
     )

time: 133 us -> 123 us (0.925)
  waiting for transfers between devices: 75.3 us -> 55.7 us
  local copies, waits for them, and re-layouts: 13 us -> 18.8 us
  starting transfers between devices: 24.4 us -> 28.6 us
    all_to_all x2, waiting for transfers between devices: 75.3 us -> 54.5 us  [the longest x1 28.2 us: shards(): lax.all_to_all(jnp.concatenate([strided_rows, summary_rows], axis=1), CTX...]
    ppermute x0 -> x2, starting transfers between devices: none -> 5.69 us  [the longest x1 3.23 us: shards(): sibling = lax.ppermute(mine, 'ctx_core', swap)]
    concatenate x0 -> x2, local copies, waits for them, and re-layouts: none -> 3.3 us  [the longest x1 1.65 us: shards(): jnp.concatenate([strided_out, terms], axis=1)]
    select_n x0 -> x3, local copies, waits for them, and re-layouts: none -> 2.92 us  [the longest x2 2.1 us: shards(): give = jnp.where(core == 0, terms[1], terms[0])]
    convert_element_type x1, other arithmetic: 0.08 us -> 1.7 us  [shards(): terms = (keep + lax.ppermute(give, 'ctx_core', swap)).astype(jnp.bfloat16)]
    all_to_all x2, starting transfers between devices: 24.4 us -> 22.9 us  [the longest x1 16.6 us: shards(): lax.all_to_all(jnp.concatenate([strided_rows, summary_rows], axis=1), CTX...]
    unnamed x29 -> x35, local copies, waits for them, and re-layouts: 4.38 us -> 3.31 us
  transfers between devices with their start and end apart: 2 -> 4, of which waited for: 2 -> 3; matrix products, arithmetic and copies ran while one was open for 3% -> 11% of each run, Pallas kernels for 0% -> 0%
where the time goes in v7:
time: 123 us
  waiting for transfers between devices  55.7 us (45%)
  starting transfers between devices  28.6 us (23%)
  local copies, waits for them, and re-layouts  18.8 us (15%)
  matrix products  12.8 us (10%)
  other arithmetic  5.55 us (5%)
  between operations  1.36 us (1%)
    all_to_all x1, waiting for transfers between devices, shards(): lax.all_to_all(jnp.concatenate([strided_rows, summary_rows], axis=1), CTX...  28.2 us
    all_to_all x1, waiting for transfers between devices, shards(): lax.all_to_all(jnp.concatenate([strided_out, terms], axis=1), CTX, 0, 0,...  26.3 us
    all_to_all x1, starting transfers between devices, shards(): lax.all_to_all(jnp.concatenate([strided_rows, summary_rows], axis=1), CTX...  16.6 us
    all_to_all x1, starting transfers between devices, shards(): lax.all_to_all(jnp.concatenate([strided_out, terms], axis=1), CTX, 0, 0,...  6.29 us
    unnamed x35, local copies, waits for them, and re-layouts  3.31 us
    ppermute x1, starting transfers between devices, shards(): sibling = lax.ppermute(mine, 'ctx_core', swap)  3.23 us
  transfers between devices with their start and end apart: 4, of which 3 were waited for; matrix products, arithmetic and copies ran while one was open for 11% of the time, Pallas kernels for 0%

profile of v7, /device:TPU:1, one launch (start us, length us, event | category | flops | bytes accessed | tf_op | source)
XLA Modules:
  0.0 122.8 jit_solution(10538829548196505481)
XLA Ops:
  0.7 1.1 reshape.353
  1.7 1.0 reshape.355
  2.7 0.4 slice_bitcast_fusion.6
  3.3 0.4 slice_bitcast_fusion.5
  3.7 1.0 maximum_bitcast_fusion
  5.2 0.3 broadcast_in_dim.63
  5.5 1.7 %copy.218 = bf16[128,32,128]{2,1,0:T(8,128)(2,1)} copy(bf16[128,32,128]{2,0,1:T(8,128)(2,1)S(1)} %pad_maximum_fusion) | data formatting | bytes 2097152 | tf_op jit(solution)/shard_map/concatenate | solution.py:156
  7.2 16.6 %all-to-all-start = ((bf16[128,32,128]{2,1,0:T(8,128)(2,1)}), bf16[128,32,128]{2,1,0:T(8,128)(2,1)S(1)}, u32[]{:S(2)}, u32[]{:S(2)}) async-start(bf16[128,32,128]{2,1,0:T(8,128)(2,1)} %copy.218), calls=%async_computation | async-start | bytes 2097152 | tf_op jit(solution)/shard_map/all_to_all | solution.py:155
  24.2 0.6 iota_compare_fusion
  24.8 28.2 %all-to-all-done = bf16[128,32,128]{2,1,0:T(8,128)(2,1)S(1)} async-done(((bf16[128,32,128]{2,1,0:T(8,128)(2,1)}), bf16[128,32,128]{2,1,0:T(8,128)(2,1)S(1)}, u32[]{:S(2)}, u32[]{:S(2)}) %all-to-all-start) | async-done | bytes 1048608 | tf_op jit(solution)/shard_map/all_to_all | solution.py:155
  53.0 3.2 %collective-permute-start = (bf16[128,16,128]{2,1,0:T(8,128)(2,1)S(1)}, bf16[128,16,128]{2,1,0:T(8,128)(2,1)S(1)}, u32[]{:S(2)}, u32[]{:S(2)}) collective-permute-start(bf16[128,16,128]{2,1,0:T(8,128)(2,1)S(1)} %slice.139), channel_id=1, source_target_pairs={{0,4},{4,0},{1,5},{5,1},{2,6},{6,2},{3,7},{7,3},{8,12},{12,8},{9,1... | collective-permute-start | bytes 1572872 | tf_op jit(solution)/shard_map/ppermute | solution.py:165
  56.6 1.2 collective-permute-done
  57.9 0.3 copy.362
  58.2 1.1 fusion.66
  59.3 0.4 copy.226
  59.7 0.5 fusion.70
  60.2 0.3 fusion.4
  60.5 0.3 fusion.30
  60.9 0.3 convolution_bitcast_fusion.6
  61.3 0.9 multiply_reduce_fusion
  62.1 0.4 convolution_bitcast_fusion
  62.6 0.6 fusion.2
  63.2 0.4 select_bitcast_fusion.1
  63.6 0.8 copy.251
  64.5 1.3 %copy.252 = f32[128,16,128]{2,0,1:T(8,128)} copy(f32[128,16,128]{2,1,0:T(8,128)S(1)} %bitcast.226) | data formatting | bytes 2097152 | tf_op jit(solution)/shard_map/jit(_where)/select_n | solution.py:186
  65.8 2.5 %collective-permute-start.1 = (f32[128,16,128]{2,0,1:T(8,128)}, f32[128,16,128]{2,0,1:T(8,128)}, u32[]{:S(2)}, u32[]{:S(2)}) collective-permute-start(f32[128,16,128]{2,0,1:T(8,128)} %copy.252), channel_id=1, source_target_pairs={{0,4},{4,0},{1,5},{5,1},{2,6},{6,2},{3,7},{7,3},{8,12},{12,8},{9,1... | collective-permute-start | bytes 3145736 | tf_op jit(solution)/shard_map/ppermute | solution.py:187
  68.3 1.1 fusion.71
  69.5 1.3 %fusion.23 = bf16[256,1,2,128]{0,3,2,1:T(8,128)(2,1)S(1)} fusion(bf16[256,2,128]{2,0,1:T(8,128)(2,1)S(1)} %bitcast.244, f32[2,256,256]{1,2,0:T(8,128)} %get-tuple-element.36, f32[2,256]{1,0:T(2,128)S(1)} %get-tuple-element.35), kind=kOutput, calls=%fused_computation.42 | convolution fusion | flops 33882112 | bytes 788480 | tf_op jit(solution)/shard_map/rgbc,brgd->crgd/dot_general | solution.py:128
  70.9 2.0 %multiply_reduce_fusion.1 = (f32[256,2]{0,1:T(2,128)S(1)}, bf16[256,1,2,128]{0,3,2,1:T(8,128)(2,1)}) fusion(f32[256,1,2,128]{0,3,2,1:T(8,128)S(1)} %copy.232, bf16[256,2,128]{2,0,1:T(8,128)(2,1)} %bitcast.260, f32[2,256,256]{1,2,0:T(8,128)} %get-tuple-element.36, f32[2,256]{1,0:T(2,128)S(1)} %get-tuple-element.35), kind=kOutput, calls=%fused_computation.80 | convolution fusion | flops 34078208 | bytes 1052672 | tf_op jit(solution)/shard_map/rgbc,crgd->brgd/dot_general | solution.py:111
  73.0 1.3 %fusion.10 = bf16[2,256,256]{1,2,0:T(8,128)(2,1)S(1)} fusion(bf16[256,2,128]{2,0,1:T(8,128)(2,1)S(1)} %bitcast.245, bf16[256,2,128]{2,0,1:T(8,128)(2,1)} %bitcast.261, f32[2,256]{1,0:T(2,128)S(1)} %bitcast.268, f32[2,256,256]{1,2,0:T(8,128)} %get-tuple-element.36, f32[2,256]{1,0:T(2,128)S(1)} %get-tuple-element.35), kind=kOutput, calls=%fused_computation.17 | convolution fusion | flops 34078720 | bytes 1052672 | tf_op jit(solution)/shard_map/brgd,crgd->rgbc/dot_general | solution.py:114
  74.7 1.1 fusion.24
  75.9 1.0 copy.231
  77.0 0.5 maximum_bitcast_fusion.1
  77.6 0.8 copy.250
  78.4 1.7 %fusion.29 = bf16[128,16,128]{2,0,1:T(8,128)(2,1)S(1)} fusion(f32[128,16,128]{2,0,1:T(8,128)} %collective-permute-done.1, f32[128,16,128]{2,1,0:T(8,128)S(1)} %bitcast.225), kind=kLoop, calls=%fused_computation.52 | loop fusion | flops 524288 | bytes 2621440 | tf_op jit(solution)/shard_map/convert_element_type | solution.py:187
  80.2 1.7 %copy.254 = bf16[128,32,128]{2,1,0:T(8,128)(2,1)} copy(bf16[128,32,128]{2,0,1:T(8,128)(2,1)S(1)} %pad_maximum_fusion.1) | data formatting | bytes 2097152 | tf_op jit(solution)/shard_map/concatenate | solution.py:189
  81.8 6.3 %all-to-all-start.1 = ((bf16[128,32,128]{2,1,0:T(8,128)(2,1)}), bf16[128,32,128]{2,1,0:T(8,128)(2,1)S(1)}, u32[]{:S(2)}, u32[]{:S(2)}) async-start(bf16[128,32,128]{2,1,0:T(8,128)(2,1)} %copy.254), calls=%async_computation.1 | async-start | bytes 2097152 | tf_op jit(solution)/shard_map/all_to_all | solution.py:188
  88.1 0.4 copy.262
  88.6 1.3 %fusion.21 = bf16[2,2,128,128]{2,3,1,0:T(8,128)(2,1)S(1)} fusion(bf16[2,128,1,2,128]{1,4,3,0,2:T(8,128)(2,1)} %copy-done.10, f32[2,2,128]{2,1,0:T(2,128)S(1)} %bitcast.267, f32[2,2,128]{2,1,0:T(2,128)S(1)} %copy_add_fusion.1, f32[2,2,128,128]{2,3,1,0:T(8,128)} %copy-done.8, f32[2,2,128]{2,1,0:T(2,128)S(1)} %copy_maximum_fusion, ...), kind=kOutput, calls=%fused_computation.38 | convolution fusion | flops 17104896 | bytes 661504 | tf_op jit(solution)/shard_map/bqgd,bkgd->bgqk/dot_general | solution.py:66
  89.9 0.3 convolution_bitcast_fusion.5
  90.2 0.2 fusion.26
  90.7 0.2 fusion.11
  91.0 26.3 %all-to-all-done.1 = bf16[128,32,128]{2,1,0:T(8,128)(2,1)S(1)} async-done(((bf16[128,32,128]{2,1,0:T(8,128)(2,1)}), bf16[128,32,128]{2,1,0:T(8,128)(2,1)S(1)}, u32[]{:S(2)}, u32[]{:S(2)}) %all-to-all-start.1) | async-done | bytes 1048608 | tf_op jit(solution)/shard_map/all_to_all | solution.py:188
  118.2 0.5 copy.255
  119.0 0.7 copy.363
  120.1 0.7 copy.364
  121.1 0.7 copy.365
  122.0 0.7 copy.366
  (82 shorter events, 4.7 us)
Async XLA Ops:
  0.6 2.6 %copy-start.6 = (bf16[256,512]{1,0:T(8,128)(2,1)S(1)}, bf16[256,512]{1,0:T(8,128)(2,1)}, u32[]{:S(2)}) copy-start(bf16[256,512]{1,0:T(8,128)(2,1)} %param.6) | copy-start | bytes 786436
  0.6 2.6 %copy-start.7 = (bf16[256,512]{1,0:T(8,128)(2,1)S(1)}, bf16[256,512]{1,0:T(8,128)(2,1)}, u32[]{:S(2)}) copy-start(bf16[256,512]{1,0:T(8,128)(2,1)} %param.7) | copy-start | bytes 786436
  4.9 56.3 %copy-start = (bf16[2,128,1,2,128]{1,4,3,0,2:T(8,128)(2,1)}, bf16[2,128,1,2,128]{1,4,3,0,2:T(8,128)(2,1)S(1)}, u32[]{:S(2)}) copy-start(bf16[2,128,1,2,128]{1,4,3,0,2:T(8,128)(2,1)S(1)} %copy.308) | copy-start | bytes 393220
  7.2 45.8 %all-to-all-start = ((bf16[128,32,128]{2,1,0:T(8,128)(2,1)}), bf16[128,32,128]{2,1,0:T(8,128)(2,1)S(1)}, u32[]{:S(2)}, u32[]{:S(2)}) async-start(bf16[128,32,128]{2,1,0:T(8,128)(2,1)} %copy.218), calls=%async_computation | async-start | bytes 2097152 | tf_op jit(solution)/shard_map/all_to_all | solution.py:155
  24.0 37.3 %copy-start.10 = (bf16[2,128,1,2,128]{1,4,3,0,2:T(8,128)(2,1)}, bf16[2,128,1,2,128]{1,4,3,0,2:T(8,128)(2,1)S(1)}, u32[]{:S(2)}) copy-start(bf16[2,128,1,2,128]{1,4,3,0,2:T(8,128)(2,1)S(1)} %copy.311) | copy-start | bytes 393220
  53.0 4.8 %collective-permute-start = (bf16[128,16,128]{2,1,0:T(8,128)(2,1)S(1)}, bf16[128,16,128]{2,1,0:T(8,128)(2,1)S(1)}, u32[]{:S(2)}, u32[]{:S(2)}) collective-permute-start(bf16[128,16,128]{2,1,0:T(8,128)(2,1)S(1)} %slice.139), channel_id=1, source_target_pairs={{0,4},{4,0},{1,5},{5,1},{2,6},{6,2},{3,7},{7,3},{8,12},{12,8},{9,1... | collective-permute-start | bytes 1572872 | tf_op jit(solution)/shard_map/ppermute | solution.py:165
  56.6 4.7 %copy-start.8 = (f32[2,2,128,128]{2,3,1,0:T(8,128)}, f32[2,2,128,128]{2,3,1,0:T(8,128)S(1)}, u32[]{:S(2)}) copy-start(f32[2,2,128,128]{2,3,1,0:T(8,128)S(1)} %get-tuple-element.30) | copy-start | bytes 786436
  59.2 9.0 %copy-start.3 = (bf16[1,128,2,1,2,128]{5,2,1,4,3,0:T(2,128)(2,1)}, bf16[1,128,2,1,2,128]{5,2,1,4,3,0:T(2,128)(2,1)S(1)}, u32[]{:S(2)}) copy-start(bf16[1,128,2,1,2,128]{5,2,1,4,3,0:T(2,128)(2,1)S(1)} %get-tuple-element.18) | copy-start | bytes 393220
  59.2 9.0 %copy-start.4 = (bf16[1,128,2,1,2,128]{5,2,1,4,3,0:T(2,128)(2,1)}, bf16[1,128,2,1,2,128]{5,2,1,4,3,0:T(2,128)(2,1)S(1)}, u32[]{:S(2)}) copy-start(bf16[1,128,2,1,2,128]{5,2,1,4,3,0:T(2,128)(2,1)S(1)} %get-tuple-element.17) | copy-start | bytes 393220
  63.6 4.6 %copy-start.13 = (pred[256,256]{0,1:T(8,128)(4,1)S(1)}, pred[256,256]{0,1:T(8,128)(4,1)}, u32[]{:S(2)}) copy-start(pred[256,256]{0,1:T(8,128)(4,1)} %iota_compare_fusion) | copy-start | bytes 196612
  64.5 4.9 %copy-start.2 = (bf16[1,128,2,1,2,128]{5,2,1,4,3,0:T(2,128)(2,1)S(1)}, bf16[1,128,2,1,2,128]{5,2,1,4,3,0:T(2,128)(2,1)}, u32[]{:S(2)}) copy-start(bf16[1,128,2,1,2,128]{5,2,1,4,3,0:T(2,128)(2,1)} %get-tuple-element.16) | copy-start | bytes 393220
  65.8 12.6 %collective-permute-start.1 = (f32[128,16,128]{2,0,1:T(8,128)}, f32[128,16,128]{2,0,1:T(8,128)}, u32[]{:S(2)}, u32[]{:S(2)}) collective-permute-start(f32[128,16,128]{2,0,1:T(8,128)} %copy.252), channel_id=1, source_target_pairs={{0,4},{4,0},{1,5},{5,1},{2,6},{6,2},{3,7},{7,3},{8,12},{12,8},{9,1... | collective-permute-start | bytes 3145736 | tf_op jit(solution)/shard_map/ppermute | solution.py:187
  70.9 3.4 %copy-start.5 = (bf16[1,128,2,1,2,128]{5,2,1,4,3,0:T(2,128)(2,1)S(1)}, bf16[1,128,2,1,2,128]{5,2,1,4,3,0:T(2,128)(2,1)}, u32[]{:S(2)}) copy-start(bf16[1,128,2,1,2,128]{5,2,1,4,3,0:T(2,128)(2,1)} %copy-done.4) | copy-start | bytes 393220
  81.8 6.7 %copy-start.1 = (bf16[2,128,1,2,128]{1,4,3,0,2:T(8,128)(2,1)S(1)}, bf16[2,128,1,2,128]{1,4,3,0,2:T(8,128)(2,1)}, u32[]{:S(2)}) copy-start(bf16[2,128,1,2,128]{1,4,3,0,2:T(8,128)(2,1)} %copy-done) | copy-start | bytes 393220
  81.8 35.5 %all-to-all-start.1 = ((bf16[128,32,128]{2,1,0:T(8,128)(2,1)}), bf16[128,32,128]{2,1,0:T(8,128)(2,1)S(1)}, u32[]{:S(2)}, u32[]{:S(2)}) async-start(bf16[128,32,128]{2,1,0:T(8,128)(2,1)} %copy.254), calls=%async_computation.1 | async-start | bytes 2097152 | tf_op jit(solution)/shard_map/all_to_all | solution.py:188
  88.6 1.9 %copy-start.9 = (f32[2,2,128,128]{2,3,1,0:T(8,128)S(1)}, f32[2,2,128,128]{2,3,1,0:T(8,128)}, u32[]{:S(2)}) copy-start(f32[2,2,128,128]{2,3,1,0:T(8,128)} %copy-done.8) | copy-start | bytes 786436
  88.6 1.9 %copy-start.11 = (bf16[2,128,1,2,128]{1,4,3,0,2:T(8,128)(2,1)S(1)}, bf16[2,128,1,2,128]{1,4,3,0,2:T(8,128)(2,1)}, u32[]{:S(2)}) copy-start(bf16[2,128,1,2,128]{1,4,3,0,2:T(8,128)(2,1)} %copy-done.10) | copy-start | bytes 393220
  118.8 3.0 %copy-start.12 = (bf16[2,128,2,128]{1,3,2,0:T(8,128)(2,1)S(1)}, bf16[2,128,2,128]{1,3,2,0:T(8,128)(2,1)}, u32[]{:S(2)}) copy-start(bf16[2,128,2,128]{1,3,2,0:T(8,128)(2,1)} %get-tuple-element.34) | copy-start | bytes 393220

commit v8 on v7

--- a/solution.py
+++ b/solution.py
@@ -164,8 +164,9 @@
     mine = received[:, strided_size:]
     sibling = lax.ppermute(mine, "ctx_core", swap)
     summary_shape = (peers * blocks_here * SUMMARY, half_heads, head_dim)
-    summary_keys = jnp.where(core == 0, mine, sibling).reshape(summary_shape)
-    summary_values = jnp.where(core == 0, sibling, mine).reshape(summary_shape)
+    both = lax.dynamic_slice_in_dim(jnp.stack([mine, sibling, mine]), core, 2, axis=0)
+    summary_keys = both[0].reshape(summary_shape)
+    summary_values = both[1].reshape(summary_shape)
 
     attended, query_grad, key_grad, value_grad, terms = fixed_heads(
         query_fixed,
@@ -182,8 +183,8 @@
     strided_out = strided_out.reshape(4, peers, -1, head_dim).transpose(1, 0, 2, 3)
     strided_out = strided_out.reshape(peers, -1, head_dim)
     terms = terms.reshape(2, peers, -1, head_dim)
-    keep = jnp.where(core == 0, terms[0], terms[1])
-    give = jnp.where(core == 0, terms[1], terms[0])
+    keep = lax.dynamic_index_in_dim(terms, core, 0, keepdims=False)
+    give = lax.dynamic_index_in_dim(terms, 1 - core, 0, keepdims=False)
     terms = (keep + lax.ppermute(give, "ctx_core", swap)).astype(jnp.bfloat16)
     returned = lax.all_to_all(
         jnp.concatenate([strided_out, terms], axis=1), CTX, 0, 0, tiled=True

time: 123 us -> 126 us (1.024)
  local copies, waits for them, and re-layouts: 18.8 us -> 20.8 us
    select_n x3 -> x0, local copies, waits for them, and re-layouts: 2.92 us -> none  [the longest x2 2.1 us: shards(): give = jnp.where(core == 0, terms[1], terms[0])]
    squeeze x0 -> x1, local copies, waits for them, and re-layouts: none -> 1.29 us  [shards(): give = lax.dynamic_index_in_dim(terms, 1 - core, 0, keepdims=False)]
    unnamed x35 -> x29, local copies, waits for them, and re-layouts: 3.31 us -> 3.3 us
  transfers between devices with their start and end apart: 4 -> 4, of which waited for: 3 -> 2; matrix products, arithmetic and copies ran while one was open for 11% -> 14% of each run, Pallas kernels for 0% -> 0%
where the time goes in v8:
time: 126 us
  waiting for transfers between devices  55.3 us (44%)
  starting transfers between devices  28.5 us (23%)
  local copies, waits for them, and re-layouts  20.8 us (17%)
  matrix products  13.4 us (11%)
  other arithmetic  6.59 us (5%)
  between operations  1.32 us (1%)
    all_to_all x1, waiting for transfers between devices, shards(): lax.all_to_all(jnp.concatenate([strided_rows, summary_rows], axis=1), CTX...  29 us
    all_to_all x1, waiting for transfers between devices, shards(): lax.all_to_all(jnp.concatenate([strided_out, terms], axis=1), CTX, 0, 0,...  26.3 us
    all_to_all x1, starting transfers between devices, shards(): lax.all_to_all(jnp.concatenate([strided_rows, summary_rows], axis=1), CTX...  16.6 us
    all_to_all x1, starting transfers between devices, shards(): lax.all_to_all(jnp.concatenate([strided_out, terms], axis=1), CTX, 0, 0,...  6.51 us
    ppermute x1, starting transfers between devices, shards(): sibling = lax.ppermute(mine, 'ctx_core', swap)  3.41 us
    unnamed x29, local copies, waits for them, and re-layouts  3.3 us
  transfers between devices with their start and end apart: 4, of which 2 were waited for; matrix products, arithmetic and copies ran while one was open for 14% of the time, Pallas kernels for 0%

profile of v8, /device:TPU:1, one launch (start us, length us, event | category | flops | bytes accessed | tf_op | source)
XLA Modules:
  0.0 125.9 jit_solution(7483513490883863589)
XLA Ops:
  0.7 1.1 reshape.341
  1.7 1.0 reshape.343
  2.7 0.4 slice_bitcast_fusion.6
  3.3 0.4 slice_bitcast_fusion.5
  3.7 1.0 maximum_bitcast_fusion
  5.2 0.3 broadcast_in_dim.63
  5.5 1.6 %copy.217 = bf16[128,32,128]{2,1,0:T(8,128)(2,1)} copy(bf16[128,32,128]{2,0,1:T(8,128)(2,1)S(1)} %pad_maximum_fusion) | data formatting | bytes 2097152 | tf_op jit(solution)/shard_map/concatenate | solution.py:156
  7.2 16.6 %all-to-all-start = ((bf16[128,32,128]{2,1,0:T(8,128)(2,1)}), bf16[128,32,128]{2,1,0:T(8,128)(2,1)S(1)}, u32[]{:S(2)}, u32[]{:S(2)}) async-start(bf16[128,32,128]{2,1,0:T(8,128)(2,1)} %copy.217), calls=%async_computation | async-start | bytes 2097152 | tf_op jit(solution)/shard_map/all_to_all | solution.py:155
  24.0 29.0 %all-to-all-done = bf16[128,32,128]{2,1,0:T(8,128)(2,1)S(1)} async-done(((bf16[128,32,128]{2,1,0:T(8,128)(2,1)}), bf16[128,32,128]{2,1,0:T(8,128)(2,1)S(1)}, u32[]{:S(2)}, u32[]{:S(2)}) %all-to-all-start) | async-done | bytes 1048608 | tf_op jit(solution)/shard_map/all_to_all | solution.py:155
  53.2 3.4 %collective-permute-start = (bf16[128,16,128]{2,1,0:T(8,128)(2,1)S(1)}, bf16[128,16,128]{2,1,0:T(8,128)(2,1)S(1)}, u32[]{:S(2)}, u32[]{:S(2)}) collective-permute-start(bf16[128,16,128]{2,1,0:T(8,128)(2,1)S(1)} %get-tuple-element.10), channel_id=1, source_target_pairs={{0,4},{4,0},{1,5},{5,1},{2,6},{6,2},{3,7},{7,3},{8,12},{12,8},{9,1... | collective-permute-start | bytes 1572872 | tf_op jit(solution)/shard_map/ppermute | solution.py:165
  57.2 0.3 copy.355
  57.5 1.1 fusion.75
  58.6 0.6 fusion.29
  59.3 0.4 copy.225
  59.8 0.5 fusion.79
  60.3 0.3 fusion.4
  60.6 0.3 fusion.37
  61.0 0.3 convolution_bitcast_fusion.6
  61.3 0.9 multiply_reduce_fusion
  62.2 0.4 convolution_bitcast_fusion
  62.6 0.8 copy.250
  63.5 0.6 fusion.2
  64.1 0.4 fusion.6
  64.5 0.8 copy.248
  65.3 0.4 fusion.33
  65.8 1.3 %copy.251 = f32[128,16,128]{2,0,1:T(8,128)} copy(f32[128,16,128]{2,1,0:T(8,128)S(1)} %get-tuple-element.5) | data formatting | bytes 2097152 | tf_op jit(solution)/shard_map/jit(dynamic_index_in_dim)/squeeze | solution.py:187
  67.1 1.9 %collective-permute-start.1 = (f32[128,16,128]{2,0,1:T(8,128)}, f32[128,16,128]{2,0,1:T(8,128)}, u32[]{:S(2)}, u32[]{:S(2)}) collective-permute-start(f32[128,16,128]{2,0,1:T(8,128)} %copy.251), channel_id=1, source_target_pairs={{0,4},{4,0},{1,5},{5,1},{2,6},{6,2},{3,7},{7,3},{8,12},{12,8},{9,1... | collective-permute-start | bytes 3145736 | tf_op jit(solution)/shard_map/ppermute | solution.py:188
  69.0 1.1 fusion.80
  70.2 1.9 %fusion.24 = bf16[256,1,2,128]{0,3,2,1:T(8,128)(2,1)} fusion(bf16[256,2,128]{2,0,1:T(8,128)(2,1)S(1)} %bitcast.246, f32[2,256,256]{1,2,0:T(8,128)} %get-tuple-element.38, f32[2,256]{1,0:T(2,128)S(1)} %get-tuple-element.37), kind=kOutput, calls=%fused_computation.50 | convolution fusion | flops 33882112 | bytes 788480 | tf_op jit(solution)/shard_map/rgbc,brgd->crgd/dot_general | solution.py:128
  72.2 1.0 copy.241
  73.2 2.0 %multiply_reduce_fusion.1 = (f32[256,2]{0,1:T(2,128)S(1)}, bf16[256,1,2,128]{0,3,2,1:T(8,128)(2,1)}) fusion(f32[256,1,2,128]{0,3,2,1:T(8,128)S(1)} %copy.231, bf16[256,2,128]{2,0,1:T(8,128)(2,1)} %bitcast.262, f32[2,256,256]{1,2,0:T(8,128)} %get-tuple-element.38, f32[2,256]{1,0:T(2,128)S(1)} %get-tuple-element.37), kind=kOutput, calls=%fused_computation.90 | convolution fusion | flops 34078208 | bytes 1052672 | tf_op jit(solution)/shard_map/rgbc,crgd->brgd/dot_general | solution.py:111
  75.2 1.3 %fusion.11 = bf16[2,256,256]{1,2,0:T(8,128)(2,1)S(1)} fusion(bf16[256,2,128]{2,0,1:T(8,128)(2,1)S(1)} %bitcast.247, bf16[256,2,128]{2,0,1:T(8,128)(2,1)} %bitcast.263, f32[2,256]{1,0:T(2,128)S(1)} %bitcast.270, f32[2,256,256]{1,2,0:T(8,128)} %get-tuple-element.38, f32[2,256]{1,0:T(2,128)S(1)} %get-tuple-element.37), kind=kOutput, calls=%fused_computation.25 | convolution fusion | flops 34078720 | bytes 1052672 | tf_op jit(solution)/shard_map/brgd,crgd->rgbc/dot_general | solution.py:114
  76.8 0.8 copy.235
  77.6 1.1 fusion.25
  78.9 1.0 copy.230
  79.9 1.4 %maximum_bitcast_fusion.1 = bf16[128,4,4,128]{3,2,0,1:T(4,128)(2,1)S(1)} fusion(bf16[1,128,4,128]{3,2,1,0:T(4,128)(2,1)S(1)} %bitcast.248, bf16[1,128,4,128]{3,2,1,0:T(4,128)(2,1)S(1)} %bitcast.250, bf16[1,128,4,128]{3,2,1,0:T(4,128)(2,1)} %bitcast.249, bf16[1,128,4,128]{3,2,1,0:T(4,128)(2,1)S(1)} %bitcast.251), kind=kLoop, calls=%fused_computation.69 | loop fusion | flops 786432 | bytes 1048576 | tf_op jit(solution)/shard_map/transpose | solution.py:183
  81.4 1.6 %fusion.36 = bf16[128,16,128]{2,0,1:T(8,128)(2,1)S(1)} fusion(f32[128,16,128]{2,0,1:T(8,128)} %collective-permute-done.1, f32[128,16,128]{2,1,0:T(8,128)S(1)} %get-tuple-element.4), kind=kLoop, calls=%fused_computation.66 | loop fusion | flops 524288 | bytes 2621440 | tf_op jit(solution)/shard_map/convert_element_type | solution.py:188
  83.1 1.6 %copy.253 = bf16[128,32,128]{2,1,0:T(8,128)(2,1)} copy(bf16[128,32,128]{2,0,1:T(8,128)(2,1)S(1)} %pad_maximum_fusion.1) | data formatting | bytes 2097152 | tf_op jit(solution)/shard_map/concatenate | solution.py:190
  84.7 6.5 %all-to-all-start.1 = ((bf16[128,32,128]{2,1,0:T(8,128)(2,1)}), bf16[128,32,128]{2,1,0:T(8,128)(2,1)S(1)}, u32[]{:S(2)}, u32[]{:S(2)}) async-start(bf16[128,32,128]{2,1,0:T(8,128)(2,1)} %copy.253), calls=%async_computation.1 | async-start | bytes 2097152 | tf_op jit(solution)/shard_map/all_to_all | solution.py:189
  91.2 0.4 copy.261
  91.7 1.3 %fusion.22 = bf16[2,2,128,128]{2,3,1,0:T(8,128)(2,1)S(1)} fusion(bf16[2,128,1,2,128]{1,4,3,0,2:T(8,128)(2,1)} %copy-done.8, f32[2,2,128]{2,1,0:T(2,128)S(1)} %bitcast.269, f32[2,2,128]{2,1,0:T(2,128)S(1)} %copy_add_fusion.1, f32[2,2,128,128]{2,3,1,0:T(8,128)} %copy-done.6, f32[2,2,128]{2,1,0:T(2,128)S(1)} %copy_maximum_fusion, ...), kind=kOutput, calls=%fused_computation.46 | convolution fusion | flops 17104896 | bytes 661504 | tf_op jit(solution)/shard_map/bqgd,bkgd->bgqk/dot_general | solution.py:66
  93.0 0.3 convolution_bitcast_fusion.5
  94.1 26.3 %all-to-all-done.1 = bf16[128,32,128]{2,1,0:T(8,128)(2,1)S(1)} async-done(((bf16[128,32,128]{2,1,0:T(8,128)(2,1)}), bf16[128,32,128]{2,1,0:T(8,128)(2,1)S(1)}, u32[]{:S(2)}, u32[]{:S(2)}) %all-to-all-start.1) | async-done | bytes 1048608 | tf_op jit(solution)/shard_map/all_to_all | solution.py:189
  121.3 0.5 copy.254
  122.1 0.7 copy.356
  123.2 0.7 copy.357
  124.2 0.7 copy.358
  125.2 0.7 copy.359
  (78 shorter events, 5.2 us)
Async XLA Ops:
  0.6 2.6 %copy-start.4 = (bf16[256,512]{1,0:T(8,128)(2,1)S(1)}, bf16[256,512]{1,0:T(8,128)(2,1)}, u32[]{:S(2)}) copy-start(bf16[256,512]{1,0:T(8,128)(2,1)} %param.6) | copy-start | bytes 786436
  0.6 2.6 %copy-start.5 = (bf16[256,512]{1,0:T(8,128)(2,1)S(1)}, bf16[256,512]{1,0:T(8,128)(2,1)}, u32[]{:S(2)}) copy-start(bf16[256,512]{1,0:T(8,128)(2,1)} %param.7) | copy-start | bytes 786436
  7.2 45.8 %all-to-all-start = ((bf16[128,32,128]{2,1,0:T(8,128)(2,1)}), bf16[128,32,128]{2,1,0:T(8,128)(2,1)S(1)}, u32[]{:S(2)}, u32[]{:S(2)}) async-start(bf16[128,32,128]{2,1,0:T(8,128)(2,1)} %copy.217), calls=%async_computation | async-start | bytes 2097152 | tf_op jit(solution)/shard_map/all_to_all | solution.py:155
  53.2 5.3 %collective-permute-start = (bf16[128,16,128]{2,1,0:T(8,128)(2,1)S(1)}, bf16[128,16,128]{2,1,0:T(8,128)(2,1)S(1)}, u32[]{:S(2)}, u32[]{:S(2)}) collective-permute-start(bf16[128,16,128]{2,1,0:T(8,128)(2,1)S(1)} %get-tuple-element.10), channel_id=1, source_target_pairs={{0,4},{4,0},{1,5},{5,1},{2,6},{6,2},{3,7},{7,3},{8,12},{12,8},{9,1... | collective-permute-start | bytes 1572872 | tf_op jit(solution)/shard_map/ppermute | solution.py:165
  56.8 4.5 %copy-start.8 = (bf16[2,128,1,2,128]{1,4,3,0,2:T(8,128)(2,1)}, bf16[2,128,1,2,128]{1,4,3,0,2:T(8,128)(2,1)S(1)}, u32[]{:S(2)}) copy-start(bf16[2,128,1,2,128]{1,4,3,0,2:T(8,128)(2,1)S(1)} %copy.308) | copy-start | bytes 393220
  57.2 4.2 %copy-start.6 = (f32[2,2,128,128]{2,3,1,0:T(8,128)}, f32[2,2,128,128]{2,3,1,0:T(8,128)S(1)}, u32[]{:S(2)}) copy-start(f32[2,2,128,128]{2,3,1,0:T(8,128)S(1)} %get-tuple-element.32) | copy-start | bytes 786436
  58.5 10.4 %copy-start.1 = (bf16[1,128,2,1,2,128]{5,2,1,4,3,0:T(2,128)(2,1)}, bf16[1,128,2,1,2,128]{5,2,1,4,3,0:T(2,128)(2,1)S(1)}, u32[]{:S(2)}) copy-start(bf16[1,128,2,1,2,128]{5,2,1,4,3,0:T(2,128)(2,1)S(1)} %get-tuple-element.20) | copy-start | bytes 393220
  58.6 10.4 %copy-start.2 = (bf16[1,128,2,1,2,128]{5,2,1,4,3,0:T(2,128)(2,1)}, bf16[1,128,2,1,2,128]{5,2,1,4,3,0:T(2,128)(2,1)S(1)}, u32[]{:S(2)}) copy-start(bf16[1,128,2,1,2,128]{5,2,1,4,3,0:T(2,128)(2,1)S(1)} %get-tuple-element.19) | copy-start | bytes 393220
  65.8 4.3 %copy-start = (bf16[1,128,2,1,2,128]{5,2,1,4,3,0:T(2,128)(2,1)S(1)}, bf16[1,128,2,1,2,128]{5,2,1,4,3,0:T(2,128)(2,1)}, u32[]{:S(2)}) copy-start(bf16[1,128,2,1,2,128]{5,2,1,4,3,0:T(2,128)(2,1)} %get-tuple-element.18) | copy-start | bytes 393220
  67.1 14.3 %collective-permute-start.1 = (f32[128,16,128]{2,0,1:T(8,128)}, f32[128,16,128]{2,0,1:T(8,128)}, u32[]{:S(2)}, u32[]{:S(2)}) collective-permute-start(f32[128,16,128]{2,0,1:T(8,128)} %copy.251), channel_id=1, source_target_pairs={{0,4},{4,0},{1,5},{5,1},{2,6},{6,2},{3,7},{7,3},{8,12},{12,8},{9,1... | collective-permute-start | bytes 3145736 | tf_op jit(solution)/shard_map/ppermute | solution.py:188
  73.2 3.4 %copy-start.3 = (bf16[1,128,2,1,2,128]{5,2,1,4,3,0:T(2,128)(2,1)S(1)}, bf16[1,128,2,1,2,128]{5,2,1,4,3,0:T(2,128)(2,1)}, u32[]{:S(2)}) copy-start(bf16[1,128,2,1,2,128]{5,2,1,4,3,0:T(2,128)(2,1)} %copy-done.2) | copy-start | bytes 393220
  84.7 35.7 %all-to-all-start.1 = ((bf16[128,32,128]{2,1,0:T(8,128)(2,1)}), bf16[128,32,128]{2,1,0:T(8,128)(2,1)S(1)}, u32[]{:S(2)}, u32[]{:S(2)}) async-start(bf16[128,32,128]{2,1,0:T(8,128)(2,1)} %copy.253), calls=%async_computation.1 | async-start | bytes 2097152 | tf_op jit(solution)/shard_map/all_to_all | solution.py:189
  91.7 1.9 %copy-start.7 = (f32[2,2,128,128]{2,3,1,0:T(8,128)S(1)}, f32[2,2,128,128]{2,3,1,0:T(8,128)}, u32[]{:S(2)}) copy-start(f32[2,2,128,128]{2,3,1,0:T(8,128)} %copy-done.6) | copy-start | bytes 786436
  91.7 1.9 %copy-start.9 = (bf16[2,128,1,2,128]{1,4,3,0,2:T(8,128)(2,1)S(1)}, bf16[2,128,1,2,128]{1,4,3,0,2:T(8,128)(2,1)}, u32[]{:S(2)}) copy-start(bf16[2,128,1,2,128]{1,4,3,0,2:T(8,128)(2,1)} %copy-done.8) | copy-start | bytes 393220
  121.9 3.0 %copy-start.10 = (bf16[2,128,2,128]{1,3,2,0:T(8,128)(2,1)S(1)}, bf16[2,128,2,128]{1,3,2,0:T(8,128)(2,1)}, u32[]{:S(2)}) copy-start(bf16[2,128,2,128]{1,3,2,0:T(8,128)(2,1)} %get-tuple-element.36) | copy-start | bytes 393220

commit v9 on v7

--- a/solution.py
+++ b/solution.py
@@ -181,10 +181,12 @@
 
     strided_out = strided_out.reshape(4, peers, -1, head_dim).transpose(1, 0, 2, 3)
     strided_out = strided_out.reshape(peers, -1, head_dim)
-    terms = terms.reshape(2, peers, -1, head_dim)
+    terms = terms.astype(jnp.bfloat16).reshape(2, peers, -1, head_dim)
     keep = jnp.where(core == 0, terms[0], terms[1])
     give = jnp.where(core == 0, terms[1], terms[0])
-    terms = (keep + lax.ppermute(give, "ctx_core", swap)).astype(jnp.bfloat16)
+    terms = (
+        keep.astype(jnp.float32) + lax.ppermute(give, "ctx_core", swap).astype(jnp.float32)
+    ).astype(jnp.bfloat16)
     returned = lax.all_to_all(
         jnp.concatenate([strided_out, terms], axis=1), CTX, 0, 0, tiled=True
     )

time: 123 us -> 121 us (0.984)
  matrix products: 12.8 us -> 8.74 us
  local copies, waits for them, and re-layouts: 18.8 us -> 20.2 us
    unnamed x35 -> x41, local copies, waits for them, and re-layouts: 3.31 us -> 3.33 us
  transfers between devices with their start and end apart: 4 -> 4, of which waited for: 3 -> 3; matrix products, arithmetic and copies ran while one was open for 11% -> 8% of each run, Pallas kernels for 0% -> 0%
where the time goes in v9:
time: 121 us
  waiting for transfers between devices  56.3 us (47%)
  starting transfers between devices  28.5 us (24%)
  local copies, waits for them, and re-layouts  20.2 us (17%)
  matrix products  8.74 us (7%)
  other arithmetic  5.62 us (5%)
  between operations  1.35 us (1%)
    all_to_all x1, waiting for transfers between devices, shards(): lax.all_to_all(jnp.concatenate([strided_rows, summary_rows], axis=1), CTX...  28.8 us
    all_to_all x1, waiting for transfers between devices, shards(): lax.all_to_all(jnp.concatenate([strided_out, terms], axis=1), CTX, 0, 0,...  26.3 us
    all_to_all x1, starting transfers between devices, shards(): lax.all_to_all(jnp.concatenate([strided_rows, summary_rows], axis=1), CTX...  16.6 us
    all_to_all x1, starting transfers between devices, shards(): lax.all_to_all(jnp.concatenate([strided_out, terms], axis=1), CTX, 0, 0,...  6.17 us
    unnamed x41, local copies, waits for them, and re-layouts  3.33 us
    ppermute x1, starting transfers between devices, shards(): sibling = lax.ppermute(mine, 'ctx_core', swap)  3.23 us
    ppermute x1, starting transfers between devices, shards(): lax.ppermute(give, 'ctx_core', swap).astype(jnp.float32)  2.44 us
  transfers between devices with their start and end apart: 4, of which 3 were waited for; matrix products, arithmetic and copies ran while one was open for 8% of the time, Pallas kernels for 0%

profile of v9, /device:TPU:1, one launch (start us, length us, event | category | flops | bytes accessed | tf_op | source)
XLA Modules:
  0.0 120.7 jit_solution(9170856023180104223)
XLA Ops:
  0.7 1.1 reshape.353
  1.7 1.0 reshape.355
  2.7 0.4 slice_bitcast_fusion.6
  3.3 0.4 slice_bitcast_fusion.5
  3.7 1.0 maximum_bitcast_fusion
  5.2 0.3 broadcast_in_dim.63
  5.5 1.6 %copy.218 = bf16[128,32,128]{2,1,0:T(8,128)(2,1)} copy(bf16[128,32,128]{2,0,1:T(8,128)(2,1)S(1)} %pad_maximum_fusion) | data formatting | bytes 2097152 | tf_op jit(solution)/shard_map/concatenate | solution.py:156
  7.2 16.6 %all-to-all-start = ((bf16[128,32,128]{2,1,0:T(8,128)(2,1)}), bf16[128,32,128]{2,1,0:T(8,128)(2,1)S(1)}, u32[]{:S(2)}, u32[]{:S(2)}) async-start(bf16[128,32,128]{2,1,0:T(8,128)(2,1)} %copy.218), calls=%async_computation | async-start | bytes 2097152 | tf_op jit(solution)/shard_map/all_to_all | solution.py:155
  24.2 28.8 %all-to-all-done = bf16[128,32,128]{2,1,0:T(8,128)(2,1)S(1)} async-done(((bf16[128,32,128]{2,1,0:T(8,128)(2,1)}), bf16[128,32,128]{2,1,0:T(8,128)(2,1)S(1)}, u32[]{:S(2)}, u32[]{:S(2)}) %all-to-all-start) | async-done | bytes 1048608 | tf_op jit(solution)/shard_map/all_to_all | solution.py:155
  53.0 3.2 %collective-permute-start = (bf16[128,16,128]{2,1,0:T(8,128)(2,1)S(1)}, bf16[128,16,128]{2,1,0:T(8,128)(2,1)S(1)}, u32[]{:S(2)}, u32[]{:S(2)}) collective-permute-start(bf16[128,16,128]{2,1,0:T(8,128)(2,1)S(1)} %slice.139), channel_id=1, source_target_pairs={{0,4},{4,0},{1,5},{5,1},{2,6},{6,2},{3,7},{7,3},{8,12},{12,8},{9,1... | collective-permute-start | bytes 1572872 | tf_op jit(solution)/shard_map/ppermute | solution.py:165
  56.6 1.2 collective-permute-done
  57.9 0.3 copy.362
  58.2 1.0 fusion.68
  59.2 0.8 copy.232
  60.1 0.3 fusion.73
  60.6 0.8 copy.242
  61.4 0.4 copy.226
  61.9 0.5 fusion.72
  62.4 0.3 fusion.4
  62.7 0.3 fusion.32
  63.1 0.3 convolution_bitcast_fusion.6
  63.4 0.4 fusion.6
  63.9 0.9 multiply_reduce_fusion
  64.8 0.6 fusion.2
  65.4 0.5 select_bitcast_fusion
  65.9 0.5 copy.251
  66.4 0.9 copy.252
  67.4 2.4 %collective-permute-start.1 = (bf16[128,16,128]{2,0,1:T(8,128)(2,1)}, bf16[128,16,128]{2,0,1:T(8,128)(2,1)}, u32[]{:S(2)}, u32[]{:S(2)}) collective-permute-start(bf16[128,16,128]{2,0,1:T(8,128)(2,1)} %copy.252), channel_id=1, source_target_pairs={{0,4},{4,0},{1,5},{5,1},{2,6},{6,2},{3,7},{7,3},{8,12},{12,8},{9,1... | collective-permute-start | bytes 1572872 | tf_op jit(solution)/shard_map/ppermute | solution.py:188
  69.9 0.9 multiply_reduce_fusion.1
  71.2 0.8 copy.236
  72.0 1.1 fusion.26
  73.3 1.0 copy.231
  74.3 1.4 %maximum_bitcast_fusion.1 = bf16[128,4,4,128]{3,2,0,1:T(4,128)(2,1)S(1)} fusion(bf16[1,128,4,128]{3,2,1,0:T(4,128)(2,1)S(1)} %bitcast.250, bf16[1,128,4,128]{3,2,1,0:T(4,128)(2,1)S(1)} %bitcast.252, bf16[1,128,4,128]{3,2,1,0:T(4,128)(2,1)} %bitcast.251, bf16[1,128,4,128]{3,2,1,0:T(4,128)(2,1)S(1)} %bitcast.253), kind=kLoop, calls=%fused_computation.58 | loop fusion | flops 786432 | bytes 1048576 | tf_op jit(solution)/shard_map/transpose | solution.py:182
  75.8 0.8 copy.250
  76.6 1.5 %fusion.31 = bf16[128,16,128]{2,0,1:T(8,128)(2,1)S(1)} fusion(f32[128,16,128]{2,1,0:T(8,128)S(1)} %bitcast.229, bf16[128,16,128]{2,0,1:T(8,128)(2,1)} %collective-permute-done.1), kind=kLoop, calls=%fused_computation.54 | loop fusion | flops 786432 | bytes 2097152 | tf_op jit(solution)/shard_map/convert_element_type | solution.py:189
  78.2 1.6 %copy.254 = bf16[128,32,128]{2,1,0:T(8,128)(2,1)} copy(bf16[128,32,128]{2,0,1:T(8,128)(2,1)S(1)} %pad_maximum_fusion.1) | data formatting | bytes 2097152 | tf_op jit(solution)/shard_map/concatenate | solution.py:191
  79.8 6.2 %all-to-all-start.1 = ((bf16[128,32,128]{2,1,0:T(8,128)(2,1)}), bf16[128,32,128]{2,1,0:T(8,128)(2,1)S(1)}, u32[]{:S(2)}, u32[]{:S(2)}) async-start(bf16[128,32,128]{2,1,0:T(8,128)(2,1)} %copy.254), calls=%async_computation.1 | async-start | bytes 2097152 | tf_op jit(solution)/shard_map/all_to_all | solution.py:190
  86.0 0.4 copy.262
  86.5 1.3 %fusion.23 = bf16[2,2,128,128]{2,3,1,0:T(8,128)(2,1)S(1)} fusion(bf16[2,128,1,2,128]{1,4,3,0,2:T(8,128)(2,1)} %copy-done.11, f32[2,2,128]{2,1,0:T(2,128)S(1)} %bitcast.271, f32[2,2,128]{2,1,0:T(2,128)S(1)} %copy_add_fusion.1, f32[2,2,128,128]{2,3,1,0:T(8,128)} %copy-done.9, f32[2,2,128]{2,1,0:T(2,128)S(1)} %copy_maximum_fusion, ...), kind=kOutput, calls=%fused_computation.40 | convolution fusion | flops 17104896 | bytes 661504 | tf_op jit(solution)/shard_map/bqgd,bkgd->bgqk/dot_general | solution.py:66
  87.8 0.3 convolution_bitcast_fusion.5
  88.1 0.2 fusion.28
  88.6 0.2 fusion.13
  88.9 26.3 %all-to-all-done.1 = bf16[128,32,128]{2,1,0:T(8,128)(2,1)S(1)} async-done(((bf16[128,32,128]{2,1,0:T(8,128)(2,1)}), bf16[128,32,128]{2,1,0:T(8,128)(2,1)S(1)}, u32[]{:S(2)}, u32[]{:S(2)}) %all-to-all-start.1) | async-done | bytes 1048608 | tf_op jit(solution)/shard_map/all_to_all | solution.py:190
  116.1 0.5 copy.255
  116.9 0.7 copy.363
  118.0 0.7 copy.364
  119.0 0.7 copy.365
  119.9 0.7 copy.366
  (88 shorter events, 4.9 us)
Async XLA Ops:
  0.6 2.6 %copy-start.7 = (bf16[256,512]{1,0:T(8,128)(2,1)S(1)}, bf16[256,512]{1,0:T(8,128)(2,1)}, u32[]{:S(2)}) copy-start(bf16[256,512]{1,0:T(8,128)(2,1)} %param.6) | copy-start | bytes 786436
  0.6 2.6 %copy-start.8 = (bf16[256,512]{1,0:T(8,128)(2,1)S(1)}, bf16[256,512]{1,0:T(8,128)(2,1)}, u32[]{:S(2)}) copy-start(bf16[256,512]{1,0:T(8,128)(2,1)} %param.7) | copy-start | bytes 786436
  7.2 45.8 %all-to-all-start = ((bf16[128,32,128]{2,1,0:T(8,128)(2,1)}), bf16[128,32,128]{2,1,0:T(8,128)(2,1)S(1)}, u32[]{:S(2)}, u32[]{:S(2)}) async-start(bf16[128,32,128]{2,1,0:T(8,128)(2,1)} %copy.218), calls=%async_computation | async-start | bytes 2097152 | tf_op jit(solution)/shard_map/all_to_all | solution.py:155
  24.0 39.9 %copy-start.11 = (bf16[2,128,1,2,128]{1,4,3,0,2:T(8,128)(2,1)}, bf16[2,128,1,2,128]{1,4,3,0,2:T(8,128)(2,1)S(1)}, u32[]{:S(2)}) copy-start(bf16[2,128,1,2,128]{1,4,3,0,2:T(8,128)(2,1)S(1)} %copy.311) | copy-start | bytes 393220
  53.0 4.8 %collective-permute-start = (bf16[128,16,128]{2,1,0:T(8,128)(2,1)S(1)}, bf16[128,16,128]{2,1,0:T(8,128)(2,1)S(1)}, u32[]{:S(2)}, u32[]{:S(2)}) collective-permute-start(bf16[128,16,128]{2,1,0:T(8,128)(2,1)S(1)} %slice.139), channel_id=1, source_target_pairs={{0,4},{4,0},{1,5},{5,1},{2,6},{6,2},{3,7},{7,3},{8,12},{12,8},{9,1... | collective-permute-start | bytes 1572872 | tf_op jit(solution)/shard_map/ppermute | solution.py:165
  56.6 7.3 %copy-start.9 = (f32[2,2,128,128]{2,3,1,0:T(8,128)}, f32[2,2,128,128]{2,3,1,0:T(8,128)S(1)}, u32[]{:S(2)}) copy-start(f32[2,2,128,128]{2,3,1,0:T(8,128)S(1)} %get-tuple-element.30) | copy-start | bytes 786436
  59.2 2.2 %copy-start = (bf16[1,128,2,1,2,128]{5,2,1,4,3,0:T(2,128)(2,1)}, bf16[1,128,2,1,2,128]{5,2,1,4,3,0:T(2,128)(2,1)S(1)}, u32[]{:S(2)}) copy-start(bf16[1,128,2,1,2,128]{5,2,1,4,3,0:T(2,128)(2,1)S(1)} %get-tuple-element.16) | copy-start | bytes 393220
  59.2 2.2 %copy-start.3 = (bf16[1,128,2,1,2,128]{5,2,1,4,3,0:T(2,128)(2,1)}, bf16[1,128,2,1,2,128]{5,2,1,4,3,0:T(2,128)(2,1)S(1)}, u32[]{:S(2)}) copy-start(bf16[1,128,2,1,2,128]{5,2,1,4,3,0:T(2,128)(2,1)S(1)} %get-tuple-element.18) | copy-start | bytes 393220
  59.2 2.2 %copy-start.4 = (bf16[1,128,2,1,2,128]{5,2,1,4,3,0:T(2,128)(2,1)}, bf16[1,128,2,1,2,128]{5,2,1,4,3,0:T(2,128)(2,1)S(1)}, u32[]{:S(2)}) copy-start(bf16[1,128,2,1,2,128]{5,2,1,4,3,0:T(2,128)(2,1)S(1)} %get-tuple-element.17) | copy-start | bytes 393220
  60.4 1.9 %copy-start.15 = (f32[2,256,256]{1,2,0:T(8,128)}, f32[2,256,256]{1,2,0:T(8,128)S(1)}, u32[]{:S(2)}) copy-start(f32[2,256,256]{1,2,0:T(8,128)S(1)} %get-tuple-element.36) | copy-start | bytes 1572868
  65.4 4.4 %copy-start.6 = (f32[256,1,2,128]{0,3,2,1:T(8,128)S(1)}, f32[256,1,2,128]{0,3,2,1:T(8,128)}, u32[]{:S(2)}) copy-start(f32[256,1,2,128]{0,3,2,1:T(8,128)} %copy.232) | copy-start | bytes 786436
  65.4 4.4 %copy-start.14 = (bf16[1,128,2,1,2,128]{5,2,1,4,3,0:T(2,128)(2,1)S(1)}, bf16[1,128,2,1,2,128]{5,2,1,4,3,0:T(2,128)(2,1)}, u32[]{:S(2)}) copy-start(bf16[1,128,2,1,2,128]{5,2,1,4,3,0:T(2,128)(2,1)} %get-tuple-element.15) | copy-start | bytes 393220
  65.4 4.4 %copy-start.16 = (f32[2,256,256]{1,2,0:T(8,128)S(1)}, f32[2,256,256]{1,2,0:T(8,128)}, u32[]{:S(2)}) copy-start(f32[2,256,256]{1,2,0:T(8,128)} %copy-done.15) | copy-start | bytes 1572868
  65.9 4.9 %copy-start.1 = (bf16[1,128,2,1,2,128]{5,2,1,4,3,0:T(2,128)(2,1)S(1)}, bf16[1,128,2,1,2,128]{5,2,1,4,3,0:T(2,128)(2,1)}, u32[]{:S(2)}) copy-start(bf16[1,128,2,1,2,128]{5,2,1,4,3,0:T(2,128)(2,1)} %copy-done) | copy-start | bytes 393220
  67.4 9.3 %collective-permute-start.1 = (bf16[128,16,128]{2,0,1:T(8,128)(2,1)}, bf16[128,16,128]{2,0,1:T(8,128)(2,1)}, u32[]{:S(2)}, u32[]{:S(2)}) collective-permute-start(bf16[128,16,128]{2,0,1:T(8,128)(2,1)} %copy.252), channel_id=1, source_target_pairs={{0,4},{4,0},{1,5},{5,1},{2,6},{6,2},{3,7},{7,3},{8,12},{12,8},{9,1... | collective-permute-start | bytes 1572872 | tf_op jit(solution)/shard_map/ppermute | solution.py:188
  69.9 1.1 copy-start.5
  70.8 3.6 %copy-start.2 = (bf16[256,1,2,128]{3,2,0,1:T(2,128)(2,1)S(1)}, bf16[256,1,2,128]{3,2,0,1:T(2,128)(2,1)}, u32[]{:S(2)}) copy-start(bf16[256,1,2,128]{3,2,0,1:T(2,128)(2,1)} %copy.242) | copy-start | bytes 393220
  79.8 35.3 %all-to-all-start.1 = ((bf16[128,32,128]{2,1,0:T(8,128)(2,1)}), bf16[128,32,128]{2,1,0:T(8,128)(2,1)S(1)}, u32[]{:S(2)}, u32[]{:S(2)}) async-start(bf16[128,32,128]{2,1,0:T(8,128)(2,1)} %copy.254), calls=%async_computation.1 | async-start | bytes 2097152 | tf_op jit(solution)/shard_map/all_to_all | solution.py:190
  86.4 1.9 %copy-start.10 = (f32[2,2,128,128]{2,3,1,0:T(8,128)S(1)}, f32[2,2,128,128]{2,3,1,0:T(8,128)}, u32[]{:S(2)}) copy-start(f32[2,2,128,128]{2,3,1,0:T(8,128)} %copy-done.9) | copy-start | bytes 786436
  86.5 1.9 %copy-start.12 = (bf16[2,128,1,2,128]{1,4,3,0,2:T(8,128)(2,1)S(1)}, bf16[2,128,1,2,128]{1,4,3,0,2:T(8,128)(2,1)}, u32[]{:S(2)}) copy-start(bf16[2,128,1,2,128]{1,4,3,0,2:T(8,128)(2,1)} %copy-done.11) | copy-start | bytes 393220
  116.7 3.0 %copy-start.13 = (bf16[2,128,2,128]{1,3,2,0:T(8,128)(2,1)S(1)}, bf16[2,128,2,128]{1,3,2,0:T(8,128)(2,1)}, u32[]{:S(2)}) copy-start(bf16[2,128,2,128]{1,3,2,0:T(8,128)(2,1)} %get-tuple-element.34) | copy-start | bytes 393220

commit v10 on v9

--- a/solution.py
+++ b/solution.py
@@ -131,6 +131,17 @@
     return jnp.stack([attended, query_grad, key_grad, value_grad])
 
 
+def head_columns(matrix, first):
+    groups = matrix.shape[1] // (4 * HD)
+    return jnp.stack(
+        [
+            matrix[:, (4 * group + first + head) * HD : (4 * group + first + head + 1) * HD]
+            for group in range(groups)
+            for head in range(2)
+        ]
+    )
+
+
 def shards(queries, keys, values, out_grad):
     scaling = 1.0 / math.sqrt(HD)
     query_fixed, query_strided = split_heads(queries)
@@ -143,12 +154,13 @@
     core = lax.axis_index("ctx_core")
     swap = [(0, 1), (1, 0)]
 
-    strided_rows = jnp.stack([query_strided, key_strided, value_strided, grad_strided])
-    strided_rows = strided_rows.reshape(4, blocks_here, peers, residues, half_heads, head_dim)
-    strided_rows = strided_rows.transpose(2, 0, 1, 3, 4, 5).reshape(peers, -1, head_dim)
-    summary_rows = jnp.stack(
-        [key_fixed[:, positions - SUMMARY :], value_fixed[:, positions - SUMMARY :]]
-    ).reshape(1, 2, -1, head_dim)
+    strided_rows = jnp.stack([head_columns(rows, 2) for rows in (queries, keys, values, out_grad)])
+    strided_rows = strided_rows.reshape(4, half_heads, blocks_here, peers, residues, head_dim)
+    strided_rows = strided_rows.transpose(3, 0, 2, 4, 1, 5).reshape(peers, -1, head_dim)
+    summary_rows = jnp.stack([head_columns(keys, 0), head_columns(values, 0)])
+    summary_rows = summary_rows.reshape(2, half_heads, blocks_here, positions, head_dim)
+    summary_rows = summary_rows[:, :, :, positions - SUMMARY :].transpose(0, 2, 3, 1, 4)
+    summary_rows = summary_rows.reshape(1, 2, -1, head_dim)
     summary_rows = jnp.broadcast_to(summary_rows, (peers // 2,) + summary_rows.shape[1:])
     summary_rows = summary_rows.reshape(peers, -1, head_dim)
     strided_size = strided_rows.shape[1]

time: 121 us -> 123 us (1.017)
  local copies, waits for them, and re-layouts: 20.2 us -> 21.9 us
    slice x4 -> x11, local copies, waits for them, and re-layouts: 0.22 us -> 4.49 us  [the longest x4 3.7 us: head_columns(): matrix[:, (4 * group + first + head) * HD:(4 * group + first + head + 1)...]
    reshape x4, local copies, waits for them, and re-layouts: 2.22 us -> 0.26 us  [split_heads(): shaped = matrix.reshape(blocks, STRIDE, matrix.shape[1] // (4 * HD), 4, HD)]
where the time goes in v10:
time: 123 us; the launch traced here: 122 us
  waiting for transfers between devices  55.4 us (45%)
  starting transfers between devices  28.7 us (23%)
  local copies, waits for them, and re-layouts  21.9 us (18%)
  matrix products  9.65 us (8%)
  other arithmetic  4.83 us (4%)
  between operations  1.43 us (1%)
    all_to_all x1, waiting for transfers between devices, shards(): lax.all_to_all(jnp.concatenate([strided_rows, summary_rows], axis=1), CTX...  27.9 us
    all_to_all x1, waiting for transfers between devices, shards(): lax.all_to_all(jnp.concatenate([strided_out, terms], axis=1), CTX, 0, 0,...  26.3 us
    all_to_all x1, starting transfers between devices, shards(): lax.all_to_all(jnp.concatenate([strided_rows, summary_rows], axis=1), CTX...  16.8 us
    all_to_all x1, starting transfers between devices, shards(): lax.all_to_all(jnp.concatenate([strided_out, terms], axis=1), CTX, 0, 0,...  6.29 us
    slice x4, local copies, waits for them, and re-layouts, head_columns(): matrix[:, (4 * group + first + head) * HD:(4 * group + first + head + 1)...  3.7 us
    unnamed x41, local copies, waits for them, and re-layouts  3.44 us
    ppermute x1, starting transfers between devices, shards(): sibling = lax.ppermute(mine, 'ctx_core', swap)  3.23 us
  transfers between devices with their start and end apart: 4, of which 3 were waited for; matrix products, arithmetic and copies ran while one was open for 8% of the time, Pallas kernels for 0%

profile of v10, /device:TPU:1, one launch (start us, length us, event | category | flops | bytes accessed | tf_op | source)
XLA Modules:
  0.0 122.0 jit_solution(6122710837236161371)
XLA Ops:
  0.6 0.9 fusion.69
  1.5 0.9 fusion.72
  2.4 1.0 fusion.70
  3.6 1.0 fusion.71
  4.9 0.3 broadcast_in_dim.63
  5.3 1.7 %copy.241 = bf16[128,32,128]{2,1,0:T(8,128)(2,1)} copy(bf16[128,32,128]{2,0,1:T(8,128)(2,1)S(1)} %pad_maximum_fusion) | data formatting | bytes 2097152 | tf_op jit(solution)/shard_map/concatenate | solution.py:168
  7.0 16.8 %all-to-all-start = ((bf16[128,32,128]{2,1,0:T(8,128)(2,1)}), bf16[128,32,128]{2,1,0:T(8,128)(2,1)S(1)}, u32[]{:S(2)}, u32[]{:S(2)}) async-start(bf16[128,32,128]{2,1,0:T(8,128)(2,1)} %copy.241), calls=%async_computation | async-start | bytes 2097152 | tf_op jit(solution)/shard_map/all_to_all | solution.py:167
  25.0 27.9 %all-to-all-done = bf16[128,32,128]{2,1,0:T(8,128)(2,1)S(1)} async-done(((bf16[128,32,128]{2,1,0:T(8,128)(2,1)}), bf16[128,32,128]{2,1,0:T(8,128)(2,1)S(1)}, u32[]{:S(2)}, u32[]{:S(2)}) %all-to-all-start) | async-done | bytes 1048608 | tf_op jit(solution)/shard_map/all_to_all | solution.py:167
  52.9 3.2 %collective-permute-start = (bf16[128,16,128]{2,1,0:T(8,128)(2,1)S(1)}, bf16[128,16,128]{2,1,0:T(8,128)(2,1)S(1)}, u32[]{:S(2)}, u32[]{:S(2)}) collective-permute-start(bf16[128,16,128]{2,1,0:T(8,128)(2,1)S(1)} %slice.161), channel_id=1, source_target_pairs={{0,4},{4,0},{1,5},{5,1},{2,6},{6,2},{3,7},{7,3},{8,12},{12,8},{9,1... | collective-permute-start | bytes 1572872 | tf_op jit(solution)/shard_map/ppermute | solution.py:177
  56.5 1.2 collective-permute-done
  58.3 0.8 copy.261
  59.6 0.8 copy.253
  60.4 1.1 fusion.76
  61.5 1.3 %fusion.25 = bf16[256,1,2,128]{0,3,2,1:T(8,128)(2,1)S(1)} fusion(bf16[256,2,128]{2,0,1:T(8,128)(2,1)S(1)} %bitcast.264, f32[2,256,256]{1,2,0:T(8,128)} %get-tuple-element.41, f32[2,256]{1,0:T(2,128)S(1)} %get-tuple-element.40), kind=kOutput, calls=%fused_computation.44 | convolution fusion | flops 33882112 | bytes 788480 | tf_op jit(solution)/shard_map/rgbc,brgd->crgd/dot_general | solution.py:128
  62.8 0.8 copy.271
  63.6 0.4 copy.250
  64.0 0.5 fusion.75
  64.5 0.3 fusion.4
  64.9 0.3 fusion.32
  65.2 0.3 convolution_bitcast_fusion.6
  65.5 0.4 fusion.6
  66.0 0.9 multiply_reduce_fusion
  66.9 0.6 fusion.2
  67.5 0.4 select_bitcast_fusion
  68.0 0.5 copy.280
  68.5 0.9 copy.281
  69.5 2.5 %collective-permute-start.1 = (bf16[128,16,128]{2,0,1:T(8,128)(2,1)}, bf16[128,16,128]{2,0,1:T(8,128)(2,1)}, u32[]{:S(2)}, u32[]{:S(2)}) collective-permute-start(bf16[128,16,128]{2,0,1:T(8,128)(2,1)} %copy.281), channel_id=1, source_target_pairs={{0,4},{4,0},{1,5},{5,1},{2,6},{6,2},{3,7},{7,3},{8,12},{12,8},{9,1... | collective-permute-start | bytes 1572872 | tf_op jit(solution)/shard_map/ppermute | solution.py:200
  72.0 0.9 multiply_reduce_fusion.1
  72.9 0.2 fusion.12
  73.1 0.2 fusion.27
  73.4 0.8 copy.265
  74.5 1.0 copy.258
  75.5 1.4 %maximum_bitcast_fusion = bf16[128,4,4,128]{3,2,0,1:T(4,128)(2,1)S(1)} fusion(bf16[1,128,4,128]{3,2,1,0:T(4,128)(2,1)} %bitcast.244, bf16[1,128,4,128]{3,2,1,0:T(4,128)(2,1)S(1)} %bitcast.246, bf16[1,128,4,128]{3,2,1,0:T(4,128)(2,1)} %bitcast.245, bf16[1,128,4,128]{3,2,1,0:T(4,128)(2,1)S(1)} %bitcast.247), kind=kLoop, calls=%fused_computation.58 | loop fusion | flops 786432 | bytes 1048576 | tf_op jit(solution)/shard_map/transpose | solution.py:194
  77.1 0.8 copy.279
  77.9 1.5 %fusion.31 = bf16[128,16,128]{2,0,1:T(8,128)(2,1)S(1)} fusion(f32[128,16,128]{2,1,0:T(8,128)S(1)} %bitcast.223, bf16[128,16,128]{2,0,1:T(8,128)(2,1)} %collective-permute-done.1), kind=kLoop, calls=%fused_computation.54 | loop fusion | flops 786432 | bytes 2097152 | tf_op jit(solution)/shard_map/convert_element_type | solution.py:201
  79.5 1.7 %copy.283 = bf16[128,32,128]{2,1,0:T(8,128)(2,1)} copy(bf16[128,32,128]{2,0,1:T(8,128)(2,1)S(1)} %pad_maximum_fusion.1) | data formatting | bytes 2097152 | tf_op jit(solution)/shard_map/concatenate | solution.py:203
  81.1 6.3 %all-to-all-start.1 = ((bf16[128,32,128]{2,1,0:T(8,128)(2,1)}), bf16[128,32,128]{2,1,0:T(8,128)(2,1)S(1)}, u32[]{:S(2)}, u32[]{:S(2)}) async-start(bf16[128,32,128]{2,1,0:T(8,128)(2,1)} %copy.283), calls=%async_computation.1 | async-start | bytes 2097152 | tf_op jit(solution)/shard_map/all_to_all | solution.py:202
  87.4 0.4 copy.291
  87.9 1.3 %fusion.23 = bf16[2,2,128,128]{2,3,1,0:T(8,128)(2,1)S(1)} fusion(bf16[2,128,1,2,128]{1,4,3,0,2:T(8,128)(2,1)S(1)} %copy-done.10, bf16[2,128,1,2,128]{1,4,3,0,2:T(8,128)(2,1)} %copy-done.11, f32[2,2,128]{2,1,0:T(2,128)S(1)} %bitcast.273, f32[2,2,128]{2,1,0:T(2,128)S(1)} %copy_add_fusion.1, f32[2,2,128,128]{2,3,1,0:T(8,128)} %copy-done.6, ...), kind=kOutput, calls=%fused_computation.40 | convolution fusion | flops 17104896 | bytes 661504 | tf_op jit(solution)/shard_map/bqgd,bkgd->bgqk/dot_general | solution.py:66
  89.2 0.3 convolution_bitcast_fusion.5
  89.5 0.2 fusion.28
  90.0 0.2 fusion.13
  90.3 26.3 %all-to-all-done.1 = bf16[128,32,128]{2,1,0:T(8,128)(2,1)S(1)} async-done(((bf16[128,32,128]{2,1,0:T(8,128)(2,1)}), bf16[128,32,128]{2,1,0:T(8,128)(2,1)S(1)}, u32[]{:S(2)}, u32[]{:S(2)}) %all-to-all-start.1) | async-done | bytes 1048608 | tf_op jit(solution)/shard_map/all_to_all | solution.py:202
  117.5 0.5 copy.284
  118.4 0.7 copy.388
  119.3 0.7 copy.387
  120.3 0.7 copy.390
  121.2 0.7 copy.389
  (95 shorter events, 5.8 us)
Async XLA Ops:
  5.3 18.5 %copy-start.2 = (bf16[256,512]{1,0:T(8,128)(2,1)S(1)}, bf16[256,512]{1,0:T(8,128)(2,1)}, u32[]{:S(2)}) copy-start(bf16[256,512]{1,0:T(8,128)(2,1)} %param.4) | copy-start | bytes 786436
  5.3 18.5 %copy-start = (bf16[256,512]{1,0:T(8,128)(2,1)S(1)}, bf16[256,512]{1,0:T(8,128)(2,1)}, u32[]{:S(2)}) copy-start(bf16[256,512]{1,0:T(8,128)(2,1)} %param.5) | copy-start | bytes 786436
  7.0 16.9 %copy-start.1 = (bf16[256,512]{1,0:T(8,128)(2,1)S(1)}, bf16[256,512]{1,0:T(8,128)(2,1)}, u32[]{:S(2)}) copy-start(bf16[256,512]{1,0:T(8,128)(2,1)} %param.6) | copy-start | bytes 786436
  7.0 17.0 %copy-start.3 = (bf16[256,512]{1,0:T(8,128)(2,1)S(1)}, bf16[256,512]{1,0:T(8,128)(2,1)}, u32[]{:S(2)}) copy-start(bf16[256,512]{1,0:T(8,128)(2,1)} %param.7) | copy-start | bytes 786436
  7.0 45.9 %all-to-all-start = ((bf16[128,32,128]{2,1,0:T(8,128)(2,1)}), bf16[128,32,128]{2,1,0:T(8,128)(2,1)S(1)}, u32[]{:S(2)}, u32[]{:S(2)}) async-start(bf16[128,32,128]{2,1,0:T(8,128)(2,1)} %copy.241), calls=%async_computation | async-start | bytes 2097152 | tf_op jit(solution)/shard_map/all_to_all | solution.py:167
  24.3 41.7 %copy-start.9 = (bf16[2,128,1,2,128]{1,4,3,0,2:T(8,128)(2,1)}, bf16[2,128,1,2,128]{1,4,3,0,2:T(8,128)(2,1)S(1)}, u32[]{:S(2)}) copy-start(bf16[2,128,1,2,128]{1,4,3,0,2:T(8,128)(2,1)S(1)} %copy.339) | copy-start | bytes 393220
  24.9 41.1 %copy-start.11 = (bf16[2,128,1,2,128]{1,4,3,0,2:T(8,128)(2,1)}, bf16[2,128,1,2,128]{1,4,3,0,2:T(8,128)(2,1)S(1)}, u32[]{:S(2)}) copy-start(bf16[2,128,1,2,128]{1,4,3,0,2:T(8,128)(2,1)S(1)} %copy.335) | copy-start | bytes 393220
  52.9 4.8 %collective-permute-start = (bf16[128,16,128]{2,1,0:T(8,128)(2,1)S(1)}, bf16[128,16,128]{2,1,0:T(8,128)(2,1)S(1)}, u32[]{:S(2)}, u32[]{:S(2)}) collective-permute-start(bf16[128,16,128]{2,1,0:T(8,128)(2,1)S(1)} %slice.161), channel_id=1, source_target_pairs={{0,4},{4,0},{1,5},{5,1},{2,6},{6,2},{3,7},{7,3},{8,12},{12,8},{9,1... | collective-permute-start | bytes 1572872 | tf_op jit(solution)/shard_map/ppermute | solution.py:177
  56.5 9.5 %copy-start.6 = (f32[2,2,128,128]{2,3,1,0:T(8,128)}, f32[2,2,128,128]{2,3,1,0:T(8,128)S(1)}, u32[]{:S(2)}) copy-start(f32[2,2,128,128]{2,3,1,0:T(8,128)S(1)} %get-tuple-element.35) | copy-start | bytes 786436
  59.3 4.3 %copy-start.12 = (bf16[1,128,2,1,2,128]{5,2,1,4,3,0:T(2,128)(2,1)}, bf16[1,128,2,1,2,128]{5,2,1,4,3,0:T(2,128)(2,1)S(1)}, u32[]{:S(2)}) copy-start(bf16[1,128,2,1,2,128]{5,2,1,4,3,0:T(2,128)(2,1)S(1)} %copy.259) | copy-start | bytes 393220
  59.4 4.1 %copy-start.4 = (bf16[1,128,2,1,2,128]{5,2,1,4,3,0:T(2,128)(2,1)}, bf16[1,128,2,1,2,128]{5,2,1,4,3,0:T(2,128)(2,1)S(1)}, u32[]{:S(2)}) copy-start(bf16[1,128,2,1,2,128]{5,2,1,4,3,0:T(2,128)(2,1)S(1)} %copy.255) | copy-start | bytes 393220
  67.5 4.4 %copy-start.8 = (f32[256,1,2,128]{0,3,2,1:T(8,128)S(1)}, f32[256,1,2,128]{0,3,2,1:T(8,128)}, u32[]{:S(2)}) copy-start(f32[256,1,2,128]{0,3,2,1:T(8,128)} %copy.261) | copy-start | bytes 786436
  67.5 4.4 %copy-start.14 = (bf16[1,128,2,1,2,128]{5,2,1,4,3,0:T(2,128)(2,1)S(1)}, bf16[1,128,2,1,2,128]{5,2,1,4,3,0:T(2,128)(2,1)}, u32[]{:S(2)}) copy-start(bf16[1,128,2,1,2,128]{5,2,1,4,3,0:T(2,128)(2,1)} %copy.253) | copy-start | bytes 393220
  67.5 4.4 %copy-start.16 = (f32[2,256,256]{1,2,0:T(8,128)S(1)}, f32[2,256,256]{1,2,0:T(8,128)}, u32[]{:S(2)}) copy-start(f32[2,256,256]{1,2,0:T(8,128)} %get-tuple-element.41) | copy-start | bytes 1572868
  68.0 4.9 %copy-start.13 = (bf16[1,128,2,1,2,128]{5,2,1,4,3,0:T(2,128)(2,1)S(1)}, bf16[1,128,2,1,2,128]{5,2,1,4,3,0:T(2,128)(2,1)}, u32[]{:S(2)}) copy-start(bf16[1,128,2,1,2,128]{5,2,1,4,3,0:T(2,128)(2,1)} %copy-done.12) | copy-start | bytes 393220
  69.5 8.4 %collective-permute-start.1 = (bf16[128,16,128]{2,0,1:T(8,128)(2,1)}, bf16[128,16,128]{2,0,1:T(8,128)(2,1)}, u32[]{:S(2)}, u32[]{:S(2)}) collective-permute-start(bf16[128,16,128]{2,0,1:T(8,128)(2,1)} %copy.281), channel_id=1, source_target_pairs={{0,4},{4,0},{1,5},{5,1},{2,6},{6,2},{3,7},{7,3},{8,12},{12,8},{9,1... | collective-permute-start | bytes 1572872 | tf_op jit(solution)/shard_map/ppermute | solution.py:200
  72.0 1.1 copy-start.5
  81.1 6.7 %copy-start.10 = (bf16[2,128,1,2,128]{1,4,3,0,2:T(8,128)(2,1)S(1)}, bf16[2,128,1,2,128]{1,4,3,0,2:T(8,128)(2,1)}, u32[]{:S(2)}) copy-start(bf16[2,128,1,2,128]{1,4,3,0,2:T(8,128)(2,1)} %copy-done.9) | copy-start | bytes 393220
  81.1 35.5 %all-to-all-start.1 = ((bf16[128,32,128]{2,1,0:T(8,128)(2,1)}), bf16[128,32,128]{2,1,0:T(8,128)(2,1)S(1)}, u32[]{:S(2)}, u32[]{:S(2)}) async-start(bf16[128,32,128]{2,1,0:T(8,128)(2,1)} %copy.283), calls=%async_computation.1 | async-start | bytes 2097152 | tf_op jit(solution)/shard_map/all_to_all | solution.py:202
  87.8 1.9 %copy-start.7 = (f32[2,2,128,128]{2,3,1,0:T(8,128)S(1)}, f32[2,2,128,128]{2,3,1,0:T(8,128)}, u32[]{:S(2)}) copy-start(f32[2,2,128,128]{2,3,1,0:T(8,128)} %copy-done.6) | copy-start | bytes 786436
  117.9 2.1 %copy-start.15 = (bf16[2,128,2,128]{1,3,2,0:T(8,128)(2,1)S(1)}, bf16[2,128,2,128]{1,3,2,0:T(8,128)(2,1)}, u32[]{:S(2)}) copy-start(bf16[2,128,2,128]{1,3,2,0:T(8,128)(2,1)} %get-tuple-element.39) | copy-start | bytes 393220

commit v11 on v9

--- a/solution.py
+++ b/solution.py
@@ -1,8 +1,11 @@
+import functools
 import math
 
 import jax
 import jax.numpy as jnp
 from jax import lax
+from jax.experimental import pallas as pl
+from jax.experimental.pallas import tpu as pltpu
 from jax.sharding import Mesh, PartitionSpec as P
 
 HD = 128
@@ -96,39 +99,51 @@
     return (attended, query_grad, key_grad, value_grad, jnp.stack([key_terms, value_terms]))
 
 
-def strided_heads(query_all, keys_all, values_all, grads_all, scaling):
-    blocks = query_all.shape[0]
-    causal = (jnp.arange(blocks)[:, None] >= jnp.arange(blocks)[None, :])[None, None]
-    scores = (
-        jnp.einsum("brgd,crgd->rgbc", query_all, keys_all, preferred_element_type=jnp.float32)
-        * scaling
-    )
-    scores = jnp.where(causal, scores, -jnp.inf)
-    row_max = jnp.max(scores, axis=-1, keepdims=True)
-    raised = jnp.exp(scores - row_max)
-    weights = raised / jnp.sum(raised, axis=-1, keepdims=True)
-    weights_low = weights.astype(jnp.bfloat16)
-    attended = jnp.einsum(
-        "rgbc,crgd->brgd", weights_low, values_all, preferred_element_type=jnp.float32
-    ).astype(jnp.bfloat16)
-    dweights = jnp.einsum(
-        "brgd,crgd->rgbc", grads_all, values_all, preferred_element_type=jnp.float32
-    )
-    row_delta = jnp.sum(grads_all.astype(jnp.float32) * attended.astype(jnp.float32), axis=-1)
-    row_delta = jnp.transpose(row_delta, (1, 2, 0))[..., None]
-    dscores = (weights * (dweights - row_delta)).astype(jnp.bfloat16)
-    query_grad = (
-        jnp.einsum("rgbc,crgd->brgd", dscores, keys_all, preferred_element_type=jnp.float32)
-        * scaling
-    ).astype(jnp.bfloat16)
-    key_grad = (
-        jnp.einsum("rgbc,brgd->crgd", dscores, query_all, preferred_element_type=jnp.float32)
-        * scaling
-    ).astype(jnp.bfloat16)
-    value_grad = jnp.einsum(
-        "rgbc,brgd->crgd", weights_low, grads_all, preferred_element_type=jnp.float32
-    ).astype(jnp.bfloat16)
-    return jnp.stack([attended, query_grad, key_grad, value_grad])
+def product(left, right, left_dim, right_dim):
+    return lax.dot_general(
+        left, right, (((left_dim,), (right_dim,)), ((), ())), preferred_element_type=jnp.float32
+    )
+
+
+def strided_kernel(rows_ref, out_ref, *, scaling):
+    _, half_heads, blocks, _ = rows_ref.shape
+    causal = lax.broadcasted_iota(jnp.int32, (blocks, blocks), 0) >= lax.broadcasted_iota(
+        jnp.int32, (blocks, blocks), 1
+    )
+    for head in range(half_heads):
+        query = rows_ref[0, head]
+        key_rows = rows_ref[1, head]
+        value_rows = rows_ref[2, head]
+        grad_rows = rows_ref[3, head]
+        scores = jnp.where(causal, product(query, key_rows, 1, 1) * scaling, -jnp.inf)
+        raised = jnp.exp(scores - jnp.max(scores, axis=1, keepdims=True))
+        weights = raised / jnp.sum(raised, axis=1, keepdims=True)
+        weights_low = weights.astype(jnp.bfloat16)
+        attended = product(weights_low, value_rows, 1, 0).astype(jnp.bfloat16)
+        row_delta = jnp.sum(
+            grad_rows.astype(jnp.float32) * attended.astype(jnp.float32), axis=1, keepdims=True
+        )
+        dscores = (weights * (product(grad_rows, value_rows, 1, 1) - row_delta)).astype(
+            jnp.bfloat16
+        )
+        out_ref[0, head] = attended
+        out_ref[1, head] = (product(dscores, key_rows, 1, 0) * scaling).astype(jnp.bfloat16)
+        out_ref[2, head] = (product(dscores, query, 0, 0) * scaling).astype(jnp.bfloat16)
+        out_ref[3, head] = product(weights_low, grad_rows, 0, 0).astype(jnp.bfloat16)
+
+
+def strided_heads(gathered, scaling):
+    arrays, blocks, residues, half_heads, head_dim = gathered.shape
+    rows = gathered.transpose(0, 2, 3, 1, 4).reshape(arrays, residues * half_heads, blocks, head_dim)
+    vmem = pl.BlockSpec(memory_space=pltpu.VMEM)
+    out = pl.pallas_call(
+        functools.partial(strided_kernel, scaling=scaling),
+        out_shape=jax.ShapeDtypeStruct(rows.shape, jnp.bfloat16),
+        in_specs=[vmem],
+        out_specs=vmem,
+    )(rows)
+    out = out.reshape(arrays, residues, half_heads, blocks, head_dim)
+    return out.transpose(0, 3, 1, 2, 4)
 
 
 def shards(queries, keys, values, out_grad):
@@ -177,7 +192,7 @@
         scaling,
         lax.axis_index("ctx_chip") * 2 + core,
     )
-    strided_out = strided_heads(gathered[0], gathered[1], gathered[2], gathered[3], scaling)
+    strided_out = strided_heads(gathered, scaling)
 
     strided_out = strided_out.reshape(4, peers, -1, head_dim).transpose(1, 0, 2, 3)
     strided_out = strided_out.reshape(peers, -1, head_dim)

time: 121 us -> 117 us (0.967)
  Pallas kernels: 0 us -> 3.43 us
  other arithmetic: 5.62 us -> 3.14 us
  matrix products: 8.74 us -> 6.35 us
  waiting for transfers between devices: 56.3 us -> 54.4 us
    convert_element_type x5 -> x0, local copies, waits for them, and re-layouts: 3.53 us -> none  [the longest x1 1.02 us: strided_heads(): attended = jnp.einsum('rgbc,crgd->brgd', weights_low, values_all, preferr...]
    pallas_call x0 -> x1, Pallas kernels: none -> 3.43 us  [strided_heads(): pl.pallas_call(functools.partial(strided_kernel, scaling=scaling), out_sh...]
    transpose x0 -> x2, local copies, waits for them, and re-layouts: none -> 2.93 us  [the longest x1 1.58 us: strided_heads(): return out.transpose(0, 3, 1, 2, 4)]
    dot_general x5 -> x0, matrix products: 2.71 us -> none  [the longest x1 1.13 us: strided_heads(): jnp.einsum('rgbc,brgd->crgd', dscores, query_all, preferred_element_type=...]
    transpose x1 -> x0, other arithmetic: 1.38 us -> none  [shards(): strided_out.reshape(4, peers, -1, head_dim).transpose(1, 0, 2, 3)]
    unnamed x41 -> x28, local copies, waits for them, and re-layouts: 3.33 us -> 4.29 us
  transfers between devices with their start and end apart: 4 -> 4, of which waited for: 3 -> 3; matrix products, arithmetic and copies ran while one was open for 8% -> 8% of each run, Pallas kernels for 0% -> 3%
where the time goes in v11:
time: 117 us; the launch traced here: 116 us
  waiting for transfers between devices  54.4 us (46%)
  starting transfers between devices  28.6 us (24%)
  local copies, waits for them, and re-layouts  19.2 us (16%)
  matrix products  6.35 us (5%)
  Pallas kernels  3.43 us (3%)
  other arithmetic  3.14 us (3%)
  between operations  1.21 us (1%)
    all_to_all x1, waiting for transfers between devices, shards(): lax.all_to_all(jnp.concatenate([strided_rows, summary_rows], axis=1), CTX...  27.6 us
    all_to_all x1, waiting for transfers between devices, shards(): lax.all_to_all(jnp.concatenate([strided_out, terms], axis=1), CTX, 0, 0,...  26.3 us
    all_to_all x1, starting transfers between devices, shards(): lax.all_to_all(jnp.concatenate([strided_rows, summary_rows], axis=1), CTX...  16.6 us
    all_to_all x1, starting transfers between devices, shards(): lax.all_to_all(jnp.concatenate([strided_out, terms], axis=1), CTX, 0, 0,...  6.3 us
    unnamed x28, local copies, waits for them, and re-layouts  4.29 us
    pallas_call x1, Pallas kernels, strided_heads(): pl.pallas_call(functools.partial(strided_kernel, scaling=scaling), out_sh...  3.43 us
    ppermute x1, starting transfers between devices, shards(): sibling = lax.ppermute(mine, 'ctx_core', swap)  3.23 us
    ppermute x1, starting transfers between devices, shards(): lax.ppermute(give, 'ctx_core', swap).astype(jnp.float32)  2.45 us
  transfers between devices with their start and end apart: 4, of which 3 were waited for; matrix products, arithmetic and copies ran while one was open for 8% of the time, Pallas kernels for 3%

profile of v11, /device:TPU:1, one launch (start us, length us, event | category | flops | bytes accessed | tf_op | source)
XLA Modules:
  0.0 116.3 jit_solution(11397668667857993093)
XLA Ops:
  0.7 1.1 reshape.250
  1.7 1.0 reshape.252
  2.7 0.4 slice_bitcast_fusion.6
  3.3 0.4 slice_bitcast_fusion.5
  3.7 1.0 maximum_bitcast_fusion
  5.2 0.3 broadcast_in_dim.45
  5.5 1.6 %copy.169 = bf16[128,32,128]{2,1,0:T(8,128)(2,1)} copy(bf16[128,32,128]{2,0,1:T(8,128)(2,1)S(1)} %pad_maximum_fusion) | data formatting | bytes 2097152 | tf_op jit(solution)/shard_map/concatenate | solution.py:171
  7.2 16.6 %all-to-all-start = ((bf16[128,32,128]{2,1,0:T(8,128)(2,1)}), bf16[128,32,128]{2,1,0:T(8,128)(2,1)S(1)}, u32[]{:S(2)}, u32[]{:S(2)}) async-start(bf16[128,32,128]{2,1,0:T(8,128)(2,1)} %copy.169), calls=%async_computation | async-start | bytes 2097152 | tf_op jit(solution)/shard_map/all_to_all | solution.py:170
  23.8 0.8 copy.242
  24.6 0.8 copy.246
  25.4 27.6 %all-to-all-done = bf16[128,32,128]{2,1,0:T(8,128)(2,1)S(1)} async-done(((bf16[128,32,128]{2,1,0:T(8,128)(2,1)}), bf16[128,32,128]{2,1,0:T(8,128)(2,1)S(1)}, u32[]{:S(2)}, u32[]{:S(2)}) %all-to-all-start) | async-done | bytes 1048608 | tf_op jit(solution)/shard_map/all_to_all | solution.py:170
  53.0 3.2 %collective-permute-start = (bf16[128,16,128]{2,1,0:T(8,128)(2,1)S(1)}, bf16[128,16,128]{2,1,0:T(8,128)(2,1)S(1)}, u32[]{:S(2)}, u32[]{:S(2)}) collective-permute-start(bf16[128,16,128]{2,1,0:T(8,128)(2,1)S(1)} %slice.119), channel_id=1, source_target_pairs={{0,4},{4,0},{1,5},{5,1},{2,6},{6,2},{3,7},{7,3},{8,12},{12,8},{9,1... | collective-permute-start | bytes 1572872 | tf_op jit(solution)/shard_map/ppermute | solution.py:180
  56.4 0.9 fusion.52
  57.3 0.5 collective-permute-done
  57.9 0.4 copy.177
  58.3 0.5 fusion.53
  58.9 0.3 fusion.3
  59.2 0.3 fusion.20
  59.6 0.3 convolution_bitcast_fusion.6
  60.1 0.4 fusion.5
  60.6 0.9 multiply_reduce_fusion
  61.4 0.6 fusion.1
  62.1 0.4 select_bitcast_fusion
  62.5 0.5 copy.190
  63.2 2.5 %collective-permute-start.1 = (bf16[128,16,128]{2,0,1:T(8,128)(2,1)S(1)}, bf16[128,16,128]{2,0,1:T(8,128)(2,1)S(1)}, u32[]{:S(2)}, u32[]{:S(2)}) collective-permute-start(bf16[128,16,128]{2,0,1:T(8,128)(2,1)S(1)} %copy.191), channel_id=1, source_target_pairs={{0,4},{4,0},{1,5},{5,1},{2,6},{6,2},{3,7},{7,3},{8,12},{12,8},{9,1... | collective-permute-start | bytes 1572872 | tf_op jit(solution)/shard_map/ppermute | solution.py:203
  65.8 1.3 %copy.180 = bf16[4,128,2,1,2,128]{5,2,1,4,0,3:T(2,128)(2,1)} copy(bf16[4,128,2,1,2,128]{5,1,4,2,0,3:T(8,128)(2,1)S(1)} %bitcast.199) | data formatting | bytes 1048576 | tf_op jit(solution)/shard_map/transpose | solution.py:176
  67.2 3.4 %shard_map.75 = bf16[4,2,256,128]{3,2,1,0:T(8,128)(2,1)} custom-call(bf16[4,2,256,128]{3,2,1,0:T(8,128)(2,1)} %bitcast.200), custom_call_target="tpu_custom_call" | custom-call | tf_op jit(solution)/shard_map/pallas_call | solution.py:139
  70.6 1.6 %copy.181 = bf16[4,256,1,2,128]{4,3,1,0,2:T(2,128)(2,1)S(1)} copy(bf16[4,256,1,2,128]{4,1,3,0,2:T(8,128)(2,1)} %bitcast.201) | data formatting | bytes 1048576 | tf_op jit(solution)/shard_map/transpose | solution.py:146
  72.3 0.8 copy.189
  73.1 0.4 fusion.19
  73.6 1.7 %copy.193 = bf16[128,32,128]{2,1,0:T(8,128)(2,1)} copy(bf16[128,32,128]{2,0,1:T(8,128)(2,1)S(1)} %pad_maximum_fusion.1) | data formatting | bytes 2097152 | tf_op jit(solution)/shard_map/concatenate | solution.py:206
  75.4 6.3 %all-to-all-start.1 = ((bf16[128,32,128]{2,1,0:T(8,128)(2,1)}), bf16[128,32,128]{2,1,0:T(8,128)(2,1)S(1)}, u32[]{:S(2)}, u32[]{:S(2)}) async-start(bf16[128,32,128]{2,1,0:T(8,128)(2,1)} %copy.193), calls=%async_computation.1 | async-start | bytes 2097152 | tf_op jit(solution)/shard_map/all_to_all | solution.py:205
  81.7 0.4 copy.201
  82.1 1.3 %fusion.15 = bf16[2,2,128,128]{2,3,1,0:T(8,128)(2,1)S(1)} fusion(bf16[2,128,1,2,128]{1,4,3,0,2:T(8,128)(2,1)} %copy.242, f32[2,2,128]{2,1,0:T(2,128)S(1)} %bitcast.227, f32[2,2,128]{2,1,0:T(2,128)S(1)} %copy_add_fusion.1, f32[2,2,128,128]{2,3,1,0:T(8,128)} %get-tuple-element.26, f32[2,2,128]{2,1,0:T(2,128)S(1)} %copy_maximum_fusion, ...), kind=kOutput, calls=%fused_computation.28 | convolution fusion | flops 17104896 | bytes 661504 | tf_op jit(solution)/shard_map/bqgd,bkgd->bgqk/dot_general | solution.py:69
  83.4 0.3 convolution_bitcast_fusion.5
  83.7 0.2 fusion.16
  84.0 0.2 convolution_bitcast_fusion.3
  84.3 0.2 fusion.7
  84.5 26.3 %all-to-all-done.1 = bf16[128,32,128]{2,1,0:T(8,128)(2,1)S(1)} async-done(((bf16[128,32,128]{2,1,0:T(8,128)(2,1)}), bf16[128,32,128]{2,1,0:T(8,128)(2,1)S(1)}, u32[]{:S(2)}, u32[]{:S(2)}) %all-to-all-start.1) | async-done | bytes 1048608 | tf_op jit(solution)/shard_map/all_to_all | solution.py:205
  111.7 0.5 copy.194
  112.4 0.2 copy.211
  112.6 0.7 copy.292
  113.4 0.2 copy.207
  113.6 0.7 copy.293
  114.4 0.2 copy.203
  114.6 0.7 copy.294
  115.4 0.2 copy.195
  115.6 0.7 copy.295
  (63 shorter events, 3.0 us)
Async XLA Ops:
  0.6 2.6 %copy-start.3 = (bf16[256,512]{1,0:T(8,128)(2,1)S(1)}, bf16[256,512]{1,0:T(8,128)(2,1)}, u32[]{:S(2)}) copy-start(bf16[256,512]{1,0:T(8,128)(2,1)} %param.6) | copy-start | bytes 786436
  0.6 2.6 %copy-start.4 = (bf16[256,512]{1,0:T(8,128)(2,1)S(1)}, bf16[256,512]{1,0:T(8,128)(2,1)}, u32[]{:S(2)}) copy-start(bf16[256,512]{1,0:T(8,128)(2,1)} %param.7) | copy-start | bytes 786436
  7.2 45.8 %all-to-all-start = ((bf16[128,32,128]{2,1,0:T(8,128)(2,1)}), bf16[128,32,128]{2,1,0:T(8,128)(2,1)S(1)}, u32[]{:S(2)}, u32[]{:S(2)}) async-start(bf16[128,32,128]{2,1,0:T(8,128)(2,1)} %copy.169), calls=%async_computation | async-start | bytes 2097152 | tf_op jit(solution)/shard_map/all_to_all | solution.py:170
  53.0 4.8 %collective-permute-start = (bf16[128,16,128]{2,1,0:T(8,128)(2,1)S(1)}, bf16[128,16,128]{2,1,0:T(8,128)(2,1)S(1)}, u32[]{:S(2)}, u32[]{:S(2)}) collective-permute-start(bf16[128,16,128]{2,1,0:T(8,128)(2,1)S(1)} %slice.119), channel_id=1, source_target_pairs={{0,4},{4,0},{1,5},{5,1},{2,6},{6,2},{3,7},{7,3},{8,12},{12,8},{9,1... | collective-permute-start | bytes 1572872 | tf_op jit(solution)/shard_map/ppermute | solution.py:180
  57.9 1.0 copy-start.5
  59.2 0.9 copy-start.2
  59.6 1.0 copy-start.7
  62.1 1.0 copy-start
  63.2 9.9 %collective-permute-start.1 = (bf16[128,16,128]{2,0,1:T(8,128)(2,1)S(1)}, bf16[128,16,128]{2,0,1:T(8,128)(2,1)S(1)}, u32[]{:S(2)}, u32[]{:S(2)}) collective-permute-start(bf16[128,16,128]{2,0,1:T(8,128)(2,1)S(1)} %copy.191), channel_id=1, source_target_pairs={{0,4},{4,0},{1,5},{5,1},{2,6},{6,2},{3,7},{7,3},{8,12},{12,8},{9,1... | collective-permute-start | bytes 1572872 | tf_op jit(solution)/shard_map/ppermute | solution.py:203
  75.4 8.1 %copy-start.1 = (bf16[2,2,128,1024]{2,3,0,1:T(8,128)(2,1)S(1)}, bf16[2,2,128,1024]{2,3,0,1:T(8,128)(2,1)}, u32[]{:S(2)}) copy-start(bf16[2,2,128,1024]{2,3,0,1:T(8,128)(2,1)} %copy-done) | copy-start | bytes 3145732
  75.4 35.5 %all-to-all-start.1 = ((bf16[128,32,128]{2,1,0:T(8,128)(2,1)}), bf16[128,32,128]{2,1,0:T(8,128)(2,1)S(1)}, u32[]{:S(2)}, u32[]{:S(2)}) async-start(bf16[128,32,128]{2,1,0:T(8,128)(2,1)} %copy.193), calls=%async_computation.1 | async-start | bytes 2097152 | tf_op jit(solution)/shard_map/all_to_all | solution.py:205
  82.1 1.9 %copy-start.6 = (f32[2,2,128,128]{2,3,1,0:T(8,128)S(1)}, f32[2,2,128,128]{2,3,1,0:T(8,128)}, u32[]{:S(2)}) copy-start(f32[2,2,128,128]{2,3,1,0:T(8,128)} %get-tuple-element.26) | copy-start | bytes 786436
  82.1 1.9 %copy-start.8 = (bf16[2,128,1,2,128]{1,4,3,0,2:T(8,128)(2,1)S(1)}, bf16[2,128,1,2,128]{1,4,3,0,2:T(8,128)(2,1)}, u32[]{:S(2)}) copy-start(bf16[2,128,1,2,128]{1,4,3,0,2:T(8,128)(2,1)} %copy.242) | copy-start | bytes 393220
  112.4 3.0 %copy-start.9 = (bf16[2,128,2,128]{1,3,2,0:T(8,128)(2,1)S(1)}, bf16[2,128,2,128]{1,3,2,0:T(8,128)(2,1)}, u32[]{:S(2)}) copy-start(bf16[2,128,2,128]{1,3,2,0:T(8,128)(2,1)} %get-tuple-element.30) | copy-start | bytes 393220

commit v12 on v11

--- a/solution.py
+++ b/solution.py
@@ -105,16 +105,32 @@
     )
 
 
-def strided_kernel(rows_ref, out_ref, *, scaling):
-    _, half_heads, blocks, _ = rows_ref.shape
-    causal = lax.broadcasted_iota(jnp.int32, (blocks, blocks), 0) >= lax.broadcasted_iota(
-        jnp.int32, (blocks, blocks), 1
-    )
+def strided_kernel(rows_ref, out_ref, *, scaling, arrays, half_heads):
+    width = arrays * 2 * half_heads
+    peers = rows_ref.shape[0] // width
+    blocks = 2 * peers
+    order = lambda dim: 2 * (lax.broadcasted_iota(jnp.int32, (blocks, blocks), dim) % peers) + (
+        lax.broadcasted_iota(jnp.int32, (blocks, blocks), dim) // peers
+    )
+    causal = order(0) >= order(1)
+
+    def load(array, head):
+        return jnp.concatenate(
+            [
+                rows_ref[pl.ds((array * 2 + block) * half_heads + head, peers, stride=width), :]
+                for block in range(2)
+            ],
+            axis=0,
+        )
+
+    def store(array, head, value):
+        out_ref[array, head] = value
+
     for head in range(half_heads):
-        query = rows_ref[0, head]
-        key_rows = rows_ref[1, head]
-        value_rows = rows_ref[2, head]
-        grad_rows = rows_ref[3, head]
+        query = load(0, head)
+        key_rows = load(1, head)
+        value_rows = load(2, head)
+        grad_rows = load(3, head)
         scores = jnp.where(causal, product(query, key_rows, 1, 1) * scaling, -jnp.inf)
         raised = jnp.exp(scores - jnp.max(scores, axis=1, keepdims=True))
         weights = raised / jnp.sum(raised, axis=1, keepdims=True)
@@ -126,24 +142,23 @@
         dscores = (weights * (product(grad_rows, value_rows, 1, 1) - row_delta)).astype(
             jnp.bfloat16
         )
-        out_ref[0, head] = attended
-        out_ref[1, head] = (product(dscores, key_rows, 1, 0) * scaling).astype(jnp.bfloat16)
-        out_ref[2, head] = (product(dscores, query, 0, 0) * scaling).astype(jnp.bfloat16)
-        out_ref[3, head] = product(weights_low, grad_rows, 0, 0).astype(jnp.bfloat16)
-
-
-def strided_heads(gathered, scaling):
-    arrays, blocks, residues, half_heads, head_dim = gathered.shape
-    rows = gathered.transpose(0, 2, 3, 1, 4).reshape(arrays, residues * half_heads, blocks, head_dim)
+        store(0, head, attended)
+        store(1, head, (product(dscores, key_rows, 1, 0) * scaling).astype(jnp.bfloat16))
+        store(2, head, (product(dscores, query, 0, 0) * scaling).astype(jnp.bfloat16))
+        store(3, head, product(weights_low, grad_rows, 0, 0).astype(jnp.bfloat16))
+
+
+def strided_heads(rows, scaling, half_heads):
+    peers, width, head_dim = rows.shape
     vmem = pl.BlockSpec(memory_space=pltpu.VMEM)
     out = pl.pallas_call(
-        functools.partial(strided_kernel, scaling=scaling),
-        out_shape=jax.ShapeDtypeStruct(rows.shape, jnp.bfloat16),
+        functools.partial(strided_kernel, scaling=scaling, arrays=4, half_heads=half_heads),
+        out_shape=jax.ShapeDtypeStruct((4, half_heads, 2 * peers, head_dim), jnp.bfloat16),
         in_specs=[vmem],
         out_specs=vmem,
-    )(rows)
-    out = out.reshape(arrays, residues, half_heads, blocks, head_dim)
-    return out.transpose(0, 3, 1, 2, 4)
+    )(rows.reshape(peers * width, head_dim))
+    out = out.reshape(4, half_heads, 2, peers, head_dim).transpose(3, 0, 2, 1, 4)
+    return out.reshape(peers, width, head_dim)
 
 
 def shards(queries, keys, values, out_grad):
@@ -170,12 +185,6 @@
     received = lax.all_to_all(
         jnp.concatenate([strided_rows, summary_rows], axis=1), CTX, 0, 0, tiled=True
     )
-    gathered = received[:, :strided_size].reshape(
-        peers, 4, blocks_here, residues, half_heads, head_dim
-    )
-    gathered = gathered.transpose(1, 0, 2, 3, 4, 5).reshape(
-        4, peers * blocks_here, residues, half_heads, head_dim
-    )
     mine = received[:, strided_size:]
     sibling = lax.ppermute(mine, "ctx_core", swap)
     summary_shape = (peers * blocks_here * SUMMARY, half_heads, head_dim)
@@ -192,10 +201,8 @@
         scaling,
         lax.axis_index("ctx_chip") * 2 + core,
     )
-    strided_out = strided_heads(gathered, scaling)
-
-    strided_out = strided_out.reshape(4, peers, -1, head_dim).transpose(1, 0, 2, 3)
-    strided_out = strided_out.reshape(peers, -1, head_dim)
+    strided_out = strided_heads(received[:, :strided_size], scaling, half_heads)
+
     terms = terms.astype(jnp.bfloat16).reshape(2, peers, -1, head_dim)
     keep = jnp.where(core == 0, terms[0], terms[1])
     give = jnp.where(core == 0, terms[1], terms[0])

time: 117 us -> 116 us (level)
  local copies, waits for them, and re-layouts: 19.2 us -> 15.5 us
  waiting for transfers between devices: 54.4 us -> 56.3 us
  other arithmetic: 3.14 us -> 5 us
    transpose x3 -> x0, local copies, waits for them, and re-layouts: 3.03 us -> none  [the longest x1 1.58 us: strided_heads(): return out.transpose(0, 3, 1, 2, 4)]
    all_to_all x1, waiting for transfers between devices: 27.6 us -> 28.8 us  [shards(): lax.all_to_all(jnp.concatenate([strided_rows, summary_rows], axis=1), CTX...]
    unnamed x28 -> x21, local copies, waits for them, and re-layouts: 4.29 us -> 3.29 us
  transfers between devices with their start and end apart: 4 -> 4, of which waited for: 3 -> 3; matrix products, arithmetic and copies ran while one was open for 8% -> 5% of each run, Pallas kernels for 3% -> 3%
where the time goes in v12:
time: 116 us
  waiting for transfers between devices  56.3 us (49%)
  starting transfers between devices  28.5 us (25%)
  local copies, waits for them, and re-layouts  15.5 us (13%)
  matrix products  5.68 us (5%)
  other arithmetic  5 us (4%)
  Pallas kernels  3.44 us (3%)
  between operations  1.2 us (1%)
    all_to_all x1, waiting for transfers between devices, shards(): lax.all_to_all(jnp.concatenate([strided_rows, summary_rows], axis=1), CTX...  28.8 us
    all_to_all x1, waiting for transfers between devices, shards(): lax.all_to_all(jnp.concatenate([strided_out, terms], axis=1), CTX, 0, 0,...  26.3 us
    all_to_all x1, starting transfers between devices, shards(): lax.all_to_all(jnp.concatenate([strided_rows, summary_rows], axis=1), CTX...  16.6 us
    all_to_all x1, starting transfers between devices, shards(): lax.all_to_all(jnp.concatenate([strided_out, terms], axis=1), CTX, 0, 0,...  6.16 us
    pallas_call x1, Pallas kernels, strided_heads(): pl.pallas_call(functools.partial(strided_kernel, scaling=scaling, arrays=...  3.44 us
    unnamed x21, local copies, waits for them, and re-layouts  3.29 us
    ppermute x1, starting transfers between devices, shards(): sibling = lax.ppermute(mine, 'ctx_core', swap)  3.23 us
    ppermute x1, starting transfers between devices, shards(): lax.ppermute(give, 'ctx_core', swap).astype(jnp.float32)  2.46 us
  transfers between devices with their start and end apart: 4, of which 3 were waited for; matrix products, arithmetic and copies ran while one was open for 5% of the time, Pallas kernels for 3%

profile of v12, /device:TPU:1, one launch (start us, length us, event | category | flops | bytes accessed | tf_op | source)
XLA Modules:
  0.0 115.7 jit_solution(17944348310146127547)
XLA Ops:
  0.7 1.1 reshape.241
  1.7 1.0 reshape.243
  2.7 0.4 slice_bitcast_fusion.6
  3.3 0.4 slice_bitcast_fusion.5
  3.7 1.0 maximum_bitcast_fusion
  5.2 0.3 broadcast_in_dim.45
  5.5 1.7 %copy.166 = bf16[128,32,128]{2,1,0:T(8,128)(2,1)} copy(bf16[128,32,128]{2,0,1:T(8,128)(2,1)S(1)} %pad_maximum_fusion) | data formatting | bytes 2097152 | tf_op jit(solution)/shard_map/concatenate | solution.py:186
  7.2 16.6 %all-to-all-start = ((bf16[128,32,128]{2,1,0:T(8,128)(2,1)}), bf16[128,32,128]{2,1,0:T(8,128)(2,1)S(1)}, u32[]{:S(2)}, u32[]{:S(2)}) async-start(bf16[128,32,128]{2,1,0:T(8,128)(2,1)} %copy.166), calls=%async_computation | async-start | bytes 2097152 | tf_op jit(solution)/shard_map/all_to_all | solution.py:185
  24.2 28.8 %all-to-all-done = bf16[128,32,128]{2,1,0:T(8,128)(2,1)S(1)} async-done(((bf16[128,32,128]{2,1,0:T(8,128)(2,1)}), bf16[128,32,128]{2,1,0:T(8,128)(2,1)S(1)}, u32[]{:S(2)}, u32[]{:S(2)}) %all-to-all-start) | async-done | bytes 1048608 | tf_op jit(solution)/shard_map/all_to_all | solution.py:185
  53.0 3.2 %collective-permute-start = (bf16[128,16,128]{2,1,0:T(8,128)(2,1)S(1)}, bf16[128,16,128]{2,1,0:T(8,128)(2,1)S(1)}, u32[]{:S(2)}, u32[]{:S(2)}) collective-permute-start(bf16[128,16,128]{2,1,0:T(8,128)(2,1)S(1)} %slice.119), channel_id=1, source_target_pairs={{0,4},{4,0},{1,5},{5,1},{2,6},{6,2},{3,7},{7,3},{8,12},{12,8},{9,1... | collective-permute-start | bytes 1572872 | tf_op jit(solution)/shard_map/ppermute | solution.py:189
  56.4 0.2 fusion.52
  56.6 1.2 %collective-permute-done = bf16[128,16,128]{2,1,0:T(8,128)(2,1)S(1)} collective-permute-done((bf16[128,16,128]{2,1,0:T(8,128)(2,1)S(1)}, bf16[128,16,128]{2,1,0:T(8,128)(2,1)S(1)}, u32[]{:S(2)}, u32[]{:S(2)}) %collective-permute-start) | collective-permute-done | bytes 524320 | tf_op jit(solution)/shard_map/ppermute | solution.py:189
  57.8 0.9 broadcast_select_fusion
  58.7 0.4 copy.174
  59.1 0.5 fusion.53
  59.7 0.3 fusion.3
  60.0 0.3 fusion.20
  60.4 0.3 convolution_bitcast_fusion.6
  60.7 0.4 fusion.5
  61.2 0.9 multiply_reduce_fusion
  62.0 0.6 fusion.1
  62.7 0.5 select_bitcast_fusion
  63.1 0.5 copy.184
  63.8 2.5 %collective-permute-start.1 = (bf16[128,16,128]{2,0,1:T(8,128)(2,1)S(1)}, bf16[128,16,128]{2,0,1:T(8,128)(2,1)}, u32[]{:S(2)}, u32[]{:S(2)}) collective-permute-start(bf16[128,16,128]{2,0,1:T(8,128)(2,1)S(1)} %copy.185), channel_id=1, source_target_pairs={{0,4},{4,0},{1,5},{5,1},{2,6},{6,2},{3,7},{7,3},{8,12},{12,8},{9,1... | collective-permute-start | bytes 1572872 | tf_op jit(solution)/shard_map/ppermute | solution.py:210
  66.3 3.4 %shard_map.75 = bf16[4,2,256,128]{3,2,1,0:T(8,128)(2,1)} custom-call(bf16[2048,128]{1,0:T(8,128)(2,1)} %bitcast.192), custom_call_target="tpu_custom_call" | custom-call | tf_op jit(solution)/shard_map/pallas_call | solution.py:154
  69.7 1.1 copy.176
  70.8 0.8 copy.183
  71.6 1.5 %fusion.19 = bf16[128,16,128]{2,0,1:T(8,128)(2,1)S(1)} fusion(f32[128,16,128]{2,1,0:T(8,128)S(1)} %bitcast.186, bf16[128,16,128]{2,0,1:T(8,128)(2,1)} %collective-permute-done.1), kind=kLoop, calls=%fused_computation.36 | loop fusion | flops 786432 | bytes 2097152 | tf_op jit(solution)/shard_map/convert_element_type | solution.py:211
  73.2 1.7 %copy.187 = bf16[128,32,128]{2,1,0:T(8,128)(2,1)} copy(bf16[128,32,128]{2,0,1:T(8,128)(2,1)S(1)} %pad_maximum_fusion.1) | data formatting | bytes 2097152 | tf_op jit(solution)/shard_map/concatenate | solution.py:213
  74.9 6.2 %all-to-all-start.1 = ((bf16[128,32,128]{2,1,0:T(8,128)(2,1)}), bf16[128,32,128]{2,1,0:T(8,128)(2,1)S(1)}, u32[]{:S(2)}, u32[]{:S(2)}) async-start(bf16[128,32,128]{2,1,0:T(8,128)(2,1)} %copy.187), calls=%async_computation.1 | async-start | bytes 2097152 | tf_op jit(solution)/shard_map/all_to_all | solution.py:212
  81.0 0.4 copy.195
  81.5 1.3 %fusion.15 = bf16[2,2,128,128]{2,3,1,0:T(8,128)(2,1)S(1)} fusion(bf16[2,128,1,2,128]{1,4,3,0,2:T(8,128)(2,1)} %copy-done.4, f32[2,2,128]{2,1,0:T(2,128)S(1)} %bitcast.215, f32[2,2,128]{2,1,0:T(2,128)S(1)} %copy_add_fusion.1, f32[2,2,128,128]{2,3,1,0:T(8,128)} %copy-done.2, f32[2,2,128]{2,1,0:T(2,128)S(1)} %copy_maximum_fusion, ...), kind=kOutput, calls=%fused_computation.28 | convolution fusion | flops 17104896 | bytes 661504 | tf_op jit(solution)/shard_map/bqgd,bkgd->bgqk/dot_general | solution.py:69
  82.8 0.3 convolution_bitcast_fusion.5
  83.1 0.2 fusion.16
  83.4 0.2 convolution_bitcast_fusion.3
  83.6 0.2 fusion.7
  83.9 26.3 %all-to-all-done.1 = bf16[128,32,128]{2,1,0:T(8,128)(2,1)S(1)} async-done(((bf16[128,32,128]{2,1,0:T(8,128)(2,1)}), bf16[128,32,128]{2,1,0:T(8,128)(2,1)S(1)}, u32[]{:S(2)}, u32[]{:S(2)}) %all-to-all-start.1) | async-done | bytes 1048608 | tf_op jit(solution)/shard_map/all_to_all | solution.py:212
  110.2 0.2 fusion.49
  110.5 0.1 copy.200
  111.1 0.5 copy.188
  111.7 0.2 copy.205
  111.9 0.7 copy.285
  112.8 0.2 copy.201
  113.0 0.7 copy.286
  113.8 0.2 copy.197
  114.0 0.7 copy.287
  114.7 0.2 copy.189
  114.9 0.7 copy.288
  (54 shorter events, 2.4 us)
Async XLA Ops:
  0.6 2.6 %copy-start = (bf16[256,512]{1,0:T(8,128)(2,1)S(1)}, bf16[256,512]{1,0:T(8,128)(2,1)}, u32[]{:S(2)}) copy-start(bf16[256,512]{1,0:T(8,128)(2,1)} %param.6) | copy-start | bytes 786436
  0.6 2.6 %copy-start.1 = (bf16[256,512]{1,0:T(8,128)(2,1)S(1)}, bf16[256,512]{1,0:T(8,128)(2,1)}, u32[]{:S(2)}) copy-start(bf16[256,512]{1,0:T(8,128)(2,1)} %param.7) | copy-start | bytes 786436
  7.2 45.8 %all-to-all-start = ((bf16[128,32,128]{2,1,0:T(8,128)(2,1)}), bf16[128,32,128]{2,1,0:T(8,128)(2,1)S(1)}, u32[]{:S(2)}, u32[]{:S(2)}) async-start(bf16[128,32,128]{2,1,0:T(8,128)(2,1)} %copy.166), calls=%async_computation | async-start | bytes 2097152 | tf_op jit(solution)/shard_map/all_to_all | solution.py:185
  24.0 37.2 %copy-start.4 = (bf16[2,128,1,2,128]{1,4,3,0,2:T(8,128)(2,1)}, bf16[2,128,1,2,128]{1,4,3,0,2:T(8,128)(2,1)S(1)}, u32[]{:S(2)}) copy-start(bf16[2,128,1,2,128]{1,4,3,0,2:T(8,128)(2,1)S(1)} %copy.235) | copy-start | bytes 393220
  53.0 4.8 %collective-permute-start = (bf16[128,16,128]{2,1,0:T(8,128)(2,1)S(1)}, bf16[128,16,128]{2,1,0:T(8,128)(2,1)S(1)}, u32[]{:S(2)}, u32[]{:S(2)}) collective-permute-start(bf16[128,16,128]{2,1,0:T(8,128)(2,1)S(1)} %slice.119), channel_id=1, source_target_pairs={{0,4},{4,0},{1,5},{5,1},{2,6},{6,2},{3,7},{7,3},{8,12},{12,8},{9,1... | collective-permute-start | bytes 1572872 | tf_op jit(solution)/shard_map/ppermute | solution.py:189
  56.6 4.6 %copy-start.2 = (f32[2,2,128,128]{2,3,1,0:T(8,128)}, f32[2,2,128,128]{2,3,1,0:T(8,128)S(1)}, u32[]{:S(2)}) copy-start(f32[2,2,128,128]{2,3,1,0:T(8,128)S(1)} %get-tuple-element.26) | copy-start | bytes 786436
  63.8 7.8 %collective-permute-start.1 = (bf16[128,16,128]{2,0,1:T(8,128)(2,1)S(1)}, bf16[128,16,128]{2,0,1:T(8,128)(2,1)}, u32[]{:S(2)}, u32[]{:S(2)}) collective-permute-start(bf16[128,16,128]{2,0,1:T(8,128)(2,1)S(1)} %copy.185), channel_id=1, source_target_pairs={{0,4},{4,0},{1,5},{5,1},{2,6},{6,2},{3,7},{7,3},{8,12},{12,8},{9,1... | collective-permute-start | bytes 1572872 | tf_op jit(solution)/shard_map/ppermute | solution.py:210
  74.9 35.3 %all-to-all-start.1 = ((bf16[128,32,128]{2,1,0:T(8,128)(2,1)}), bf16[128,32,128]{2,1,0:T(8,128)(2,1)S(1)}, u32[]{:S(2)}, u32[]{:S(2)}) async-start(bf16[128,32,128]{2,1,0:T(8,128)(2,1)} %copy.187), calls=%async_computation.1 | async-start | bytes 2097152 | tf_op jit(solution)/shard_map/all_to_all | solution.py:212
  81.5 1.9 %copy-start.3 = (f32[2,2,128,128]{2,3,1,0:T(8,128)S(1)}, f32[2,2,128,128]{2,3,1,0:T(8,128)}, u32[]{:S(2)}) copy-start(f32[2,2,128,128]{2,3,1,0:T(8,128)} %copy-done.2) | copy-start | bytes 786436
  81.5 1.9 %copy-start.5 = (bf16[2,128,1,2,128]{1,4,3,0,2:T(8,128)(2,1)S(1)}, bf16[2,128,1,2,128]{1,4,3,0,2:T(8,128)(2,1)}, u32[]{:S(2)}) copy-start(bf16[2,128,1,2,128]{1,4,3,0,2:T(8,128)(2,1)} %copy-done.4) | copy-start | bytes 393220
  111.7 3.0 %copy-start.6 = (bf16[2,128,2,128]{1,3,2,0:T(8,128)(2,1)S(1)}, bf16[2,128,2,128]{1,3,2,0:T(8,128)(2,1)}, u32[]{:S(2)}) copy-start(bf16[2,128,2,128]{1,3,2,0:T(8,128)(2,1)} %get-tuple-element.30) | copy-start | bytes 393220

commit v13 on v12

--- a/solution.py
+++ b/solution.py
@@ -124,7 +124,11 @@
         )
 
     def store(array, head, value):
-        out_ref[array, head] = value
+        value = value.astype(jnp.float32)
+        for block in range(2):
+            out_ref[pl.ds((array * 2 + block) * half_heads + head, peers, stride=width), :] = value[
+                block * peers : (block + 1) * peers
+            ]
 
     for head in range(half_heads):
         query = load(0, head)
@@ -153,12 +157,11 @@
     vmem = pl.BlockSpec(memory_space=pltpu.VMEM)
     out = pl.pallas_call(
         functools.partial(strided_kernel, scaling=scaling, arrays=4, half_heads=half_heads),
-        out_shape=jax.ShapeDtypeStruct((4, half_heads, 2 * peers, head_dim), jnp.bfloat16),
+        out_shape=jax.ShapeDtypeStruct((peers * width, head_dim), jnp.float32),
         in_specs=[vmem],
         out_specs=vmem,
     )(rows.reshape(peers * width, head_dim))
-    out = out.reshape(4, half_heads, 2, peers, head_dim).transpose(3, 0, 2, 1, 4)
-    return out.reshape(peers, width, head_dim)
+    return out.reshape(peers, width, head_dim).astype(jnp.bfloat16)
 
 
 def shards(queries, keys, values, out_grad):

time: 116 us -> 116 us (level)
  local copies, waits for them, and re-layouts: 15.5 us -> 12.7 us
  other arithmetic: 5 us -> 6.95 us
    concatenate x1 -> x0, local copies, waits for them, and re-layouts: 1.65 us -> none  [shards(): jnp.concatenate([strided_out, terms], axis=1)]
    convert_element_type x0 -> x1, other arithmetic: none -> 1.28 us  [strided_heads(): return out.reshape(peers, width, head_dim).astype(jnp.bfloat16)]
where the time goes in v13:
time: 116 us; the launch traced here: 115 us
  waiting for transfers between devices  56.3 us (49%)
  starting transfers between devices  28.5 us (25%)
  local copies, waits for them, and re-layouts  12.7 us (11%)
  other arithmetic  6.95 us (6%)
  matrix products  5.67 us (5%)
  Pallas kernels  3.7 us (3%)
  between operations  1.19 us (1%)
    all_to_all x1, waiting for transfers between devices, shards(): lax.all_to_all(jnp.concatenate([strided_rows, summary_rows], axis=1), CTX...  28.8 us
    all_to_all x1, waiting for transfers between devices, shards(): lax.all_to_all(jnp.concatenate([strided_out, terms], axis=1), CTX, 0, 0,...  26.3 us
    all_to_all x1, starting transfers between devices, shards(): lax.all_to_all(jnp.concatenate([strided_rows, summary_rows], axis=1), CTX...  16.6 us
    all_to_all x1, starting transfers between devices, shards(): lax.all_to_all(jnp.concatenate([strided_out, terms], axis=1), CTX, 0, 0,...  6.16 us
    pallas_call x1, Pallas kernels, strided_heads(): pl.pallas_call(functools.partial(strided_kernel, scaling=scaling, arrays=...  3.7 us
    unnamed x21, local copies, waits for them, and re-layouts  3.29 us
    ppermute x1, starting transfers between devices, shards(): sibling = lax.ppermute(mine, 'ctx_core', swap)  3.23 us
    ppermute x1, starting transfers between devices, shards(): lax.ppermute(give, 'ctx_core', swap).astype(jnp.float32)  2.48 us
  transfers between devices with their start and end apart: 4, of which 3 were waited for; matrix products, arithmetic and copies ran while one was open for 5% of the time, Pallas kernels for 3%

profile of v13, /device:TPU:1, one launch (start us, length us, event | category | flops | bytes accessed | tf_op | source)
XLA Modules:
  0.0 115.0 jit_solution(5364785201727385055)
XLA Ops:
  0.7 1.1 reshape.237
  1.7 1.0 reshape.239
  2.7 0.4 slice_bitcast_fusion.6
  3.3 0.4 slice_bitcast_fusion.5
  3.7 1.0 maximum_bitcast_fusion
  5.2 0.3 broadcast_in_dim.45
  5.5 1.7 %copy.156 = bf16[128,32,128]{2,1,0:T(8,128)(2,1)} copy(bf16[128,32,128]{2,0,1:T(8,128)(2,1)S(1)} %pad_maximum_fusion) | data formatting | bytes 2097152 | tf_op jit(solution)/shard_map/concatenate | solution.py:189
  7.2 16.6 %all-to-all-start = ((bf16[128,32,128]{2,1,0:T(8,128)(2,1)}), bf16[128,32,128]{2,1,0:T(8,128)(2,1)S(1)}, u32[]{:S(2)}, u32[]{:S(2)}) async-start(bf16[128,32,128]{2,1,0:T(8,128)(2,1)} %copy.156), calls=%async_computation | async-start | bytes 2097152 | tf_op jit(solution)/shard_map/all_to_all | solution.py:188
  24.2 28.8 %all-to-all-done = bf16[128,32,128]{2,1,0:T(8,128)(2,1)S(1)} async-done(((bf16[128,32,128]{2,1,0:T(8,128)(2,1)}), bf16[128,32,128]{2,1,0:T(8,128)(2,1)S(1)}, u32[]{:S(2)}, u32[]{:S(2)}) %all-to-all-start) | async-done | bytes 1048608 | tf_op jit(solution)/shard_map/all_to_all | solution.py:188
  53.0 3.2 %collective-permute-start = (bf16[128,16,128]{2,1,0:T(8,128)(2,1)S(1)}, bf16[128,16,128]{2,1,0:T(8,128)(2,1)S(1)}, u32[]{:S(2)}, u32[]{:S(2)}) collective-permute-start(bf16[128,16,128]{2,1,0:T(8,128)(2,1)S(1)} %slice.119), channel_id=1, source_target_pairs={{0,4},{4,0},{1,5},{5,1},{2,6},{6,2},{3,7},{7,3},{8,12},{12,8},{9,1... | collective-permute-start | bytes 1572872 | tf_op jit(solution)/shard_map/ppermute | solution.py:192
  56.4 0.2 fusion.52
  56.6 1.2 %collective-permute-done = bf16[128,16,128]{2,1,0:T(8,128)(2,1)S(1)} collective-permute-done((bf16[128,16,128]{2,1,0:T(8,128)(2,1)S(1)}, bf16[128,16,128]{2,1,0:T(8,128)(2,1)S(1)}, u32[]{:S(2)}, u32[]{:S(2)}) %collective-permute-start) | collective-permute-done | bytes 524320 | tf_op jit(solution)/shard_map/ppermute | solution.py:192
  57.8 0.9 broadcast_select_fusion
  58.7 0.4 copy.164
  59.1 0.5 fusion.53
  59.7 0.3 fusion.3
  60.0 0.3 fusion.20
  60.4 0.3 convolution_bitcast_fusion.6
  60.7 0.4 fusion.5
  61.2 0.9 multiply_reduce_fusion
  62.0 0.6 fusion.1
  62.7 0.5 select_bitcast_fusion
  63.1 0.5 copy.173
  63.7 2.5 %collective-permute-start.1 = (bf16[128,16,128]{2,1,0:T(8,128)(2,1)S(1)}, bf16[128,16,128]{2,1,0:T(8,128)(2,1)}, u32[]{:S(2)}, u32[]{:S(2)}) collective-permute-start(bf16[128,16,128]{2,1,0:T(8,128)(2,1)S(1)} %bitcast.198), channel_id=1, source_target_pairs={{0,4},{4,0},{1,5},{5,1},{2,6},{6,2},{3,7},{7,3},{8,12},{12,8},{9,1... | collective-permute-start | bytes 1572872 | tf_op jit(solution)/shard_map/ppermute | solution.py:213
  66.2 3.7 %shard_map.75 = f32[2048,128]{1,0:T(8,128)} custom-call(bf16[2048,128]{1,0:T(8,128)(2,1)} %bitcast.184), custom_call_target="tpu_custom_call" | custom-call | tf_op jit(solution)/shard_map/pallas_call | solution.py:158
  69.9 1.3 %convert_element_type.63 = bf16[2048,128]{1,0:T(8,128)(2,1)S(1)} convert(f32[2048,128]{1,0:T(8,128)} %shard_map.75) | non-fusion elementwise | flops 262144 | bytes 1572864 | tf_op jit(solution)/shard_map/convert_element_type | solution.py:164
  71.1 0.8 copy.172
  72.0 1.2 %fusion.18 = bf16[128,16,128]{2,1,0:T(8,128)(2,1)S(1)} fusion(bf16[128,16,128]{2,1,0:T(8,128)(2,1)} %collective-permute-done.1, f32[128,16,128]{2,1,0:T(8,128)S(1)} %bitcast.183), kind=kLoop, calls=%fused_computation.35 | loop fusion | flops 786432 | bytes 2097152 | tf_op jit(solution)/shard_map/convert_element_type | solution.py:214
  73.1 1.1 pad_maximum_fusion.1
  74.2 6.2 %all-to-all-start.1 = ((bf16[128,32,128]{2,1,0:T(8,128)(2,1)}), bf16[128,32,128]{2,1,0:T(8,128)(2,1)S(1)}, u32[]{:S(2)}, u32[]{:S(2)}) async-start(bf16[128,32,128]{2,1,0:T(8,128)(2,1)} %pad_maximum_fusion.1), calls=%async_computation.1 | async-start | bytes 2097152 | tf_op jit(solution)/shard_map/all_to_all | solution.py:215
  80.4 0.4 copy.181
  80.8 1.3 %fusion.15 = bf16[2,2,128,128]{2,3,1,0:T(8,128)(2,1)S(1)} fusion(bf16[2,128,1,2,128]{1,4,3,0,2:T(8,128)(2,1)} %copy-done.4, f32[2,2,128]{2,1,0:T(2,128)S(1)} %bitcast.211, f32[2,2,128]{2,1,0:T(2,128)S(1)} %copy_add_fusion, f32[2,2,128,128]{2,3,1,0:T(8,128)} %copy-done.2, f32[2,2,128]{2,1,0:T(2,128)S(1)} %copy_maximum_fusion, ...), kind=kOutput, calls=%fused_computation.28 | convolution fusion | flops 17104896 | bytes 661504 | tf_op jit(solution)/shard_map/bqgd,bkgd->bgqk/dot_general | solution.py:69
  82.1 0.3 convolution_bitcast_fusion.5
  82.4 0.2 fusion.16
  82.7 0.2 convolution_bitcast_fusion.3
  82.9 0.2 fusion.7
  83.2 26.3 %all-to-all-done.1 = bf16[128,32,128]{2,1,0:T(8,128)(2,1)S(1)} async-done(((bf16[128,32,128]{2,1,0:T(8,128)(2,1)}), bf16[128,32,128]{2,1,0:T(8,128)(2,1)S(1)}, u32[]{:S(2)}, u32[]{:S(2)}) %all-to-all-start.1) | async-done | bytes 1048608 | tf_op jit(solution)/shard_map/all_to_all | solution.py:215
  109.5 0.2 fusion.49
  109.8 0.1 copy.185
  110.4 0.5 copy.174
  111.0 0.2 copy.190
  111.3 0.7 copy.264
  112.1 0.2 copy.186
  112.3 0.7 copy.265
  113.1 0.2 copy.183
  113.3 0.7 copy.266
  114.1 0.2 copy.175
  114.3 0.7 copy.267
  (52 shorter events, 2.1 us)
Async XLA Ops:
  0.6 2.6 %copy-start = (bf16[256,512]{1,0:T(8,128)(2,1)S(1)}, bf16[256,512]{1,0:T(8,128)(2,1)}, u32[]{:S(2)}) copy-start(bf16[256,512]{1,0:T(8,128)(2,1)} %param.6) | copy-start | bytes 786436
  0.6 2.6 %copy-start.1 = (bf16[256,512]{1,0:T(8,128)(2,1)S(1)}, bf16[256,512]{1,0:T(8,128)(2,1)}, u32[]{:S(2)}) copy-start(bf16[256,512]{1,0:T(8,128)(2,1)} %param.7) | copy-start | bytes 786436
  7.2 45.8 %all-to-all-start = ((bf16[128,32,128]{2,1,0:T(8,128)(2,1)}), bf16[128,32,128]{2,1,0:T(8,128)(2,1)S(1)}, u32[]{:S(2)}, u32[]{:S(2)}) async-start(bf16[128,32,128]{2,1,0:T(8,128)(2,1)} %copy.156), calls=%async_computation | async-start | bytes 2097152 | tf_op jit(solution)/shard_map/all_to_all | solution.py:188
  24.0 37.2 %copy-start.4 = (bf16[2,128,1,2,128]{1,4,3,0,2:T(8,128)(2,1)}, bf16[2,128,1,2,128]{1,4,3,0,2:T(8,128)(2,1)S(1)}, u32[]{:S(2)}) copy-start(bf16[2,128,1,2,128]{1,4,3,0,2:T(8,128)(2,1)S(1)} %copy.219) | copy-start | bytes 393220
  53.0 4.8 %collective-permute-start = (bf16[128,16,128]{2,1,0:T(8,128)(2,1)S(1)}, bf16[128,16,128]{2,1,0:T(8,128)(2,1)S(1)}, u32[]{:S(2)}, u32[]{:S(2)}) collective-permute-start(bf16[128,16,128]{2,1,0:T(8,128)(2,1)S(1)} %slice.119), channel_id=1, source_target_pairs={{0,4},{4,0},{1,5},{5,1},{2,6},{6,2},{3,7},{7,3},{8,12},{12,8},{9,1... | collective-permute-start | bytes 1572872 | tf_op jit(solution)/shard_map/ppermute | solution.py:192
  56.6 4.6 %copy-start.2 = (f32[2,2,128,128]{2,3,1,0:T(8,128)}, f32[2,2,128,128]{2,3,1,0:T(8,128)S(1)}, u32[]{:S(2)}) copy-start(f32[2,2,128,128]{2,3,1,0:T(8,128)S(1)} %get-tuple-element.26) | copy-start | bytes 786436
  63.7 8.3 %collective-permute-start.1 = (bf16[128,16,128]{2,1,0:T(8,128)(2,1)S(1)}, bf16[128,16,128]{2,1,0:T(8,128)(2,1)}, u32[]{:S(2)}, u32[]{:S(2)}) collective-permute-start(bf16[128,16,128]{2,1,0:T(8,128)(2,1)S(1)} %bitcast.198), channel_id=1, source_target_pairs={{0,4},{4,0},{1,5},{5,1},{2,6},{6,2},{3,7},{7,3},{8,12},{12,8},{9,1... | collective-permute-start | bytes 1572872 | tf_op jit(solution)/shard_map/ppermute | solution.py:213
  74.2 35.3 %all-to-all-start.1 = ((bf16[128,32,128]{2,1,0:T(8,128)(2,1)}), bf16[128,32,128]{2,1,0:T(8,128)(2,1)S(1)}, u32[]{:S(2)}, u32[]{:S(2)}) async-start(bf16[128,32,128]{2,1,0:T(8,128)(2,1)} %pad_maximum_fusion.1), calls=%async_computation.1 | async-start | bytes 2097152 | tf_op jit(solution)/shard_map/all_to_all | solution.py:215
  80.8 1.9 %copy-start.3 = (f32[2,2,128,128]{2,3,1,0:T(8,128)S(1)}, f32[2,2,128,128]{2,3,1,0:T(8,128)}, u32[]{:S(2)}) copy-start(f32[2,2,128,128]{2,3,1,0:T(8,128)} %copy-done.2) | copy-start | bytes 786436
  80.8 1.9 %copy-start.5 = (bf16[2,128,1,2,128]{1,4,3,0,2:T(8,128)(2,1)S(1)}, bf16[2,128,1,2,128]{1,4,3,0,2:T(8,128)(2,1)}, u32[]{:S(2)}) copy-start(bf16[2,128,1,2,128]{1,4,3,0,2:T(8,128)(2,1)} %copy-done.4) | copy-start | bytes 393220
  111.0 3.0 %copy-start.6 = (bf16[2,128,2,128]{1,3,2,0:T(8,128)(2,1)S(1)}, bf16[2,128,2,128]{1,3,2,0:T(8,128)(2,1)}, u32[]{:S(2)}) copy-start(bf16[2,128,2,128]{1,3,2,0:T(8,128)(2,1)} %get-tuple-element.30) | copy-start | bytes 393220

commit v14 on v13

--- a/solution.py
+++ b/solution.py
@@ -215,12 +215,6 @@
     returned = lax.all_to_all(
         jnp.concatenate([strided_out, terms], axis=1), CTX, 0, 0, tiled=True
     )
-    strided_out = returned[:, :strided_size].reshape(
-        peers, 4, blocks_here, residues, half_heads, head_dim
-    )
-    strided_out = strided_out.transpose(1, 2, 0, 3, 4, 5).reshape(
-        4, blocks_here, positions, half_heads, head_dim
-    )
     shares = returned[:, strided_size:].astype(jnp.float32)
     shares = jnp.sum(shares.reshape(peers // 2, 2, -1, head_dim), axis=0)
     shares = shares.reshape(2, blocks_here, SUMMARY, half_heads, head_dim)
@@ -231,12 +225,33 @@
         [value_grad[:, : positions - SUMMARY], value_grad[:, positions - SUMMARY :] + shares[1]],
         axis=1,
     )
-    return (
-        join_heads(attended, strided_out[0]),
-        join_heads(query_grad.astype(jnp.bfloat16), strided_out[1]),
-        join_heads(key_grad.astype(jnp.bfloat16), strided_out[2]),
-        join_heads(value_grad.astype(jnp.bfloat16), strided_out[3]),
-    )
+    fixed = [
+        part.astype(jnp.bfloat16).reshape(blocks_here * positions, half_heads * head_dim)
+        for part in (attended, query_grad, key_grad, value_grad)
+    ]
+    width = returned.shape[1]
+    vmem = pl.BlockSpec(memory_space=pltpu.VMEM)
+    return pl.pallas_call(
+        functools.partial(join_kernel, blocks_here=blocks_here, half_heads=half_heads, width=width),
+        out_shape=[jax.ShapeDtypeStruct(queries.shape, jnp.bfloat16)] * 4,
+        in_specs=[vmem] * 5,
+        out_specs=[vmem] * 4,
+    )(returned.reshape(peers * width, head_dim), *fixed)
+
+
+def join_kernel(returned_ref, *refs, blocks_here, half_heads, width):
+    fixed_refs, out_refs = refs[:4], refs[4:]
+    peers = returned_ref.shape[0] // width
+    fixed_width = fixed_refs[0].shape[1]
+    for array in range(4):
+        out_refs[array][:, :fixed_width] = fixed_refs[array][...]
+        for block in range(blocks_here):
+            for head in range(half_heads):
+                row = (array * blocks_here + block) * half_heads + head
+                out_refs[array][
+                    block * peers : (block + 1) * peers,
+                    fixed_width + head * HD : fixed_width + (head + 1) * HD,
+                ] = returned_ref[pl.ds(row, peers, stride=width), :]
 
 
 def solution(mesh):

time: 116 us -> 118 us (1.017)
  waiting for transfers between devices: 56.3 us -> 53.2 us
  Pallas kernels: 3.7 us -> 6.18 us
  matrix products: 5.67 us -> 7.31 us
    all_to_all x1, waiting for transfers between devices: 26.3 us -> 23 us  [shards(): lax.all_to_all(jnp.concatenate([strided_out, terms], axis=1), CTX, 0, 0,...]
    pallas_call x0 -> x1, Pallas kernels: none -> 2.47 us  [shards(): pl.pallas_call(functools.partial(join_kernel, blocks_here=blocks_here, ha...]
    unnamed x21 -> x42, local copies, waits for them, and re-layouts: 3.29 us -> 3.62 us
  transfers between devices with their start and end apart: 4 -> 4, of which waited for: 3 -> 3; matrix products, arithmetic and copies ran while one was open for 5% -> 7% of each run, Pallas kernels for 3% -> 3%
where the time goes in v14:
time: 118 us; the launch traced here: 117 us
  waiting for transfers between devices  53.2 us (45%)
  starting transfers between devices  28.5 us (24%)
  local copies, waits for them, and re-layouts  13.3 us (11%)
  other arithmetic  7.57 us (6%)
  matrix products  7.31 us (6%)
  Pallas kernels  6.18 us (5%)
  between operations  1.23 us (1%)
    all_to_all x1, waiting for transfers between devices, shards(): lax.all_to_all(jnp.concatenate([strided_rows, summary_rows], axis=1), CTX...  29.1 us
    all_to_all x1, waiting for transfers between devices, shards(): lax.all_to_all(jnp.concatenate([strided_out, terms], axis=1), CTX, 0, 0,...  23 us
    all_to_all x1, starting transfers between devices, shards(): lax.all_to_all(jnp.concatenate([strided_rows, summary_rows], axis=1), CTX...  16.6 us
    all_to_all x1, starting transfers between devices, shards(): lax.all_to_all(jnp.concatenate([strided_out, terms], axis=1), CTX, 0, 0,...  6.16 us
    pallas_call x1, Pallas kernels, strided_heads(): pl.pallas_call(functools.partial(strided_kernel, scaling=scaling, arrays=...  3.71 us
    unnamed x42, local copies, waits for them, and re-layouts  3.62 us
    ppermute x1, starting transfers between devices, shards(): sibling = lax.ppermute(mine, 'ctx_core', swap)  3.23 us
    pallas_call x1, Pallas kernels, shards(): pl.pallas_call(functools.partial(join_kernel, blocks_here=blocks_here, ha...  2.47 us
  transfers between devices with their start and end apart: 4, of which 3 were waited for; matrix products, arithmetic and copies ran while one was open for 7% of the time, Pallas kernels for 3%

profile of v14, /device:TPU:1, one launch (start us, length us, event | category | flops | bytes accessed | tf_op | source)
XLA Modules:
  0.0 117.2 jit_solution(9967443270106833036)
XLA Ops:
  0.7 1.1 reshape.158
  1.7 1.0 reshape.159
  2.7 0.4 slice_bitcast_fusion.2
  3.4 0.4 slice_bitcast_fusion.1
  3.8 1.0 maximum_bitcast_fusion
  5.2 0.3 broadcast_in_dim.42
  5.6 1.7 %copy.200 = bf16[128,32,128]{2,1,0:T(8,128)(2,1)} copy(bf16[128,32,128]{2,0,1:T(8,128)(2,1)S(1)} %pad_maximum_fusion) | data formatting | bytes 2097152 | tf_op jit(solution)/shard_map/concatenate | solution.py:189
  7.3 16.6 %all-to-all-start = ((bf16[128,32,128]{2,1,0:T(8,128)(2,1)}), bf16[128,32,128]{2,1,0:T(8,128)(2,1)S(1)}, u32[]{:S(2)}, u32[]{:S(2)}) async-start(bf16[128,32,128]{2,1,0:T(8,128)(2,1)} %copy.200), calls=%async_computation | async-start | bytes 2097152 | tf_op jit(solution)/shard_map/all_to_all | solution.py:188
  23.9 29.1 %all-to-all-done = bf16[128,32,128]{2,1,0:T(8,128)(2,1)S(1)} async-done(((bf16[128,32,128]{2,1,0:T(8,128)(2,1)}), bf16[128,32,128]{2,1,0:T(8,128)(2,1)S(1)}, u32[]{:S(2)}, u32[]{:S(2)}) %all-to-all-start) | async-done | bytes 1048608 | tf_op jit(solution)/shard_map/all_to_all | solution.py:188
  53.1 3.2 %collective-permute-start = (bf16[128,16,128]{2,1,0:T(8,128)(2,1)S(1)}, bf16[128,16,128]{2,1,0:T(8,128)(2,1)S(1)}, u32[]{:S(2)}, u32[]{:S(2)}) collective-permute-start(bf16[128,16,128]{2,1,0:T(8,128)(2,1)S(1)} %slice.95), channel_id=1, source_target_pairs={{0,4},{4,0},{1,5},{5,1},{2,6},{6,2},{3,7},{7,3},{8,12},{12,8},{9,1... | collective-permute-start | bytes 1572872 | tf_op jit(solution)/shard_map/ppermute | solution.py:192
  56.4 0.3 fusion.43
  56.7 1.1 collective-permute-done
  57.9 0.9 broadcast_select_fusion.1
  58.8 0.5 fusion.44
  59.3 0.3 fusion.22
  59.5 0.3 fusion.3
  59.9 0.2 fusion.33
  60.1 0.4 copy.240
  60.5 0.2 convolution_bitcast_fusion.4
  60.7 0.4 fusion.18
  61.1 0.4 fusion.5
  61.6 1.2 multiply_reduce_fusion
  62.7 1.8 %fusion.1 = bf16[2,2,128,1024]{2,3,0,1:T(8,128)(2,1)S(1)} fusion(bf16[1024,2,128,1]{0,2,3,1:T(8,128)(2,1)} %copy-done.1, f32[2,2,128]{2,0,1:T(2,128)S(1)} %bitcast.181, f32[2,2,128]{2,0,1:T(2,128)S(1)} %copy-done.17, f32[2,2,128,1024]{2,3,0,1:T(8,128)S(1)} %get-tuple-element.22, f32[2,2,128]{2,0,1:T(2,128)S(1)} %copy.207, ...), kind=kOutput, calls=%fused_computation.2 | convolution fusion | flops 136839168 | bytes 3807232 | tf_op jit(solution)/shard_map/bqgd,mgd->bgqm/dot_general | solution.py:72
  64.5 0.4 select_bitcast_fusion
  65.0 1.3 %copy.219 = bf16[1024,2,128]{2,1,0:T(2,128)(2,1)} copy(bf16[1024,2,128]{2,0,1:T(8,128)(2,1)S(1)} %get-tuple-element.7) | data formatting | bytes 1048576 | tf_op jit(solution)/shard_map/jit(_where)/select_n | solution.py:211
  66.3 2.5 %collective-permute-start.1 = (bf16[128,16,128]{2,1,0:T(8,128)(2,1)}, bf16[128,16,128]{2,1,0:T(8,128)(2,1)}, u32[]{:S(2)}, u32[]{:S(2)}) collective-permute-start(bf16[128,16,128]{2,1,0:T(8,128)(2,1)} %bitcast.34), channel_id=1, source_target_pairs={{0,4},{4,0},{1,5},{5,1},{2,6},{6,2},{3,7},{7,3},{8,12},{12,8},{9,1... | collective-permute-start | bytes 1572872 | tf_op jit(solution)/shard_map/ppermute | solution.py:213
  68.8 3.7 %shard_map.75 = f32[2048,128]{1,0:T(8,128)} custom-call(bf16[2048,128]{1,0:T(8,128)(2,1)} %bitcast.159), custom_call_target="tpu_custom_call" | custom-call | tf_op jit(solution)/shard_map/pallas_call | solution.py:158
  72.5 1.3 %convert_element_type.54 = bf16[2048,128]{1,0:T(8,128)(2,1)S(1)} convert(f32[2048,128]{1,0:T(8,128)} %shard_map.75) | non-fusion elementwise | flops 262144 | bytes 1572864 | tf_op jit(solution)/shard_map/convert_element_type | solution.py:164
  73.8 0.8 copy.218
  74.6 1.1 fusion.17
  75.8 1.1 pad_maximum_fusion.1
  76.8 6.2 %all-to-all-start.1 = ((bf16[128,32,128]{2,1,0:T(8,128)(2,1)}), bf16[128,32,128]{2,1,0:T(8,128)(2,1)S(1)}, u32[]{:S(2)}, u32[]{:S(2)}) async-start(bf16[128,32,128]{2,1,0:T(8,128)(2,1)} %pad_maximum_fusion.1), calls=%async_computation.1 | async-start | bytes 2097152 | tf_op jit(solution)/shard_map/all_to_all | solution.py:215
  83.0 0.8 copy.266
  83.8 0.4 copy.224
  84.2 0.2 convolution_bitcast_fusion.2
  84.5 0.7 copy-done.12
  85.2 1.3 %fusion.14 = bf16[2,2,128,128]{3,2,1,0:T(8,128)(2,1)S(1)} fusion(bf16[2,128,1,2,128]{1,4,3,0,2:T(8,128)(2,1)} %copy.266, f32[2,2,128]{2,1,0:T(2,128)S(1)} %copy.223, bf16[2,128,1,2,128]{4,3,1,0,2:T(2,128)(2,1)S(1)} %get-tuple-element.28, f32[2,2,128]{2,1,0:T(2,128)S(1)} %copy_add_fusion, f32[2,2,128,128]{3,2,1,0:T(8,128)} %copy-done.11, ...), kind=kOutput, calls=%fused_computation.27 | convolution fusion | flops 17104896 | bytes 661504 | tf_op jit(solution)/shard_map/bqgd,bkgd->bgqk/dot_general | solution.py:69
  86.6 0.5 convolution_bitcast_fusion.5
  87.1 0.2 fusion.13
  87.3 0.1 copy.227
  87.4 0.7 copy.324
  88.1 0.2 fusion.7
  88.5 0.7 copy.325
  89.2 23.0 %all-to-all-done.1 = bf16[128,32,128]{2,1,0:T(8,128)(2,1)S(1)} async-done(((bf16[128,32,128]{2,1,0:T(8,128)(2,1)}), bf16[128,32,128]{2,1,0:T(8,128)(2,1)S(1)}, u32[]{:S(2)}, u32[]{:S(2)}) %all-to-all-start.1) | async-done | bytes 1048608 | tf_op jit(solution)/shard_map/all_to_all | solution.py:215
  112.3 0.8 fusion.34
  113.2 0.7 copy.322
  114.1 0.7 copy.323
  114.8 2.5 %shard_map.76 = (bf16[256,512]{1,0:T(8,128)(2,1)}, bf16[256,512]{1,0:T(8,128)(2,1)}, bf16[256,512]{1,0:T(8,128)(2,1)}, bf16[256,512]{1,0:T(8,128)(2,1)}) custom-call(bf16[4096,128]{1,0:T(8,128)(2,1)} %bitcast.157, bf16[256,256]{1,0:T(8,128)(2,1)} %bitcast.169, bf16[256,256]{1,0:T(8,128)(2,1)} %bitcast.168, bf16[256,256]{1,0:T(8,128)(2,1)} %bitcast.171, ...), custom_call_target="tpu_custom_call" | custom-call | tf_op jit(solution)/shard_map/pallas_call | solution.py:234
  (69 shorter events, 1.6 us)
Async XLA Ops:
  0.6 2.6 %copy-start.14 = (bf16[256,512]{1,0:T(8,128)(2,1)S(1)}, bf16[256,512]{1,0:T(8,128)(2,1)}, u32[]{:S(2)}) copy-start(bf16[256,512]{1,0:T(8,128)(2,1)} %param.6) | copy-start | bytes 786436
  0.6 2.6 %copy-start.15 = (bf16[256,512]{1,0:T(8,128)(2,1)S(1)}, bf16[256,512]{1,0:T(8,128)(2,1)}, u32[]{:S(2)}) copy-start(bf16[256,512]{1,0:T(8,128)(2,1)} %param.7) | copy-start | bytes 786436
  3.1 53.3 %copy-start.4 = (bf16[2,128,1,2,128]{4,3,1,0,2:T(2,128)(2,1)}, bf16[2,128,1,2,128]{4,3,1,0,2:T(2,128)(2,1)S(1)}, u32[]{:S(2)}) copy-start(bf16[2,128,1,2,128]{4,3,1,0,2:T(2,128)(2,1)S(1)} %get-tuple-element.14) | copy-start | bytes 393220
  3.1 55.6 %copy-start.6 = (bf16[2,128,1,2,128]{4,3,1,0,2:T(2,128)(2,1)}, bf16[2,128,1,2,128]{4,3,1,0,2:T(2,128)(2,1)S(1)}, u32[]{:S(2)}) copy-start(bf16[2,128,1,2,128]{4,3,1,0,2:T(2,128)(2,1)S(1)} %get-tuple-element.26) | copy-start | bytes 393220
  3.7 1.8 %copy-start.9 = (bf16[2,128,1,2,128]{4,3,1,0,2:T(2,128)(2,1)}, bf16[2,128,1,2,128]{4,3,1,0,2:T(2,128)(2,1)S(1)}, u32[]{:S(2)}) copy-start(bf16[2,128,1,2,128]{4,3,1,0,2:T(2,128)(2,1)S(1)} %get-tuple-element.16) | copy-start | bytes 393220
  7.3 45.8 %all-to-all-start = ((bf16[128,32,128]{2,1,0:T(8,128)(2,1)}), bf16[128,32,128]{2,1,0:T(8,128)(2,1)S(1)}, u32[]{:S(2)}, u32[]{:S(2)}) async-start(bf16[128,32,128]{2,1,0:T(8,128)(2,1)} %copy.200), calls=%async_computation | async-start | bytes 2097152 | tf_op jit(solution)/shard_map/all_to_all | solution.py:188
  53.1 4.8 %collective-permute-start = (bf16[128,16,128]{2,1,0:T(8,128)(2,1)S(1)}, bf16[128,16,128]{2,1,0:T(8,128)(2,1)S(1)}, u32[]{:S(2)}, u32[]{:S(2)}) collective-permute-start(bf16[128,16,128]{2,1,0:T(8,128)(2,1)S(1)} %slice.95), channel_id=1, source_target_pairs={{0,4},{4,0},{1,5},{5,1},{2,6},{6,2},{3,7},{7,3},{8,12},{12,8},{9,1... | collective-permute-start | bytes 1572872 | tf_op jit(solution)/shard_map/ppermute | solution.py:192
  56.7 3.3 %copy-start.11 = (f32[2,2,128,128]{3,2,1,0:T(8,128)}, f32[2,2,128,128]{3,2,1,0:T(8,128)S(1)}, u32[]{:S(2)}) copy-start(f32[2,2,128,128]{3,2,1,0:T(8,128)S(1)} %get-tuple-element.20) | copy-start | bytes 786436
  58.8 1.1 copy-start.2
  59.8 1.2 %copy-start.16 = (f32[2,2,128]{2,0,1:T(2,128)}, f32[2,2,128]{2,0,1:T(2,128)S(1)}, u32[]{:S(2)}) copy-start(f32[2,2,128]{2,0,1:T(2,128)S(1)} %copy.210) | copy-start | bytes 6148
  60.5 2.2 %copy-start.1 = (bf16[1024,2,128,1]{0,2,3,1:T(8,128)(2,1)}, bf16[1024,2,128,1]{0,2,3,1:T(8,128)(2,1)S(1)}, u32[]{:S(2)}) copy-start(bf16[1024,2,128,1]{0,2,3,1:T(8,128)(2,1)S(1)} %copy.240) | copy-start | bytes 1572868
  61.1 1.6 %copy-start.17 = (f32[2,2,128]{2,0,1:T(2,128)S(1)}, f32[2,2,128]{2,0,1:T(2,128)}, u32[]{:S(2)}) copy-start(f32[2,2,128]{2,0,1:T(2,128)} %copy-done.16) | copy-start | bytes 6148
  62.7 1.8 %copy-start.7 = (bf16[2,128,1,2,128]{4,3,1,0,2:T(2,128)(2,1)S(1)}, bf16[2,128,1,2,128]{4,3,1,0,2:T(2,128)(2,1)}, u32[]{:S(2)}) copy-start(bf16[2,128,1,2,128]{4,3,1,0,2:T(2,128)(2,1)} %copy-done.6) | copy-start | bytes 393220
  66.3 8.3 %collective-permute-start.1 = (bf16[128,16,128]{2,1,0:T(8,128)(2,1)}, bf16[128,16,128]{2,1,0:T(8,128)(2,1)}, u32[]{:S(2)}, u32[]{:S(2)}) collective-permute-start(bf16[128,16,128]{2,1,0:T(8,128)(2,1)} %bitcast.34), channel_id=1, source_target_pairs={{0,4},{4,0},{1,5},{5,1},{2,6},{6,2},{3,7},{7,3},{8,12},{12,8},{9,1... | collective-permute-start | bytes 1572872 | tf_op jit(solution)/shard_map/ppermute | solution.py:213
  75.8 7.3 %copy-start.10 = (bf16[2,128,1,2,128]{4,3,1,0,2:T(2,128)(2,1)S(1)}, bf16[2,128,1,2,128]{4,3,1,0,2:T(2,128)(2,1)}, u32[]{:S(2)}) copy-start(bf16[2,128,1,2,128]{4,3,1,0,2:T(2,128)(2,1)} %copy-done.9) | copy-start | bytes 393220
  75.8 8.0 %copy-start.3 = (bf16[128,16,128]{2,1,0:T(8,128)(2,1)S(1)}, bf16[128,16,128]{2,1,0:T(8,128)(2,1)}, u32[]{:S(2)}) copy-start(bf16[128,16,128]{2,1,0:T(8,128)(2,1)} %copy-done.2) | copy-start | bytes 1572868
  76.8 35.3 %all-to-all-start.1 = ((bf16[128,32,128]{2,1,0:T(8,128)(2,1)}), bf16[128,32,128]{2,1,0:T(8,128)(2,1)S(1)}, u32[]{:S(2)}, u32[]{:S(2)}) async-start(bf16[128,32,128]{2,1,0:T(8,128)(2,1)} %pad_maximum_fusion.1), calls=%async_computation.1 | async-start | bytes 2097152 | tf_op jit(solution)/shard_map/all_to_all | solution.py:215
  84.2 2.9 %copy-start.5 = (bf16[2,128,1,2,128]{4,3,1,0,2:T(2,128)(2,1)S(1)}, bf16[2,128,1,2,128]{4,3,1,0,2:T(2,128)(2,1)}, u32[]{:S(2)}) copy-start(bf16[2,128,1,2,128]{4,3,1,0,2:T(2,128)(2,1)} %copy-done.4) | copy-start | bytes 393220
  84.5 0.7 copy-start.12
  85.2 2.9 %copy-start.8 = (bf16[2,128,1,2,128]{4,3,1,0,2:T(2,128)(2,1)S(1)}, bf16[2,128,1,2,128]{4,3,1,0,2:T(2,128)(2,1)}, u32[]{:S(2)}) copy-start(bf16[2,128,1,2,128]{4,3,1,0,2:T(2,128)(2,1)} %copy-done.6) | copy-start | bytes 393220
  86.5 1.8 %copy-start.13 = (bf16[2,128,2,128]{3,1,0,2:T(8,128)(2,1)S(1)}, bf16[2,128,2,128]{3,1,0,2:T(8,128)(2,1)}, u32[]{:S(2)}) copy-start(bf16[2,128,2,128]{3,1,0,2:T(8,128)(2,1)} %get-tuple-element.24) | copy-start | bytes 393220
  112.2 2.6 %copy-start = (bf16[128,32,128]{2,1,0:T(8,128)(2,1)}, bf16[128,32,128]{2,1,0:T(8,128)(2,1)S(1)}, u32[]{:S(2)}) copy-start(bf16[128,32,128]{2,1,0:T(8,128)(2,1)S(1)} %all-to-all-done.1) | copy-start | bytes 3145732

commit v15 on v13

--- a/solution.py
+++ b/solution.py
@@ -190,6 +190,8 @@
     )
     mine = received[:, strided_size:]
     sibling = lax.ppermute(mine, "ctx_core", swap)
+    strided_out = strided_heads(received[:, :strided_size], scaling, half_heads)
+    strided_out, sibling = lax.optimization_barrier((strided_out, sibling))
     summary_shape = (peers * blocks_here * SUMMARY, half_heads, head_dim)
     summary_keys = jnp.where(core == 0, mine, sibling).reshape(summary_shape)
     summary_values = jnp.where(core == 0, sibling, mine).reshape(summary_shape)
@@ -204,7 +206,6 @@
         scaling,
         lax.axis_index("ctx_chip") * 2 + core,
     )
-    strided_out = strided_heads(received[:, :strided_size], scaling, half_heads)
 
     terms = terms.astype(jnp.bfloat16).reshape(2, peers, -1, head_dim)
     keep = jnp.where(core == 0, terms[0], terms[1])

time: 116 us -> 115 us (level)
  local copies, waits for them, and re-layouts: 12.7 us -> 15.2 us
  other arithmetic: 6.95 us -> 5.04 us
  waiting for transfers between devices: 56.3 us -> 54.8 us
    all_to_all x1, waiting for transfers between devices: 28.8 us -> 27.6 us  [shards(): lax.all_to_all(jnp.concatenate([strided_rows, summary_rows], axis=1), CTX...]
    ppermute x1, waiting for transfers between devices: 1.18 us -> 0.01 us  [shards(): sibling = lax.ppermute(mine, 'ctx_core', swap)]
    unnamed x21 -> x27, local copies, waits for them, and re-layouts: 3.29 us -> 4.18 us
  transfers between devices with their start and end apart: 4 -> 4, of which waited for: 3 -> 3; matrix products, arithmetic and copies ran while one was open for 5% -> 6% of each run, Pallas kernels for 3% -> 3%
where the time goes in v15:
time: 115 us; the launch traced here: 114 us
  waiting for transfers between devices  54.8 us (48%)
  starting transfers between devices  28.2 us (25%)
  local copies, waits for them, and re-layouts  15.2 us (13%)
  matrix products  6.33 us (6%)
  other arithmetic  5.04 us (4%)
  Pallas kernels  3.69 us (3%)
  between operations  1.17 us (1%)
    all_to_all x1, waiting for transfers between devices, shards(): lax.all_to_all(jnp.concatenate([strided_rows, summary_rows], axis=1), CTX...  27.6 us
    all_to_all x1, waiting for transfers between devices, shards(): lax.all_to_all(jnp.concatenate([strided_out, terms], axis=1), CTX, 0, 0,...  26.3 us
    all_to_all x1, starting transfers between devices, shards(): lax.all_to_all(jnp.concatenate([strided_rows, summary_rows], axis=1), CTX...  16.6 us
    all_to_all x1, starting transfers between devices, shards(): lax.all_to_all(jnp.concatenate([strided_out, terms], axis=1), CTX, 0, 0,...  6.29 us
    unnamed x27, local copies, waits for them, and re-layouts  4.18 us
    pallas_call x1, Pallas kernels, strided_heads(): pl.pallas_call(functools.partial(strided_kernel, scaling=scaling, arrays=...  3.69 us
    ppermute x1, starting transfers between devices, shards(): sibling = lax.ppermute(mine, 'ctx_core', swap)  3.22 us
  transfers between devices with their start and end apart: 4, of which 3 were waited for; matrix products, arithmetic and copies ran while one was open for 6% of the time, Pallas kernels for 3%

profile of v15, /device:TPU:1, one launch (start us, length us, event | category | flops | bytes accessed | tf_op | source)
XLA Modules:
  0.0 114.4 jit_solution(7817495883451164526)
XLA Ops:
  0.7 1.1 reshape.237
  1.7 1.0 reshape.239
  2.7 0.4 slice_bitcast_fusion.6
  3.3 0.4 slice_bitcast_fusion.5
  3.7 1.0 maximum_bitcast_fusion
  5.2 0.3 broadcast_in_dim.45
  5.5 1.6 %copy.156 = bf16[128,32,128]{2,1,0:T(8,128)(2,1)} copy(bf16[128,32,128]{2,0,1:T(8,128)(2,1)S(1)} %pad_maximum_fusion) | data formatting | bytes 2097152 | tf_op jit(solution)/shard_map/concatenate | solution.py:189
  7.2 16.6 %all-to-all-start = ((bf16[128,32,128]{2,1,0:T(8,128)(2,1)}), bf16[128,32,128]{2,1,0:T(8,128)(2,1)S(1)}, u32[]{:S(2)}, u32[]{:S(2)}) async-start(bf16[128,32,128]{2,1,0:T(8,128)(2,1)} %copy.156), calls=%async_computation | async-start | bytes 2097152 | tf_op jit(solution)/shard_map/all_to_all | solution.py:188
  23.8 0.8 copy.219
  24.6 0.8 copy.221
  25.4 27.6 %all-to-all-done = bf16[128,32,128]{2,1,0:T(8,128)(2,1)S(1)} async-done(((bf16[128,32,128]{2,1,0:T(8,128)(2,1)}), bf16[128,32,128]{2,1,0:T(8,128)(2,1)S(1)}, u32[]{:S(2)}, u32[]{:S(2)}) %all-to-all-start) | async-done | bytes 1048608 | tf_op jit(solution)/shard_map/all_to_all | solution.py:188
  53.0 1.0 fusion.50
  54.0 3.2 %collective-permute-start = (bf16[128,16,128]{2,1,0:T(8,128)(2,1)S(1)}, bf16[128,16,128]{2,1,0:T(8,128)(2,1)S(1)}, u32[]{:S(2)}, u32[]{:S(2)}) collective-permute-start(bf16[128,16,128]{2,1,0:T(8,128)(2,1)S(1)} %get-tuple-element.14), channel_id=1, source_target_pairs={{0,4},{4,0},{1,5},{5,1},{2,6},{6,2},{3,7},{7,3},{8,12},{12,8},{9,1... | collective-permute-start | bytes 1572872 | tf_op jit(solution)/shard_map/ppermute | solution.py:192
  57.3 0.9 fusion.53
  58.2 3.7 %shard_map.75 = f32[2048,128]{1,0:T(8,128)} custom-call(bf16[2048,128]{1,0:T(8,128)(2,1)} %bitcast.189), custom_call_target="tpu_custom_call" | custom-call | tf_op jit(solution)/shard_map/pallas_call | solution.py:158
  61.9 1.3 %convert_element_type.60 = bf16[2048,128]{1,0:T(8,128)(2,1)S(1)} convert(f32[2048,128]{1,0:T(8,128)} %shard_map.75) | non-fusion elementwise | flops 262144 | bytes 1572864 | tf_op jit(solution)/shard_map/convert_element_type | solution.py:164
  63.3 0.4 copy.164
  63.7 0.5 fusion.54
  64.3 0.3 fusion.3
  64.6 0.3 fusion.20
  65.0 0.3 convolution_bitcast_fusion.6
  65.3 0.2 copy-done.2
  65.5 0.4 fusion.5
  66.0 0.9 multiply_reduce_fusion
  66.8 0.6 fusion.1
  67.5 0.4 select_bitcast_fusion
  67.9 0.5 copy.173
  68.5 2.1 %collective-permute-start.1 = (bf16[128,16,128]{2,1,0:T(8,128)(2,1)S(1)}, bf16[128,16,128]{2,1,0:T(8,128)(2,1)S(1)}, u32[]{:S(2)}, u32[]{:S(2)}) collective-permute-start(bf16[128,16,128]{2,1,0:T(8,128)(2,1)S(1)} %bitcast.198), channel_id=1, source_target_pairs={{0,4},{4,0},{1,5},{5,1},{2,6},{6,2},{3,7},{7,3},{8,12},{12,8},{9,1... | collective-permute-start | bytes 1572872 | tf_op jit(solution)/shard_map/ppermute | solution.py:214
  70.6 0.8 copy.172
  71.4 0.9 collective-permute-done.1
  72.4 1.0 pad_maximum_fusion.1
  73.5 6.3 %all-to-all-start.1 = ((bf16[128,32,128]{2,1,0:T(8,128)(2,1)}), bf16[128,32,128]{2,1,0:T(8,128)(2,1)S(1)}, u32[]{:S(2)}, u32[]{:S(2)}) async-start(bf16[128,32,128]{2,1,0:T(8,128)(2,1)} %pad_maximum_fusion.1), calls=%async_computation.1 | async-start | bytes 2097152 | tf_op jit(solution)/shard_map/all_to_all | solution.py:216
  79.8 0.4 copy.181
  80.2 1.3 %fusion.15 = bf16[2,2,128,128]{2,3,1,0:T(8,128)(2,1)S(1)} fusion(bf16[2,128,1,2,128]{1,4,3,0,2:T(8,128)(2,1)} %copy.219, f32[2,2,128]{2,1,0:T(2,128)S(1)} %bitcast.211, f32[2,2,128]{2,1,0:T(2,128)S(1)} %copy_add_fusion, f32[2,2,128,128]{2,3,1,0:T(8,128)} %get-tuple-element.31, f32[2,2,128]{2,1,0:T(2,128)S(1)} %copy_maximum_fusion, ...), kind=kOutput, calls=%fused_computation.28 | convolution fusion | flops 17104896 | bytes 661504 | tf_op jit(solution)/shard_map/bqgd,bkgd->bgqk/dot_general | solution.py:69
  81.5 0.3 convolution_bitcast_fusion.5
  81.8 0.2 fusion.16
  82.1 0.2 convolution_bitcast_fusion.3
  82.4 0.2 fusion.7
  82.6 26.3 %all-to-all-done.1 = bf16[128,32,128]{2,1,0:T(8,128)(2,1)S(1)} async-done(((bf16[128,32,128]{2,1,0:T(8,128)(2,1)}), bf16[128,32,128]{2,1,0:T(8,128)(2,1)S(1)}, u32[]{:S(2)}, u32[]{:S(2)}) %all-to-all-start.1) | async-done | bytes 1048608 | tf_op jit(solution)/shard_map/all_to_all | solution.py:216
  109.8 0.5 copy.174
  110.5 0.2 copy.190
  110.7 0.7 copy.264
  111.5 0.2 copy.186
  111.7 0.7 copy.265
  112.5 0.2 copy.183
  112.7 0.7 copy.266
  113.5 0.2 copy.175
  113.7 0.7 copy.267
  (58 shorter events, 2.4 us)
Async XLA Ops:
  0.6 2.6 %copy-start.3 = (bf16[256,512]{1,0:T(8,128)(2,1)S(1)}, bf16[256,512]{1,0:T(8,128)(2,1)}, u32[]{:S(2)}) copy-start(bf16[256,512]{1,0:T(8,128)(2,1)} %param.6) | copy-start | bytes 786436
  0.6 2.6 %copy-start.4 = (bf16[256,512]{1,0:T(8,128)(2,1)S(1)}, bf16[256,512]{1,0:T(8,128)(2,1)}, u32[]{:S(2)}) copy-start(bf16[256,512]{1,0:T(8,128)(2,1)} %param.7) | copy-start | bytes 786436
  7.2 45.8 %all-to-all-start = ((bf16[128,32,128]{2,1,0:T(8,128)(2,1)}), bf16[128,32,128]{2,1,0:T(8,128)(2,1)S(1)}, u32[]{:S(2)}, u32[]{:S(2)}) async-start(bf16[128,32,128]{2,1,0:T(8,128)(2,1)} %copy.156), calls=%async_computation | async-start | bytes 2097152 | tf_op jit(solution)/shard_map/all_to_all | solution.py:188
  54.0 9.2 %collective-permute-start = (bf16[128,16,128]{2,1,0:T(8,128)(2,1)S(1)}, bf16[128,16,128]{2,1,0:T(8,128)(2,1)S(1)}, u32[]{:S(2)}, u32[]{:S(2)}) collective-permute-start(bf16[128,16,128]{2,1,0:T(8,128)(2,1)S(1)} %get-tuple-element.14), channel_id=1, source_target_pairs={{0,4},{4,0},{1,5},{5,1},{2,6},{6,2},{3,7},{7,3},{8,12},{12,8},{9,1... | collective-permute-start | bytes 1572872 | tf_op jit(solution)/shard_map/ppermute | solution.py:192
  63.3 1.0 copy-start.5
  64.6 0.9 copy-start.2
  65.0 1.0 copy-start.7
  67.5 1.0 copy-start
  68.5 3.8 %collective-permute-start.1 = (bf16[128,16,128]{2,1,0:T(8,128)(2,1)S(1)}, bf16[128,16,128]{2,1,0:T(8,128)(2,1)S(1)}, u32[]{:S(2)}, u32[]{:S(2)}) collective-permute-start(bf16[128,16,128]{2,1,0:T(8,128)(2,1)S(1)} %bitcast.198), channel_id=1, source_target_pairs={{0,4},{4,0},{1,5},{5,1},{2,6},{6,2},{3,7},{7,3},{8,12},{12,8},{9,1... | collective-permute-start | bytes 1572872 | tf_op jit(solution)/shard_map/ppermute | solution.py:214
  73.5 8.1 %copy-start.1 = (bf16[2,2,128,1024]{2,3,0,1:T(8,128)(2,1)S(1)}, bf16[2,2,128,1024]{2,3,0,1:T(8,128)(2,1)}, u32[]{:S(2)}) copy-start(bf16[2,2,128,1024]{2,3,0,1:T(8,128)(2,1)} %copy-done) | copy-start | bytes 3145732
  73.5 35.5 %all-to-all-start.1 = ((bf16[128,32,128]{2,1,0:T(8,128)(2,1)}), bf16[128,32,128]{2,1,0:T(8,128)(2,1)S(1)}, u32[]{:S(2)}, u32[]{:S(2)}) async-start(bf16[128,32,128]{2,1,0:T(8,128)(2,1)} %pad_maximum_fusion.1), calls=%async_computation.1 | async-start | bytes 2097152 | tf_op jit(solution)/shard_map/all_to_all | solution.py:216
  80.2 1.9 %copy-start.6 = (f32[2,2,128,128]{2,3,1,0:T(8,128)S(1)}, f32[2,2,128,128]{2,3,1,0:T(8,128)}, u32[]{:S(2)}) copy-start(f32[2,2,128,128]{2,3,1,0:T(8,128)} %get-tuple-element.31) | copy-start | bytes 786436
  80.2 1.9 %copy-start.8 = (bf16[2,128,1,2,128]{1,4,3,0,2:T(8,128)(2,1)S(1)}, bf16[2,128,1,2,128]{1,4,3,0,2:T(8,128)(2,1)}, u32[]{:S(2)}) copy-start(bf16[2,128,1,2,128]{1,4,3,0,2:T(8,128)(2,1)} %copy.219) | copy-start | bytes 393220
  110.4 3.0 %copy-start.9 = (bf16[2,128,2,128]{1,3,2,0:T(8,128)(2,1)S(1)}, bf16[2,128,2,128]{1,3,2,0:T(8,128)(2,1)}, u32[]{:S(2)}) copy-start(bf16[2,128,2,128]{1,3,2,0:T(8,128)(2,1)} %get-tuple-element.35) | copy-start | bytes 393220

commit v16 on v15

--- a/solution.py
+++ b/solution.py
@@ -39,7 +39,9 @@
     blocks_here, positions, half_heads, head_dim = query.shape
     summary_count = flat_keys.shape[0]
     block_ids = here * blocks_here + jnp.arange(blocks_here, dtype=jnp.int32)
-    summary_block = jnp.arange(summary_count, dtype=jnp.int32) // SUMMARY
+    summary_block = (jnp.arange(summary_count, dtype=jnp.int32) // (SUMMARY // 2)) % (
+        summary_count // SUMMARY
+    )
     earlier = (summary_block[None, :] < block_ids[:, None])[:, None, None, :]
     causal = (jnp.arange(positions)[:, None] >= jnp.arange(positions)[None, :])[None, None]
     local_scores = (
@@ -181,7 +183,8 @@
     strided_rows = strided_rows.transpose(2, 0, 1, 3, 4, 5).reshape(peers, -1, head_dim)
     summary_rows = jnp.stack(
         [key_fixed[:, positions - SUMMARY :], value_fixed[:, positions - SUMMARY :]]
-    ).reshape(1, 2, -1, head_dim)
+    ).reshape(2, blocks_here, 2, SUMMARY // 2, half_heads, head_dim)
+    summary_rows = summary_rows.transpose(2, 0, 1, 3, 4, 5).reshape(1, 2, -1, head_dim)
     summary_rows = jnp.broadcast_to(summary_rows, (peers // 2,) + summary_rows.shape[1:])
     summary_rows = summary_rows.reshape(peers, -1, head_dim)
     strided_size = strided_rows.shape[1]
@@ -192,9 +195,12 @@
     sibling = lax.ppermute(mine, "ctx_core", swap)
     strided_out = strided_heads(received[:, :strided_size], scaling, half_heads)
     strided_out, sibling = lax.optimization_barrier((strided_out, sibling))
+    both = jnp.stack([mine, sibling]).reshape(
+        2, peers, 2, blocks_here * SUMMARY // 2, half_heads, head_dim
+    )
     summary_shape = (peers * blocks_here * SUMMARY, half_heads, head_dim)
-    summary_keys = jnp.where(core == 0, mine, sibling).reshape(summary_shape)
-    summary_values = jnp.where(core == 0, sibling, mine).reshape(summary_shape)
+    summary_keys = both[:, :, 0].reshape(summary_shape)
+    summary_values = both[:, :, 1].reshape(summary_shape)
 
     attended, query_grad, key_grad, value_grad, terms = fixed_heads(
         query_fixed,
@@ -207,9 +213,9 @@
         lax.axis_index("ctx_chip") * 2 + core,
     )
 
-    terms = terms.astype(jnp.bfloat16).reshape(2, peers, -1, head_dim)
-    keep = jnp.where(core == 0, terms[0], terms[1])
-    give = jnp.where(core == 0, terms[1], terms[0])
+    terms = terms.astype(jnp.bfloat16).reshape(2, 2, peers, -1, head_dim).transpose(1, 2, 0, 3, 4)
+    terms = terms.reshape(2, peers, -1, head_dim)
+    keep, give = terms[0], terms[1]
     terms = (
         keep.astype(jnp.float32) + lax.ppermute(give, "ctx_core", swap).astype(jnp.float32)
     ).astype(jnp.bfloat16)
@@ -224,7 +230,8 @@
     )
     shares = returned[:, strided_size:].astype(jnp.float32)
     shares = jnp.sum(shares.reshape(peers // 2, 2, -1, head_dim), axis=0)
-    shares = shares.reshape(2, blocks_here, SUMMARY, half_heads, head_dim)
+    shares = shares.reshape(2, 2, blocks_here, SUMMARY // 2, half_heads, head_dim)
+    shares = shares.transpose(1, 2, 0, 3, 4, 5).reshape(2, blocks_here, SUMMARY, half_heads, head_dim)
     key_grad = jnp.concatenate(
         [key_grad[:, : positions - SUMMARY], key_grad[:, positions - SUMMARY :] + shares[0]], axis=1
     )

time: 115 us -> 118 us (1.026)
  waiting for transfers between devices: 54.8 us -> 58.4 us
  matrix products: 6.33 us -> 4.62 us
    reshape x4, local copies, waits for them, and re-layouts: 2.22 us -> 4.07 us  [split_heads(): shaped = matrix.reshape(blocks, STRIDE, matrix.shape[1] // (4 * HD), 4, HD)]
    all_to_all x1, waiting for transfers between devices: 26.3 us -> 27.7 us  [shards(): lax.all_to_all(jnp.concatenate([strided_out, terms], axis=1), CTX, 0, 0,...]
    all_to_all x1, waiting for transfers between devices: 27.6 us -> 28.8 us  [shards(): lax.all_to_all(jnp.concatenate([strided_rows, summary_rows], axis=1), CTX...]
    unnamed x27 -> x16, local copies, waits for them, and re-layouts: 4.18 us -> 3.5 us
  transfers between devices with their start and end apart: 4 -> 4, of which waited for: 3 -> 3; matrix products, arithmetic and copies ran while one was open for 6% -> 3% of each run, Pallas kernels for 3% -> 3%
where the time goes in v16:
time: 118 us
  waiting for transfers between devices  58.4 us (49%)
  starting transfers between devices  28.1 us (24%)
  local copies, waits for them, and re-layouts  15.5 us (13%)
  other arithmetic  6.17 us (5%)
  matrix products  4.62 us (4%)
  Pallas kernels  3.79 us (3%)
    all_to_all x1, waiting for transfers between devices, shards(): lax.all_to_all(jnp.concatenate([strided_rows, summary_rows], axis=1), CTX...  28.8 us
    all_to_all x1, waiting for transfers between devices, shards(): lax.all_to_all(jnp.concatenate([strided_out, terms], axis=1), CTX, 0, 0,...  27.7 us
    all_to_all x1, starting transfers between devices, shards(): lax.all_to_all(jnp.concatenate([strided_rows, summary_rows], axis=1), CTX...  16.6 us
    all_to_all x1, starting transfers between devices, shards(): lax.all_to_all(jnp.concatenate([strided_out, terms], axis=1), CTX, 0, 0,...  6.16 us
    reshape x4, local copies, waits for them, and re-layouts, split_heads(): shaped = matrix.reshape(blocks, STRIDE, matrix.shape[1] // (4 * HD), 4, HD)  4.07 us
    pallas_call x1, Pallas kernels, strided_heads(): pl.pallas_call(functools.partial(strided_kernel, scaling=scaling, arrays=...  3.79 us
    unnamed x16, local copies, waits for them, and re-layouts  3.5 us
    ppermute x1, starting transfers between devices, shards(): sibling = lax.ppermute(mine, 'ctx_core', swap)  3.41 us
  transfers between devices with their start and end apart: 4, of which 3 were waited for; matrix products, arithmetic and copies ran while one was open for 3% of the time, Pallas kernels for 3%

profile of v16, /device:TPU:1, one launch (start us, length us, event | category | flops | bytes accessed | tf_op | source)
XLA Modules:
  0.0 117.8 jit_solution(17149487666885577025)
XLA Ops:
  0.6 1.0 reshape.257
  1.6 1.0 reshape.255
  2.7 1.0 reshape.259
  3.7 1.0 reshape.260
  4.7 0.4 slice_bitcast_fusion.5
  5.4 0.4 slice_bitcast_fusion.6
  5.9 1.0 maximum_bitcast_fusion.1
  7.0 0.3 broadcast_in_dim.45
  7.4 1.6 %copy.167 = bf16[128,32,128]{2,1,0:T(8,128)(2,1)} copy(bf16[128,32,128]{2,0,1:T(8,128)(2,1)S(1)} %pad_maximum_fusion) | data formatting | bytes 2097152 | tf_op jit(solution)/shard_map/concatenate | solution.py:192
  9.0 16.6 %all-to-all-start = ((bf16[128,32,128]{2,1,0:T(8,128)(2,1)}), bf16[128,32,128]{2,1,0:T(8,128)(2,1)S(1)}, u32[]{:S(2)}, u32[]{:S(2)}) async-start(bf16[128,32,128]{2,1,0:T(8,128)(2,1)} %copy.167), calls=%async_computation | async-start | bytes 2097152 | tf_op jit(solution)/shard_map/all_to_all | solution.py:191
  26.0 28.8 %all-to-all-done = bf16[128,32,128]{2,1,0:T(8,128)(2,1)S(1)} async-done(((bf16[128,32,128]{2,1,0:T(8,128)(2,1)}), bf16[128,32,128]{2,1,0:T(8,128)(2,1)S(1)}, u32[]{:S(2)}, u32[]{:S(2)}) %all-to-all-start) | async-done | bytes 1048608 | tf_op jit(solution)/shard_map/all_to_all | solution.py:191
  54.8 1.0 fusion.51
  56.0 3.4 %collective-permute-start = (bf16[128,16,128]{2,0,1:T(8,128)(2,1)S(1)}, bf16[128,16,128]{2,0,1:T(8,128)(2,1)S(1)}, u32[]{:S(2)}, u32[]{:S(2)}) collective-permute-start(bf16[128,16,128]{2,0,1:T(8,128)(2,1)S(1)} %copy.235), channel_id=1, source_target_pairs={{0,4},{4,0},{1,5},{5,1},{2,6},{6,2},{3,7},{7,3},{8,12},{12,8},{9,1... | collective-permute-start | bytes 1572872 | tf_op jit(solution)/shard_map/ppermute | solution.py:195
  59.5 0.2 fusion.54
  59.7 3.8 %shard_map.75 = f32[2048,128]{1,0:T(8,128)} custom-call(bf16[2048,128]{1,0:T(8,128)(2,1)} %bitcast.203), custom_call_target="tpu_custom_call" | custom-call | tf_op jit(solution)/shard_map/pallas_call | solution.py:160
  63.5 1.3 %convert_element_type.61 = bf16[2048,128]{1,0:T(8,128)(2,1)S(1)} convert(f32[2048,128]{1,0:T(8,128)} %shard_map.75) | non-fusion elementwise | flops 262144 | bytes 1572864 | tf_op jit(solution)/shard_map/convert_element_type | solution.py:166
  64.9 0.4 copy.169
  65.3 0.5 fusion.55
  65.9 0.3 fusion.3
  66.2 0.3 fusion.22
  66.5 0.4 fusion.8
  67.0 0.5 copy.185
  67.5 0.4 copy.175
  67.9 0.3 convolution_bitcast_fusion.6
  68.3 0.9 multiply_reduce_fusion
  69.2 0.6 fusion.1
  69.8 0.4 fusion.7
  70.2 0.5 copy.183
  71.1 1.9 %collective-permute-start.1 = (bf16[128,16,128]{2,1,0:T(8,128)(2,1)S(1)}, bf16[128,16,128]{2,1,0:T(8,128)(2,1)S(1)}, u32[]{:S(2)}, u32[]{:S(2)}) collective-permute-start(bf16[128,16,128]{2,1,0:T(8,128)(2,1)S(1)} %bitcast.215), channel_id=1, source_target_pairs={{0,4},{4,0},{1,5},{5,1},{2,6},{6,2},{3,7},{7,3},{8,12},{12,8},{9,1... | collective-permute-start | bytes 1572872 | tf_op jit(solution)/shard_map/ppermute | solution.py:220
  73.0 1.9 %collective-permute-done.1 = bf16[128,16,128]{2,1,0:T(8,128)(2,1)S(1)} collective-permute-done((bf16[128,16,128]{2,1,0:T(8,128)(2,1)S(1)}, bf16[128,16,128]{2,1,0:T(8,128)(2,1)S(1)}, u32[]{:S(2)}, u32[]{:S(2)}) %collective-permute-start.1) | collective-permute-done | bytes 524320 | tf_op jit(solution)/shard_map/ppermute | solution.py:220
  75.0 1.0 pad_maximum_fusion.1
  76.0 6.2 %all-to-all-start.1 = ((bf16[128,32,128]{2,1,0:T(8,128)(2,1)}), bf16[128,32,128]{2,1,0:T(8,128)(2,1)S(1)}, u32[]{:S(2)}, u32[]{:S(2)}) async-start(bf16[128,32,128]{2,1,0:T(8,128)(2,1)} %pad_maximum_fusion.1), calls=%async_computation.1 | async-start | bytes 2097152 | tf_op jit(solution)/shard_map/all_to_all | solution.py:222
  82.2 0.2 fusion.17
  82.5 0.3 convolution_bitcast_fusion.5
  82.8 0.2 fusion.18
  83.1 0.2 fusion.9
  83.4 0.2 convolution_bitcast_fusion.3
  83.7 27.7 %all-to-all-done.1 = bf16[128,32,128]{2,1,0:T(8,128)(2,1)S(1)} async-done(((bf16[128,32,128]{2,1,0:T(8,128)(2,1)}), bf16[128,32,128]{2,1,0:T(8,128)(2,1)S(1)}, u32[]{:S(2)}, u32[]{:S(2)}) %all-to-all-start.1) | async-done | bytes 1048608 | tf_op jit(solution)/shard_map/all_to_all | solution.py:222
  111.5 0.5 copy.188
  112.1 0.9 pad_maximum_fusion.3
  113.0 0.2 copy.189
  113.2 0.7 copy.279
  114.0 0.2 copy.197
  114.2 0.7 copy.278
  115.4 0.2 copy.201
  115.6 0.7 copy.277
  116.8 0.2 copy.206
  117.0 0.7 copy.276
  (53 shorter events, 3.0 us)
Async XLA Ops:
  9.0 45.8 %all-to-all-start = ((bf16[128,32,128]{2,1,0:T(8,128)(2,1)}), bf16[128,32,128]{2,1,0:T(8,128)(2,1)S(1)}, u32[]{:S(2)}, u32[]{:S(2)}) async-start(bf16[128,32,128]{2,1,0:T(8,128)(2,1)} %copy.167), calls=%async_computation | async-start | bytes 2097152 | tf_op jit(solution)/shard_map/all_to_all | solution.py:191
  25.9 56.2 %copy-start.2 = (bf16[2,128,1,2,128]{1,4,3,0,2:T(8,128)(2,1)}, bf16[2,128,1,2,128]{1,4,3,0,2:T(8,128)(2,1)S(1)}, u32[]{:S(2)}) copy-start(bf16[2,128,1,2,128]{1,4,3,0,2:T(8,128)(2,1)S(1)} %copy.236) | copy-start | bytes 393220
  56.0 8.8 %collective-permute-start = (bf16[128,16,128]{2,0,1:T(8,128)(2,1)S(1)}, bf16[128,16,128]{2,0,1:T(8,128)(2,1)S(1)}, u32[]{:S(2)}, u32[]{:S(2)}) collective-permute-start(bf16[128,16,128]{2,0,1:T(8,128)(2,1)S(1)} %copy.235), channel_id=1, source_target_pairs={{0,4},{4,0},{1,5},{5,1},{2,6},{6,2},{3,7},{7,3},{8,12},{12,8},{9,1... | collective-permute-start | bytes 1572872 | tf_op jit(solution)/shard_map/ppermute | solution.py:195
  59.7 22.5 %copy-start = (f32[2,2,128,128]{2,3,1,0:T(8,128)}, f32[2,2,128,128]{2,3,1,0:T(8,128)S(1)}, u32[]{:S(2)}) copy-start(f32[2,2,128,128]{2,3,1,0:T(8,128)S(1)} %get-tuple-element.31) | copy-start | bytes 786436
  71.1 3.8 %collective-permute-start.1 = (bf16[128,16,128]{2,1,0:T(8,128)(2,1)S(1)}, bf16[128,16,128]{2,1,0:T(8,128)(2,1)S(1)}, u32[]{:S(2)}, u32[]{:S(2)}) collective-permute-start(bf16[128,16,128]{2,1,0:T(8,128)(2,1)S(1)} %bitcast.215), channel_id=1, source_target_pairs={{0,4},{4,0},{1,5},{5,1},{2,6},{6,2},{3,7},{7,3},{8,12},{12,8},{9,1... | collective-permute-start | bytes 1572872 | tf_op jit(solution)/shard_map/ppermute | solution.py:220
  76.0 35.3 %all-to-all-start.1 = ((bf16[128,32,128]{2,1,0:T(8,128)(2,1)}), bf16[128,32,128]{2,1,0:T(8,128)(2,1)S(1)}, u32[]{:S(2)}, u32[]{:S(2)}) async-start(bf16[128,32,128]{2,1,0:T(8,128)(2,1)} %pad_maximum_fusion.1), calls=%async_computation.1 | async-start | bytes 2097152 | tf_op jit(solution)/shard_map/all_to_all | solution.py:222
  82.5 1.0 copy-start.1
  82.5 1.0 copy-start.3

commit v17 on v15

--- a/solution.py
+++ b/solution.py
@@ -105,7 +105,10 @@
     )
 
 
-def strided_kernel(rows_ref, out_ref, *, scaling, arrays, half_heads):
+def strided_kernel(rows_ref, *refs, scaling, arrays, half_heads, heads):
+    out_ref = refs[-1]
+    if len(refs) == 2:
+        out_ref[...] = refs[0][...]
     width = arrays * 2 * half_heads
     peers = rows_ref.shape[0] // width
     blocks = 2 * peers
@@ -130,7 +133,7 @@
                 block * peers : (block + 1) * peers
             ]
 
-    for head in range(half_heads):
+    for head in heads:
         query = load(0, head)
         key_rows = load(1, head)
         value_rows = load(2, head)
@@ -152,16 +155,18 @@
         store(3, head, product(weights_low, grad_rows, 0, 0).astype(jnp.bfloat16))
 
 
-def strided_heads(rows, scaling, half_heads):
+def strided_heads(rows, scaling, half_heads, heads, previous=None):
     peers, width, head_dim = rows.shape
     vmem = pl.BlockSpec(memory_space=pltpu.VMEM)
-    out = pl.pallas_call(
-        functools.partial(strided_kernel, scaling=scaling, arrays=4, half_heads=half_heads),
+    operands = [rows.reshape(peers * width, head_dim)] + ([] if previous is None else [previous])
+    return pl.pallas_call(
+        functools.partial(
+            strided_kernel, scaling=scaling, arrays=4, half_heads=half_heads, heads=heads
+        ),
         out_shape=jax.ShapeDtypeStruct((peers * width, head_dim), jnp.float32),
-        in_specs=[vmem],
+        in_specs=[vmem] * len(operands),
         out_specs=vmem,
-    )(rows.reshape(peers * width, head_dim))
-    return out.reshape(peers, width, head_dim).astype(jnp.bfloat16)
+    )(*operands)
 
 
 def shards(queries, keys, values, out_grad):
@@ -190,7 +195,8 @@
     )
     mine = received[:, strided_size:]
     sibling = lax.ppermute(mine, "ctx_core", swap)
-    strided_out = strided_heads(received[:, :strided_size], scaling, half_heads)
+    strided_rows = received[:, :strided_size]
+    strided_out = strided_heads(strided_rows, scaling, half_heads, (0,))
     strided_out, sibling = lax.optimization_barrier((strided_out, sibling))
     summary_shape = (peers * blocks_here * SUMMARY, half_heads, head_dim)
     summary_keys = jnp.where(core == 0, mine, sibling).reshape(summary_shape)
@@ -210,9 +216,11 @@
     terms = terms.astype(jnp.bfloat16).reshape(2, peers, -1, head_dim)
     keep = jnp.where(core == 0, terms[0], terms[1])
     give = jnp.where(core == 0, terms[1], terms[0])
-    terms = (
-        keep.astype(jnp.float32) + lax.ppermute(give, "ctx_core", swap).astype(jnp.float32)
-    ).astype(jnp.bfloat16)
+    given = lax.ppermute(give, "ctx_core", swap)
+    strided_out = strided_heads(strided_rows, scaling, half_heads, range(1, half_heads), strided_out)
+    strided_out, given = lax.optimization_barrier((strided_out, given))
+    strided_out = strided_out.reshape(peers, strided_size, head_dim).astype(jnp.bfloat16)
+    terms = (keep.astype(jnp.float32) + given.astype(jnp.float32)).astype(jnp.bfloat16)
     returned = lax.all_to_all(
         jnp.concatenate([strided_out, terms], axis=1), CTX, 0, 0, tiled=True
     )

time: 115 us -> 116 us (level)
  Pallas kernels: 3.69 us -> 6.36 us
    pallas_call x1 -> x2, Pallas kernels: 3.69 us -> 6.36 us  [strided_heads(): pl.pallas_call(functools.partial(strided_kernel, scaling=scaling, arrays=...]
    unnamed x27 -> x25, local copies, waits for them, and re-layouts: 4.18 us -> 3.89 us
  transfers between devices with their start and end apart: 4 -> 4, of which waited for: 3 -> 2; matrix products, arithmetic and copies ran while one was open for 6% -> 4% of each run, Pallas kernels for 3% -> 5%
where the time goes in v17:
time: 116 us
  waiting for transfers between devices  54.5 us (47%)
  starting transfers between devices  28.5 us (25%)
  local copies, waits for them, and re-layouts  14.9 us (13%)
  Pallas kernels  6.36 us (5%)
  matrix products  5.66 us (5%)
  other arithmetic  4.86 us (4%)
  between operations  1.17 us (1%)
    all_to_all x1, waiting for transfers between devices, shards(): lax.all_to_all(jnp.concatenate([strided_rows, summary_rows], axis=1), CTX...  28.2 us
    all_to_all x1, waiting for transfers between devices, shards(): lax.all_to_all(jnp.concatenate([strided_out, terms], axis=1), CTX, 0, 0,...  26.3 us
    all_to_all x1, starting transfers between devices, shards(): lax.all_to_all(jnp.concatenate([strided_rows, summary_rows], axis=1), CTX...  16.6 us
    all_to_all x1, starting transfers between devices, shards(): lax.all_to_all(jnp.concatenate([strided_out, terms], axis=1), CTX, 0, 0,...  6.51 us
    pallas_call x2, Pallas kernels, strided_heads(): pl.pallas_call(functools.partial(strided_kernel, scaling=scaling, arrays=...  6.36 us
    unnamed x25, local copies, waits for them, and re-layouts  3.89 us
    ppermute x1, starting transfers between devices, shards(): sibling = lax.ppermute(mine, 'ctx_core', swap)  3.22 us
  transfers between devices with their start and end apart: 4, of which 2 were waited for; matrix products, arithmetic and copies ran while one was open for 4% of the time, Pallas kernels for 5%

profile of v17, /device:TPU:1, one launch (start us, length us, event | category | flops | bytes accessed | tf_op | source)
XLA Modules:
  0.0 115.9 jit_solution(3353541401982206532)
XLA Ops:
  0.7 1.1 reshape.238
  1.7 1.0 reshape.240
  2.7 0.4 slice_bitcast_fusion.6
  3.3 0.4 slice_bitcast_fusion.5
  3.7 1.0 maximum_bitcast_fusion
  5.2 0.3 broadcast_in_dim.45
  5.5 1.6 %copy.156 = bf16[128,32,128]{2,1,0:T(8,128)(2,1)} copy(bf16[128,32,128]{2,0,1:T(8,128)(2,1)S(1)} %pad_maximum_fusion) | data formatting | bytes 2097152 | tf_op jit(solution)/shard_map/concatenate | solution.py:194
  7.2 16.6 %all-to-all-start = ((bf16[128,32,128]{2,1,0:T(8,128)(2,1)}), bf16[128,32,128]{2,1,0:T(8,128)(2,1)S(1)}, u32[]{:S(2)}, u32[]{:S(2)}) async-start(bf16[128,32,128]{2,1,0:T(8,128)(2,1)} %copy.156), calls=%async_computation | async-start | bytes 2097152 | tf_op jit(solution)/shard_map/all_to_all | solution.py:193
  24.0 0.8 copy.221
  24.8 28.2 %all-to-all-done = bf16[128,32,128]{2,1,0:T(8,128)(2,1)S(1)} async-done(((bf16[128,32,128]{2,1,0:T(8,128)(2,1)}), bf16[128,32,128]{2,1,0:T(8,128)(2,1)S(1)}, u32[]{:S(2)}, u32[]{:S(2)}) %all-to-all-start) | async-done | bytes 1048608 | tf_op jit(solution)/shard_map/all_to_all | solution.py:193
  53.0 1.0 fusion.50
  54.0 3.2 %collective-permute-start = (bf16[128,16,128]{2,1,0:T(8,128)(2,1)S(1)}, bf16[128,16,128]{2,1,0:T(8,128)(2,1)S(1)}, u32[]{:S(2)}, u32[]{:S(2)}) collective-permute-start(bf16[128,16,128]{2,1,0:T(8,128)(2,1)S(1)} %get-tuple-element.18), channel_id=1, source_target_pairs={{0,4},{4,0},{1,5},{5,1},{2,6},{6,2},{3,7},{7,3},{8,12},{12,8},{9,1... | collective-permute-start | bytes 1572872 | tf_op jit(solution)/shard_map/ppermute | solution.py:197
  57.3 0.2 fusion.53
  57.5 3.0 %shard_map.75.refs_0_ = f32[2048,128]{1,0:T(8,128)} custom-call(bf16[2048,128]{1,0:T(8,128)(2,1)} %bitcast.183), custom_call_target="tpu_custom_call" | custom-call | tf_op jit(solution)/shard_map/pallas_call | solution.py:162
  60.6 0.4 copy.164
  61.1 0.5 fusion.54
  61.6 0.3 fusion.3
  62.0 0.3 fusion.20
  62.3 0.3 convolution_bitcast_fusion.6
  62.7 0.2 copy-done.1
  62.9 0.4 fusion.5
  63.3 0.9 multiply_reduce_fusion
  64.2 0.6 fusion.1
  64.8 0.4 select_bitcast_fusion
  65.2 0.5 copy.172
  65.8 2.1 %collective-permute-start.1 = (bf16[128,16,128]{2,1,0:T(8,128)(2,1)S(1)}, bf16[128,16,128]{2,1,0:T(8,128)(2,1)}, u32[]{:S(2)}, u32[]{:S(2)}) collective-permute-start(bf16[128,16,128]{2,1,0:T(8,128)(2,1)S(1)} %bitcast.199), channel_id=1, source_target_pairs={{0,4},{4,0},{1,5},{5,1},{2,6},{6,2},{3,7},{7,3},{8,12},{12,8},{9,1... | collective-permute-start | bytes 1572872 | tf_op jit(solution)/shard_map/ppermute | solution.py:219
  67.9 3.3 %shard_map.76 = f32[2048,128]{1,0:T(8,128)} custom-call(bf16[2048,128]{1,0:T(8,128)(2,1)} %bitcast.184, f32[2048,128]{1,0:T(8,128)} %shard_map.75.refs_0_), custom_call_target="tpu_custom_call" | custom-call | tf_op jit(solution)/shard_map/pallas_call | solution.py:162
  71.2 0.8 copy.173
  72.1 0.4 copy-done
  72.5 1.2 %fusion.18 = bf16[128,16,128]{2,1,0:T(8,128)(2,1)S(1)} fusion(bf16[128,16,128]{2,1,0:T(8,128)(2,1)} %collective-permute-done.1, f32[128,16,128]{2,1,0:T(8,128)S(1)} %bitcast.185), kind=kLoop, calls=%fused_computation.35 | loop fusion | flops 786432 | bytes 2097152 | tf_op jit(solution)/shard_map/convert_element_type | solution.py:223
  73.7 1.0 pad_maximum_fusion.1
  74.7 6.5 %all-to-all-start.1 = ((bf16[128,32,128]{2,1,0:T(8,128)(2,1)}), bf16[128,32,128]{2,1,0:T(8,128)(2,1)S(1)}, u32[]{:S(2)}, u32[]{:S(2)}) async-start(bf16[128,32,128]{2,1,0:T(8,128)(2,1)} %pad_maximum_fusion.1), calls=%async_computation.1 | async-start | bytes 2097152 | tf_op jit(solution)/shard_map/all_to_all | solution.py:224
  81.3 0.4 copy.181
  81.7 1.3 %fusion.15 = bf16[2,2,128,128]{2,3,1,0:T(8,128)(2,1)S(1)} fusion(bf16[2,128,1,2,128]{1,4,3,0,2:T(8,128)(2,1)} %copy-done.6, f32[2,2,128]{2,1,0:T(2,128)S(1)} %bitcast.212, f32[2,2,128]{2,1,0:T(2,128)S(1)} %copy_add_fusion, f32[2,2,128,128]{2,3,1,0:T(8,128)} %copy-done.4, f32[2,2,128]{2,1,0:T(2,128)S(1)} %copy_maximum_fusion, ...), kind=kOutput, calls=%fused_computation.28 | convolution fusion | flops 17104896 | bytes 661504 | tf_op jit(solution)/shard_map/bqgd,bkgd->bgqk/dot_general | solution.py:69
  83.0 0.3 convolution_bitcast_fusion.5
  83.3 0.2 fusion.16
  83.6 0.2 convolution_bitcast_fusion.3
  83.8 0.2 fusion.7
  84.1 26.3 %all-to-all-done.1 = bf16[128,32,128]{2,1,0:T(8,128)(2,1)S(1)} async-done(((bf16[128,32,128]{2,1,0:T(8,128)(2,1)}), bf16[128,32,128]{2,1,0:T(8,128)(2,1)S(1)}, u32[]{:S(2)}, u32[]{:S(2)}) %all-to-all-start.1) | async-done | bytes 1048608 | tf_op jit(solution)/shard_map/all_to_all | solution.py:224
  111.3 0.5 copy.174
  112.0 0.2 copy.190
  112.2 0.7 copy.264
  113.0 0.2 copy.186
  113.2 0.7 copy.265
  114.0 0.2 copy.183
  114.2 0.7 copy.266
  115.0 0.2 copy.175
  115.2 0.7 copy.267
  (57 shorter events, 2.4 us)
Async XLA Ops:
  0.6 2.6 %copy-start.2 = (bf16[256,512]{1,0:T(8,128)(2,1)S(1)}, bf16[256,512]{1,0:T(8,128)(2,1)}, u32[]{:S(2)}) copy-start(bf16[256,512]{1,0:T(8,128)(2,1)} %param.6) | copy-start | bytes 786436
  0.6 2.6 %copy-start.3 = (bf16[256,512]{1,0:T(8,128)(2,1)S(1)}, bf16[256,512]{1,0:T(8,128)(2,1)}, u32[]{:S(2)}) copy-start(bf16[256,512]{1,0:T(8,128)(2,1)} %param.7) | copy-start | bytes 786436
  7.2 45.8 %all-to-all-start = ((bf16[128,32,128]{2,1,0:T(8,128)(2,1)}), bf16[128,32,128]{2,1,0:T(8,128)(2,1)S(1)}, u32[]{:S(2)}, u32[]{:S(2)}) async-start(bf16[128,32,128]{2,1,0:T(8,128)(2,1)} %copy.156), calls=%async_computation | async-start | bytes 2097152 | tf_op jit(solution)/shard_map/all_to_all | solution.py:193
  24.0 39.3 %copy-start.6 = (bf16[2,128,1,2,128]{1,4,3,0,2:T(8,128)(2,1)}, bf16[2,128,1,2,128]{1,4,3,0,2:T(8,128)(2,1)S(1)}, u32[]{:S(2)}) copy-start(bf16[2,128,1,2,128]{1,4,3,0,2:T(8,128)(2,1)S(1)} %copy.219) | copy-start | bytes 393220
  54.0 6.6 %collective-permute-start = (bf16[128,16,128]{2,1,0:T(8,128)(2,1)S(1)}, bf16[128,16,128]{2,1,0:T(8,128)(2,1)S(1)}, u32[]{:S(2)}, u32[]{:S(2)}) collective-permute-start(bf16[128,16,128]{2,1,0:T(8,128)(2,1)S(1)} %get-tuple-element.18), channel_id=1, source_target_pairs={{0,4},{4,0},{1,5},{5,1},{2,6},{6,2},{3,7},{7,3},{8,12},{12,8},{9,1... | collective-permute-start | bytes 1572872 | tf_op jit(solution)/shard_map/ppermute | solution.py:197
  57.5 5.8 %copy-start.4 = (f32[2,2,128,128]{2,3,1,0:T(8,128)}, f32[2,2,128,128]{2,3,1,0:T(8,128)S(1)}, u32[]{:S(2)}) copy-start(f32[2,2,128,128]{2,3,1,0:T(8,128)S(1)} %get-tuple-element.35) | copy-start | bytes 786436
  61.9 0.9 copy-start.1
  65.8 6.3 %collective-permute-start.1 = (bf16[128,16,128]{2,1,0:T(8,128)(2,1)S(1)}, bf16[128,16,128]{2,1,0:T(8,128)(2,1)}, u32[]{:S(2)}, u32[]{:S(2)}) collective-permute-start(bf16[128,16,128]{2,1,0:T(8,128)(2,1)S(1)} %bitcast.199), channel_id=1, source_target_pairs={{0,4},{4,0},{1,5},{5,1},{2,6},{6,2},{3,7},{7,3},{8,12},{12,8},{9,1... | collective-permute-start | bytes 1572872 | tf_op jit(solution)/shard_map/ppermute | solution.py:219
  71.2 1.2 %copy-start = (f32[2048,128]{1,0:T(8,128)S(1)}, f32[2048,128]{1,0:T(8,128)}, u32[]{:S(2)}) copy-start(f32[2048,128]{1,0:T(8,128)} %shard_map.76) | copy-start | bytes 3145732
  74.7 35.7 %all-to-all-start.1 = ((bf16[128,32,128]{2,1,0:T(8,128)(2,1)}), bf16[128,32,128]{2,1,0:T(8,128)(2,1)S(1)}, u32[]{:S(2)}, u32[]{:S(2)}) async-start(bf16[128,32,128]{2,1,0:T(8,128)(2,1)} %pad_maximum_fusion.1), calls=%async_computation.1 | async-start | bytes 2097152 | tf_op jit(solution)/shard_map/all_to_all | solution.py:224
  81.7 1.9 %copy-start.5 = (f32[2,2,128,128]{2,3,1,0:T(8,128)S(1)}, f32[2,2,128,128]{2,3,1,0:T(8,128)}, u32[]{:S(2)}) copy-start(f32[2,2,128,128]{2,3,1,0:T(8,128)} %copy-done.4) | copy-start | bytes 786436
  81.7 1.9 %copy-start.7 = (bf16[2,128,1,2,128]{1,4,3,0,2:T(8,128)(2,1)S(1)}, bf16[2,128,1,2,128]{1,4,3,0,2:T(8,128)(2,1)}, u32[]{:S(2)}) copy-start(bf16[2,128,1,2,128]{1,4,3,0,2:T(8,128)(2,1)} %copy-done.6) | copy-start | bytes 393220
  111.9 3.0 %copy-start.8 = (bf16[2,128,2,128]{1,3,2,0:T(8,128)(2,1)S(1)}, bf16[2,128,2,128]{1,3,2,0:T(8,128)(2,1)}, u32[]{:S(2)}) copy-start(bf16[2,128,2,128]{1,3,2,0:T(8,128)(2,1)} %get-tuple-element.39) | copy-start | bytes 393220

commit v18 on v15

--- a/solution.py
+++ b/solution.py
@@ -161,7 +161,7 @@
         in_specs=[vmem],
         out_specs=vmem,
     )(rows.reshape(peers * width, head_dim))
-    return out.reshape(peers, width, head_dim).astype(jnp.bfloat16)
+    return out.reshape(peers, width, head_dim)
 
 
 def shards(queries, keys, values, out_grad):
@@ -214,7 +214,11 @@
         keep.astype(jnp.float32) + lax.ppermute(give, "ctx_core", swap).astype(jnp.float32)
     ).astype(jnp.bfloat16)
     returned = lax.all_to_all(
-        jnp.concatenate([strided_out, terms], axis=1), CTX, 0, 0, tiled=True
+        jnp.concatenate([strided_out, terms.astype(jnp.float32)], axis=1).astype(jnp.bfloat16),
+        CTX,
+        0,
+        0,
+        tiled=True,
     )
     strided_out = returned[:, :strided_size].reshape(
         peers, 4, blocks_here, residues, half_heads, head_dim

time: 115 us -> 113 us (0.983)
  other arithmetic: 5.04 us -> 3.82 us
    convert_element_type x1 -> x0, other arithmetic: 1.28 us -> none  [strided_heads(): return out.reshape(peers, width, head_dim).astype(jnp.bfloat16)]
    unnamed x27 -> x25, local copies, waits for them, and re-layouts: 4.18 us -> 3.49 us
  transfers between devices with their start and end apart: 4 -> 4, of which waited for: 3 -> 3; matrix products, arithmetic and copies ran while one was open for 6% -> 4% of each run, Pallas kernels for 3% -> 3%
where the time goes in v18:
time: 113 us; the launch traced here: 112 us
  waiting for transfers between devices  55.3 us (49%)
  starting transfers between devices  28.1 us (25%)
  local copies, waits for them, and re-layouts  14.5 us (13%)
  matrix products  5.67 us (5%)
  other arithmetic  3.82 us (3%)
  Pallas kernels  3.79 us (3%)
  between operations  1.18 us (1%)
    all_to_all x1, waiting for transfers between devices, shards(): lax.all_to_all(jnp.concatenate([strided_rows, summary_rows], axis=1), CTX...  28.2 us
    all_to_all x1, waiting for transfers between devices, shards(): lax.all_to_all(jnp.concatenate([strided_out, terms.astype(jnp.float32)],...  26.3 us
    all_to_all x1, starting transfers between devices, shards(): lax.all_to_all(jnp.concatenate([strided_rows, summary_rows], axis=1), CTX...  16.6 us
    all_to_all x1, starting transfers between devices, shards(): lax.all_to_all(jnp.concatenate([strided_out, terms.astype(jnp.float32)],...  6.16 us
    pallas_call x1, Pallas kernels, strided_heads(): pl.pallas_call(functools.partial(strided_kernel, scaling=scaling, arrays=...  3.79 us
    unnamed x25, local copies, waits for them, and re-layouts  3.49 us
    ppermute x1, starting transfers between devices, shards(): sibling = lax.ppermute(mine, 'ctx_core', swap)  3.22 us
  transfers between devices with their start and end apart: 4, of which 3 were waited for; matrix products, arithmetic and copies ran while one was open for 4% of the time, Pallas kernels for 3%

profile of v18, /device:TPU:1, one launch (start us, length us, event | category | flops | bytes accessed | tf_op | source)
XLA Modules:
  0.0 112.4 jit_solution(17020002389908421931)
XLA Ops:
  0.7 1.1 reshape.238
  1.7 1.0 reshape.240
  2.7 0.4 slice_bitcast_fusion.6
  3.3 0.4 slice_bitcast_fusion.5
  3.7 1.0 maximum_bitcast_fusion
  5.2 0.3 broadcast_in_dim.45
  5.5 1.6 %copy.156 = bf16[128,32,128]{2,1,0:T(8,128)(2,1)} copy(bf16[128,32,128]{2,0,1:T(8,128)(2,1)S(1)} %pad_maximum_fusion) | data formatting | bytes 2097152 | tf_op jit(solution)/shard_map/concatenate | solution.py:189
  7.2 16.6 %all-to-all-start = ((bf16[128,32,128]{2,1,0:T(8,128)(2,1)}), bf16[128,32,128]{2,1,0:T(8,128)(2,1)S(1)}, u32[]{:S(2)}, u32[]{:S(2)}) async-start(bf16[128,32,128]{2,1,0:T(8,128)(2,1)} %copy.156), calls=%async_computation | async-start | bytes 2097152 | tf_op jit(solution)/shard_map/all_to_all | solution.py:188
  24.0 0.8 copy.221
  24.8 28.2 %all-to-all-done = bf16[128,32,128]{2,1,0:T(8,128)(2,1)S(1)} async-done(((bf16[128,32,128]{2,1,0:T(8,128)(2,1)}), bf16[128,32,128]{2,1,0:T(8,128)(2,1)S(1)}, u32[]{:S(2)}, u32[]{:S(2)}) %all-to-all-start) | async-done | bytes 1048608 | tf_op jit(solution)/shard_map/all_to_all | solution.py:188
  53.0 1.0 fusion.50
  54.0 3.2 %collective-permute-start = (bf16[128,16,128]{2,1,0:T(8,128)(2,1)S(1)}, bf16[128,16,128]{2,1,0:T(8,128)(2,1)S(1)}, u32[]{:S(2)}, u32[]{:S(2)}) collective-permute-start(bf16[128,16,128]{2,1,0:T(8,128)(2,1)S(1)} %get-tuple-element.14), channel_id=1, source_target_pairs={{0,4},{4,0},{1,5},{5,1},{2,6},{6,2},{3,7},{7,3},{8,12},{12,8},{9,1... | collective-permute-start | bytes 1572872 | tf_op jit(solution)/shard_map/ppermute | solution.py:192
  57.3 0.2 fusion.53
  57.5 3.8 %shard_map.75 = f32[2048,128]{1,0:T(8,128)} custom-call(bf16[2048,128]{1,0:T(8,128)(2,1)} %bitcast.189), custom_call_target="tpu_custom_call" | custom-call | tf_op jit(solution)/shard_map/pallas_call | solution.py:158
  61.4 0.4 copy.164
  61.8 0.5 fusion.54
  62.4 0.3 fusion.3
  62.7 0.3 fusion.20
  63.1 0.3 convolution_bitcast_fusion.6
  63.4 0.2 copy-done.1
  63.6 0.4 fusion.5
  64.1 0.9 multiply_reduce_fusion
  64.9 0.6 fusion.1
  65.6 0.4 select_bitcast_fusion
  66.0 0.5 copy.173
  66.6 2.1 %collective-permute-start.1 = (bf16[128,16,128]{2,1,0:T(8,128)(2,1)S(1)}, bf16[128,16,128]{2,1,0:T(8,128)(2,1)S(1)}, u32[]{:S(2)}, u32[]{:S(2)}) collective-permute-start(bf16[128,16,128]{2,1,0:T(8,128)(2,1)S(1)} %bitcast.198), channel_id=1, source_target_pairs={{0,4},{4,0},{1,5},{5,1},{2,6},{6,2},{3,7},{7,3},{8,12},{12,8},{9,1... | collective-permute-start | bytes 1572872 | tf_op jit(solution)/shard_map/ppermute | solution.py:214
  68.8 0.8 copy.172
  69.6 0.8 collective-permute-done.1
  70.5 1.0 pad_maximum_fusion.1
  71.5 6.2 %all-to-all-start.1 = ((bf16[128,32,128]{2,1,0:T(8,128)(2,1)}), bf16[128,32,128]{2,1,0:T(8,128)(2,1)S(1)}, u32[]{:S(2)}, u32[]{:S(2)}) async-start(bf16[128,32,128]{2,1,0:T(8,128)(2,1)} %pad_maximum_fusion.1), calls=%async_computation.1 | async-start | bytes 2097152 | tf_op jit(solution)/shard_map/all_to_all | solution.py:216
  77.7 0.4 copy.181
  78.2 1.3 %fusion.15 = bf16[2,2,128,128]{2,3,1,0:T(8,128)(2,1)S(1)} fusion(bf16[2,128,1,2,128]{1,4,3,0,2:T(8,128)(2,1)} %copy-done.6, f32[2,2,128]{2,1,0:T(2,128)S(1)} %bitcast.211, f32[2,2,128]{2,1,0:T(2,128)S(1)} %copy_add_fusion, f32[2,2,128,128]{2,3,1,0:T(8,128)} %copy-done.4, f32[2,2,128]{2,1,0:T(2,128)S(1)} %copy_maximum_fusion, ...), kind=kOutput, calls=%fused_computation.28 | convolution fusion | flops 17104896 | bytes 661504 | tf_op jit(solution)/shard_map/bqgd,bkgd->bgqk/dot_general | solution.py:69
  79.5 0.3 convolution_bitcast_fusion.5
  79.8 0.2 fusion.16
  80.0 0.2 convolution_bitcast_fusion.3
  80.3 0.2 fusion.7
  80.6 26.3 %all-to-all-done.1 = bf16[128,32,128]{2,1,0:T(8,128)(2,1)S(1)} async-done(((bf16[128,32,128]{2,1,0:T(8,128)(2,1)}), bf16[128,32,128]{2,1,0:T(8,128)(2,1)S(1)}, u32[]{:S(2)}, u32[]{:S(2)}) %all-to-all-start.1) | async-done | bytes 1048608 | tf_op jit(solution)/shard_map/all_to_all | solution.py:216
  106.9 0.2 fusion.49
  107.2 0.1 copy.185
  107.8 0.5 copy.174
  108.4 0.2 copy.190
  108.6 0.7 copy.264
  109.5 0.2 copy.186
  109.7 0.7 copy.265
  110.4 0.2 copy.183
  110.6 0.7 copy.266
  111.4 0.2 copy.175
  111.6 0.7 copy.267
  (56 shorter events, 2.2 us)
Async XLA Ops:
  0.6 2.6 %copy-start.2 = (bf16[256,512]{1,0:T(8,128)(2,1)S(1)}, bf16[256,512]{1,0:T(8,128)(2,1)}, u32[]{:S(2)}) copy-start(bf16[256,512]{1,0:T(8,128)(2,1)} %param.6) | copy-start | bytes 786436
  0.6 2.6 %copy-start.3 = (bf16[256,512]{1,0:T(8,128)(2,1)S(1)}, bf16[256,512]{1,0:T(8,128)(2,1)}, u32[]{:S(2)}) copy-start(bf16[256,512]{1,0:T(8,128)(2,1)} %param.7) | copy-start | bytes 786436
  7.2 45.8 %all-to-all-start = ((bf16[128,32,128]{2,1,0:T(8,128)(2,1)}), bf16[128,32,128]{2,1,0:T(8,128)(2,1)S(1)}, u32[]{:S(2)}, u32[]{:S(2)}) async-start(bf16[128,32,128]{2,1,0:T(8,128)(2,1)} %copy.156), calls=%async_computation | async-start | bytes 2097152 | tf_op jit(solution)/shard_map/all_to_all | solution.py:188
  24.0 40.1 %copy-start.6 = (bf16[2,128,1,2,128]{1,4,3,0,2:T(8,128)(2,1)}, bf16[2,128,1,2,128]{1,4,3,0,2:T(8,128)(2,1)S(1)}, u32[]{:S(2)}) copy-start(bf16[2,128,1,2,128]{1,4,3,0,2:T(8,128)(2,1)S(1)} %copy.219) | copy-start | bytes 393220
  54.0 7.4 %collective-permute-start = (bf16[128,16,128]{2,1,0:T(8,128)(2,1)S(1)}, bf16[128,16,128]{2,1,0:T(8,128)(2,1)S(1)}, u32[]{:S(2)}, u32[]{:S(2)}) collective-permute-start(bf16[128,16,128]{2,1,0:T(8,128)(2,1)S(1)} %get-tuple-element.14), channel_id=1, source_target_pairs={{0,4},{4,0},{1,5},{5,1},{2,6},{6,2},{3,7},{7,3},{8,12},{12,8},{9,1... | collective-permute-start | bytes 1572872 | tf_op jit(solution)/shard_map/ppermute | solution.py:192
  57.5 6.5 %copy-start.4 = (f32[2,2,128,128]{2,3,1,0:T(8,128)}, f32[2,2,128,128]{2,3,1,0:T(8,128)S(1)}, u32[]{:S(2)}) copy-start(f32[2,2,128,128]{2,3,1,0:T(8,128)S(1)} %get-tuple-element.31) | copy-start | bytes 786436
  62.7 0.9 copy-start.1
  65.6 3.1 %copy-start = (f32[2048,128]{1,0:T(8,128)S(1)}, f32[2048,128]{1,0:T(8,128)}, u32[]{:S(2)}) copy-start(f32[2048,128]{1,0:T(8,128)} %shard_map.75) | copy-start | bytes 3145732
  66.6 3.8 %collective-permute-start.1 = (bf16[128,16,128]{2,1,0:T(8,128)(2,1)S(1)}, bf16[128,16,128]{2,1,0:T(8,128)(2,1)S(1)}, u32[]{:S(2)}, u32[]{:S(2)}) collective-permute-start(bf16[128,16,128]{2,1,0:T(8,128)(2,1)S(1)} %bitcast.198), channel_id=1, source_target_pairs={{0,4},{4,0},{1,5},{5,1},{2,6},{6,2},{3,7},{7,3},{8,12},{12,8},{9,1... | collective-permute-start | bytes 1572872 | tf_op jit(solution)/shard_map/ppermute | solution.py:214
  71.5 35.3 %all-to-all-start.1 = ((bf16[128,32,128]{2,1,0:T(8,128)(2,1)}), bf16[128,32,128]{2,1,0:T(8,128)(2,1)S(1)}, u32[]{:S(2)}, u32[]{:S(2)}) async-start(bf16[128,32,128]{2,1,0:T(8,128)(2,1)} %pad_maximum_fusion.1), calls=%async_computation.1 | async-start | bytes 2097152 | tf_op jit(solution)/shard_map/all_to_all | solution.py:216
  78.1 1.9 %copy-start.5 = (f32[2,2,128,128]{2,3,1,0:T(8,128)S(1)}, f32[2,2,128,128]{2,3,1,0:T(8,128)}, u32[]{:S(2)}) copy-start(f32[2,2,128,128]{2,3,1,0:T(8,128)} %copy-done.4) | copy-start | bytes 786436
  78.2 1.9 %copy-start.7 = (bf16[2,128,1,2,128]{1,4,3,0,2:T(8,128)(2,1)S(1)}, bf16[2,128,1,2,128]{1,4,3,0,2:T(8,128)(2,1)}, u32[]{:S(2)}) copy-start(bf16[2,128,1,2,128]{1,4,3,0,2:T(8,128)(2,1)} %copy-done.6) | copy-start | bytes 393220
  108.4 3.0 %copy-start.8 = (bf16[2,128,2,128]{1,3,2,0:T(8,128)(2,1)S(1)}, bf16[2,128,2,128]{1,3,2,0:T(8,128)(2,1)}, u32[]{:S(2)}) copy-start(bf16[2,128,2,128]{1,3,2,0:T(8,128)(2,1)} %get-tuple-element.35) | copy-start | bytes 393220
